TPU v7x, 128 devices: a whole 4x4x4 slice. The times are simulated.
128 devices in a mesh: skyy: 8 (over x, core), skyx: 16 (over z, y).
Axes of the slice: x: 4, y: 4, z: 4, core: 2. Of those that a mesh axis runs over, the one named last changes fastest.
Arguments:
- tiles: bfloat16 [8, 128, 256, 256], P('skyy', 'skyx'), may hold values from -6 to 6
- coeffs: bfloat16 [8, 128, 5, 256, 256], P('skyy', 'skyx'), may hold values from -4 to 4
- weights: bfloat16 [8, 128], P('skyy', 'skyx'), may hold values from 0.25 to 4
- tile_slot: int32 [8, 128], P('skyy', 'skyx'), may hold values from 0 to 31, as said below
- slot_offset: int32 [2, 8, 512], P(None, 'skyy', 'skyx'), may hold values from -224 to 480
Outputs:
- coadd: float32 [4096, 8192], P('skyy', 'skyx')
- detection: float32 [4096, 8192], P('skyy', 'skyx')
Inputs may be any that keep to these rules, and one draw needn't show every extreme that they name: `tile_slot`: within one device the values are distinct; each device sends at most 2 tiles to one patch, and in every row of patches one patch receives 2 tiles from every device of that row.
All inputs are finite; a program needn't handle non-finite values.
Results may differ from a plain program's by a relative error of at most 0.013.
Values may be sent and summed in bfloat16 or wider, within the bound.
No kernel may reach another device: no remote copies, remote signals or barrier semaphores. Data moves between devices by JAX's collectives and lax.ppermute only.
A program may use at most 192 MiB of HBM per device.

v0:
```python
import jax
import jax.numpy as jnp
from jax import lax
from jax.sharding import PartitionSpec as P

NB = 5
REACH = 10
CAP = 2
PATCH = 512


basis_widths = (1.0, 1.8, 2.6, 3.6, 5.0)
detect_width = 2.5


def padded(cells, sides, width):
    for axis, dim in sides:
        count = lax.axis_size(axis)
        ends = count - 1
        head = lax.slice_in_dim(cells, 0, width, axis=dim)
        tail = lax.slice_in_dim(cells, cells.shape[dim] - width, cells.shape[dim], axis=dim)
        cells = jnp.concatenate(
            [
                lax.ppermute(tail, axis, [(i, (i + 1) % count) for i in range(ends)]),
                cells,
                lax.ppermute(head, axis, [((i + 1) % count, i) for i in range(ends)]),
            ],
            axis=dim,
        )
    return cells


def band_matrices(size):
    rows = jnp.arange(size, dtype=jnp.int32)[:, None]
    cols = jnp.arange(size, dtype=jnp.int32)[None, :]
    gap = (cols - rows).astype(jnp.float32)
    inside = jnp.abs(cols - rows) <= REACH
    taps = jnp.arange(-REACH, REACH + 1).astype(jnp.float32)
    mats = []
    for width in basis_widths:
        total = jnp.sum(jnp.exp(-taps * taps / (2.0 * width * width)))
        mats.append(jnp.where(inside, jnp.exp(-gap * gap / (2.0 * width * width)) / total, 0.0))
    return jnp.stack(mats).astype(jnp.bfloat16)


def match_batch(batch_tiles, batch_coeffs, basis):
    vert = jnp.einsum(
        "bij,mjk->mbik", basis, batch_tiles, preferred_element_type=jnp.float32
    ).astype(jnp.bfloat16)
    horiz = jnp.einsum("mbik,bjk->mbij", vert, basis, preferred_element_type=jnp.float32)
    result = jnp.sum(batch_coeffs.astype(jnp.float32) * horiz, axis=1).astype(jnp.bfloat16)
    return lax.optimization_barrier(result)


def coadd_patch(matched, slot_weight, offsets, patch):
    slot_count = matched.shape[0]
    size = matched.shape[1]
    local = jnp.arange(size, dtype=jnp.int32)
    pixel = jnp.arange(patch, dtype=jnp.int32)
    row_hit = offsets[0][:, None, None] + local[None, :, None] == pixel[None, None, :]
    col_hit = offsets[1][:, None, None] + local[None, :, None] == pixel[None, None, :]
    row_place = row_hit.astype(jnp.bfloat16)
    placed = jnp.einsum("sip,sij->psj", row_place, matched, preferred_element_type=jnp.float32)
    placed = placed.astype(jnp.bfloat16).reshape(patch, slot_count * size)
    zero_weight = jnp.zeros((), jnp.bfloat16)
    col_place = jnp.where(col_hit, slot_weight[:, None, None], zero_weight).reshape(
        slot_count * size, patch
    )
    numer = jnp.dot(placed, col_place, preferred_element_type=jnp.float32)
    row_cover = jnp.any(row_hit, axis=1).astype(jnp.float32)
    col_cover = jnp.where(jnp.any(col_hit, axis=1), slot_weight[:, None].astype(jnp.float32), 0.0)
    cover = jnp.dot(
        row_cover.T, col_cover, precision=lax.Precision.HIGHEST, preferred_element_type=jnp.float32
    )
    return numer / (1.0 + cover)


def detect_kernel():
    taps = jnp.arange(-REACH, REACH + 1).astype(jnp.float32)
    kernel = jnp.exp(-taps * taps / (2.0 * detect_width * detect_width))
    return kernel / jnp.sum(kernel)


def vertical_pass(extended, out_rows):
    kernel = detect_kernel()
    vert = jnp.zeros((out_rows, extended.shape[1]), jnp.float32)
    for step in range(2 * REACH + 1):
        vert = vert + kernel[step] * extended[step : step + out_rows, :]
    return vert


def horizontal_pass(vert, out_cols):
    kernel = detect_kernel()
    result = jnp.zeros((vert.shape[0], out_cols), jnp.float32)
    for step in range(2 * REACH + 1):
        result = result + kernel[step] * vert[:, step : step + out_cols]
    return result


def body(tiles, coeffs, weights, tile_slot, slot_offset):
    count = tiles.shape[1]
    size = tiles.shape[2]
    columns = lax.axis_size("skyx")
    slots = columns * CAP
    patch = PATCH
    basis = band_matrices(size)
    own_tiles = tiles[0]
    own_coeffs = coeffs[0]
    own_weight = weights[0]
    own_slot = tile_slot[0]
    offsets = slot_offset[:, 0, :]
    send_weight = (
        jnp.zeros((slots,), jnp.bfloat16).at[own_slot].set(own_weight).reshape(columns, CAP)
    )
    grouped_tiles = own_tiles.reshape(count // CAP, CAP, size, size)
    grouped_coeffs = own_coeffs.reshape(count // CAP, CAP, NB, size, size)
    own_matched = lax.map(
        lambda pair: match_batch(pair[0], pair[1], basis), (grouped_tiles, grouped_coeffs)
    )
    own_matched = own_matched.reshape(count, size, size)
    send_matched = jnp.zeros((slots, size, size), jnp.bfloat16).at[own_slot].set(own_matched)
    send_matched = send_matched.reshape(columns, CAP, size, size)
    matched, recv_weight = (
        lax.all_to_all(send_matched, "skyx", split_axis=0, concat_axis=0, tiled=True),
        lax.all_to_all(send_weight, "skyx", split_axis=0, concat_axis=0, tiled=True),
    )
    matched = matched.reshape(slots, size, size)
    recv_weight = recv_weight.reshape(slots)
    coadd = coadd_patch(matched, recv_weight, offsets, patch)
    extended = padded(coadd.astype(jnp.bfloat16), (("skyy", 0), ("skyx", 1)), REACH).astype(
        coadd.dtype
    )
    detection = horizontal_pass(vertical_pass(extended, patch), patch)
    return (coadd, detection)


def solution(mesh):
    in_specs = (
        P("skyy", "skyx", None, None),
        P("skyy", "skyx", None, None, None),
        P("skyy", "skyx"),
        P("skyy", "skyx"),
        P(None, "skyy", "skyx"),
    )
    out_specs = (P("skyy", "skyx"), P("skyy", "skyx"))
    return jax.shard_map(body, mesh=mesh, in_specs=in_specs, out_specs=out_specs, check_vma=False)
```

profile of v0, /device:TPU:29, one launch (start us, length us, event | category | flops | bytes accessed | tf_op | source)
XLA Modules:
  0.0 177.6 jit_solution(14792422301894020463)
XLA Ops:
  0.6 0.7 fusion.76
  1.3 0.7 scatter_custom_fusion.1
  2.0 0.7 all_to_all.12
  2.7 7.6 %all-to-all-start.1 = ((bf16[16,1,2]{2,1,0:T(2,128)(2,1)}), bf16[16,1,2]{2,1,0:T(2,128)(2,1)S(1)}, u32[]{:S(2)}, u32[]{:S(2)}) async-start(bf16[16,1,2]{2,1,0:T(2,128)(2,1)} %all_to_all.12), calls=%async_computation.1 | async-start | bytes 16384 | tf_op jit(solution)/shard_map/all_to_all | solution.py:125
  10.4 0.6 exponential_reduce_fusion.4
  11.0 0.7 exponential_reduce_fusion.3
  11.7 0.6 exponential_reduce_fusion.2
  12.3 0.6 exponential_reduce_fusion.1
  12.9 0.7 exponential_reduce_fusion
  13.6 0.7 fusion.68
  14.3 1.5 copy.14
  15.8 0.8 fusion.69
  16.6 0.6 fusion.70
  17.2 0.7 fusion.71
  17.9 0.7 fusion.72
  18.7 9.5 %while.10 = (s32[]{:T(128)}, bf16[4,2,256,256]{3,2,1,0:T(8,128)(2,1)S(1)}, bf16[4,2,5,256,256]{4,3,2,1,0:T(8,128)(2,1)}, bf16[4,2,256,256]{2,3,1,0:T(8,128)(2,1)...) while((s32[]{:T(128)}, bf16[4,2,256,256]{3,2,1,0:T(8,128)(2,1)S(1)}, ...), condition=%wide.region_7.8_spmd, body=%wide.region_5.0_spmd.sunk | while | flops 673579008 | bytes 3671113 | solution.py:117
  18.7 2.3 %fusion.95 = bf16[2,256,256]{2,1,0:T(8,128)(2,1)S(1)} fusion(bf16[5,256,256]{2,1,0:T(8,128)(2,1)S(1)} %get-tuple-element.133, bf16[4,2,256,256]{2,3,1,0:T(8,128)(2,1)S(1)} %get-tuple-element.132, s32[]{:T(128)} %get-tuple-element.123, bf16[4,2,5,256,256]{4,3,2,1,0:T(8,128)(2,1)} %get-tuple-element.131), kind=kOutput, calls=%fused_computation.3.clone.1 | convolution fusion | flops 673579008 | bytes 3146752 | tf_op jit(solution)/shard_map/while/body/eval_jaxpr/mbik,bjk->mbij/dot_general | solution.py:50
  21.1 2.3 %fusion.95 = bf16[2,256,256]{2,1,0:T(8,128)(2,1)S(1)} fusion(bf16[5,256,256]{2,1,0:T(8,128)(2,1)S(1)} %get-tuple-element.133, bf16[4,2,256,256]{2,3,1,0:T(8,128)(2,1)S(1)} %get-tuple-element.132, s32[]{:T(128)} %get-tuple-element.123, bf16[4,2,5,256,256]{4,3,2,1,0:T(8,128)(2,1)} %get-tuple-element.131), kind=kOutput, calls=%fused_computation.3.clone.1 | convolution fusion | flops 673579008 | bytes 3146752 | tf_op jit(solution)/shard_map/while/body/eval_jaxpr/mbik,bjk->mbij/dot_general | solution.py:50
  23.4 2.3 %fusion.95 = bf16[2,256,256]{2,1,0:T(8,128)(2,1)S(1)} fusion(bf16[5,256,256]{2,1,0:T(8,128)(2,1)S(1)} %get-tuple-element.133, bf16[4,2,256,256]{2,3,1,0:T(8,128)(2,1)S(1)} %get-tuple-element.132, s32[]{:T(128)} %get-tuple-element.123, bf16[4,2,5,256,256]{4,3,2,1,0:T(8,128)(2,1)} %get-tuple-element.131), kind=kOutput, calls=%fused_computation.3.clone.1 | convolution fusion | flops 673579008 | bytes 3146752 | tf_op jit(solution)/shard_map/while/body/eval_jaxpr/mbik,bjk->mbij/dot_general | solution.py:50
  25.8 2.3 %fusion.95 = bf16[2,256,256]{2,1,0:T(8,128)(2,1)S(1)} fusion(bf16[5,256,256]{2,1,0:T(8,128)(2,1)S(1)} %get-tuple-element.133, bf16[4,2,256,256]{2,3,1,0:T(8,128)(2,1)S(1)} %get-tuple-element.132, s32[]{:T(128)} %get-tuple-element.123, bf16[4,2,5,256,256]{4,3,2,1,0:T(8,128)(2,1)} %get-tuple-element.131), kind=kOutput, calls=%fused_computation.3.clone.1 | convolution fusion | flops 673579008 | bytes 3146752 | tf_op jit(solution)/shard_map/while/body/eval_jaxpr/mbik,bjk->mbij/dot_general | solution.py:50
  28.2 2.4 %broadcast_in_dim.55 = bf16[32,256,256]{2,1,0:T(8,128)(2,1)} broadcast(bf16[]{:T(256)} %constant.22.clone.1), dimensions={} | broadcast | bytes 4194306 | tf_op jit(solution)/shard_map/broadcast_in_dim | solution.py:121
  30.6 2.8 %scatter_fusion = bf16[32,256,256]{2,1,0:T(8,128)(2,1)} fusion(bf16[32,256,256]{2,1,0:T(8,128)(2,1)} %broadcast_in_dim.55, s32[8]{0:T(128)S(1)} %fusion.76, bf16[8,256,256]{2,1,0:T(8,128)(2,1)S(1)} %bitcast.84), kind=kCustom, calls=%fused_computation | custom fusion | bytes 3145760 | tf_op jit(solution)/shard_map/scatter | solution.py:121
  33.5 6.4 %copy.16 = bf16[16,2,256,256]{2,3,1,0:T(8,128)(2,1)} copy(bf16[16,2,256,256]{3,2,1,0:T(8,128)(2,1)} %bitcast.82) | data formatting | bytes 8388608 | tf_op jit(solution)/shard_map/reshape | solution.py:122
  39.9 0.0 all-to-all-done.1
  39.9 6.8 %all-to-all-start = ((bf16[16,2,256,256]{2,3,1,0:T(8,128)(2,1)}), bf16[16,2,256,256]{2,3,1,0:T(8,128)(2,1)}, u32[]{:S(2)}, u32[]{:S(2)}) async-start(bf16[16,2,256,256]{2,3,1,0:T(8,128)(2,1)} %copy.16), calls=%async_computation | async-start | bytes 8388608 | tf_op jit(solution)/shard_map/all_to_all | solution.py:124
  46.7 0.6 fusion.79
  47.3 0.7 broadcast_divide_fusion
  48.0 0.1 iota_add_fusion
  48.1 3.1 %fusion.10 = pred[32,512]{1,0:T(8,128)(4,1)S(1)} fusion(s32[32,256]{1,0:T(8,128)S(1)} %get-tuple-element.84), kind=kLoop, calls=%fused_computation.14 | loop fusion | flops 8372224 | bytes 49152 | tf_op jit(solution)/shard_map/reduce_or | solution.py:71
  51.2 3.1 %fusion.12 = pred[32,512]{1,0:T(8,128)(4,1)S(1)} fusion(s32[32,256]{1,0:T(8,128)S(1)} %get-tuple-element.85), kind=kLoop, calls=%fused_computation.17 | loop fusion | flops 8372224 | bytes 49152 | tf_op jit(solution)/shard_map/reduce_or | solution.py:70
  54.4 0.1 broadcast_in_dim.59
  54.5 51.5 %all-to-all-done = bf16[16,2,256,256]{2,3,1,0:T(8,128)(2,1)} async-done(((bf16[16,2,256,256]{2,3,1,0:T(8,128)(2,1)}), bf16[16,2,256,256]{2,3,1,0:T(8,128)(2,1)}, u32[]{:S(2)}, u32[]{:S(2)}) %all-to-all-start) | async-done | bytes 4194336 | tf_op jit(solution)/shard_map/all_to_all | solution.py:124
  105.9 10.5 %fusion.22 = f32[512,512]{1,0:T(8,128)S(1)} fusion(s32[32,256]{1,0:T(8,128)S(1)} %get-tuple-element.84, bf16[32]{0:T(256)(128)(2,1)S(1)} %broadcast_in_dim.59, bf16[32,256,256]{1,2,0:T(8,128)(2,1)} %bitcast.14, s32[32,256]{1,0:T(8,128)S(1)} %get-tuple-element.85), kind=kOutput, calls=%fused_computation.26 | convolution fusion | flops 6459228160 | bytes 5308480 | tf_op jit(solution)/shard_map/dot_general | solution.py:69
  116.5 1.7 fusion.85
  118.2 5.1 %collective-permute-start = (bf16[10,512]{1,0:T(8,128)(2,1)S(1)}, bf16[10,512]{1,0:T(8,128)(2,1)S(1)}, u32[]{:S(2)}, u32[]{:S(2)}) collective-permute-start(bf16[10,512]{1,0:T(8,128)(2,1)S(1)} %get-tuple-element.57), channel_id=1, source_target_pairs={{0,16},{16,32},{32,48},{48,64},{64,80},{80,96},{96,112},{1,17},{17... | collective-permute-start | bytes 30728 | tf_op jit(solution)/shard_map/ppermute | solution.py:24
  123.3 1.9 %collective-permute-start.1 = (bf16[10,512]{1,0:T(8,128)(2,1)S(1)}, bf16[10,512]{1,0:T(8,128)(2,1)S(1)}, u32[]{:S(2)}, u32[]{:S(2)}) collective-permute-start(bf16[10,512]{1,0:T(8,128)(2,1)S(1)} %get-tuple-element.58), channel_id=1, source_target_pairs={{16,0},{32,16},{48,32},{64,48},{80,64},{96,80},{112,96},{17,1},{33... | collective-permute-start | bytes 30728 | tf_op jit(solution)/shard_map/ppermute | solution.py:26
  125.2 0.7 fusion.83
  126.0 0.0 collective-permute-done
  126.0 2.4 %collective-permute-done.1 = bf16[10,512]{1,0:T(8,128)(2,1)S(1)} collective-permute-done((bf16[10,512]{1,0:T(8,128)(2,1)S(1)}, bf16[10,512]{1,0:T(8,128)(2,1)S(1)}, u32[]{:S(2)}, u32[]{:S(2)}) %collective-permute-start.1) | collective-permute-done | bytes 10272 | tf_op jit(solution)/shard_map/ppermute | solution.py:26
  128.4 0.1 pad_maximum_fusion.2
  128.5 3.3 %collective-permute-start.2 = (bf16[532,10]{1,0:T(8,128)(2,1)S(1)}, bf16[532,10]{1,0:T(8,128)(2,1)S(1)}, u32[]{:S(2)}, u32[]{:S(2)}) collective-permute-start(bf16[532,10]{1,0:T(8,128)(2,1)S(1)} %get-tuple-element.55), channel_id=1, source_target_pairs={{0,1},{1,2},{2,3},{3,4},{4,5},{5,6},{6,7},{7,8},{8,9},{9,10},{10,1... | collective-permute-start | bytes 31928 | tf_op jit(solution)/shard_map/ppermute | solution.py:24
  131.8 2.2 %collective-permute-start.3 = (bf16[532,10]{1,0:T(8,128)(2,1)S(1)}, bf16[532,10]{1,0:T(8,128)(2,1)S(1)}, u32[]{:S(2)}, u32[]{:S(2)}) collective-permute-start(bf16[532,10]{1,0:T(8,128)(2,1)S(1)} %get-tuple-element.56), channel_id=1, source_target_pairs={{1,0},{2,1},{3,2},{4,3},{5,4},{6,5},{7,6},{8,7},{9,8},{10,9},{11,1... | collective-permute-start | bytes 31928 | tf_op jit(solution)/shard_map/ppermute | solution.py:26
  134.0 0.7 fusion.84
  134.7 0.6 collective-permute-done.2
  135.3 5.9 %collective-permute-done.3 = bf16[532,10]{1,0:T(8,128)(2,1)S(1)} collective-permute-done((bf16[532,10]{1,0:T(8,128)(2,1)S(1)}, bf16[532,10]{1,0:T(8,128)(2,1)S(1)}, u32[]{:S(2)}, u32[]{:S(2)}) %collective-permute-start.3) | collective-permute-done | bytes 10672 | tf_op jit(solution)/shard_map/ppermute | solution.py:26
  141.3 0.5 maximum_convert_fusion
  141.7 16.4 %fusion.28 = f32[512,532]{1,0:T(8,128)S(1)} fusion(f32[532,532]{1,0:T(8,128)S(1)} %maximum_convert_fusion, f32[]{:T(128)} %bitcast.40, f32[]{:T(128)} %bitcast.39, f32[]{:T(128)} %bitcast.38, f32[]{:T(128)} %bitcast.37, f32[]{:T(128)} %bitcast.36, f32[]{:T(128)} %bitcast.35, f32[]{:T(128)} %bitcast.34, f32[]{:T(128)} %bitcast.33, f32[]{:T(128)} %bitcast.32, ...), kind=kLoop, calls=%fused_computation.30 | loop fusion | flops 11167744 | bytes 23969876 | tf_op jit(solution)/shard_map/add | solution.py:88
  158.1 19.4 %fusion.48 = f32[512,512]{1,0:T(8,128)} fusion(f32[512,532]{1,0:T(8,128)S(1)} %fusion.28, f32[]{:T(128)} %bitcast.40, f32[]{:T(128)} %bitcast.39, f32[]{:T(128)} %bitcast.38, f32[]{:T(128)} %bitcast.37, f32[]{:T(128)} %bitcast.36, f32[]{:T(128)} %bitcast.35, f32[]{:T(128)} %bitcast.34, f32[]{:T(128)} %bitcast.33, f32[]{:T(128)} %bitcast.32, f32[]{:T(128)} %bitcast.31, ...), kind=kLoop, calls=%fused_computation.71 | loop fusion | flops 10747904 | bytes 23068756 | tf_op jit(solution)/shard_map/add | solution.py:96
  (11 shorter events, 0.2 us)
Async XLA Ops:
  2.7 37.1 %all-to-all-start.1 = ((bf16[16,1,2]{2,1,0:T(2,128)(2,1)}), bf16[16,1,2]{2,1,0:T(2,128)(2,1)S(1)}, u32[]{:S(2)}, u32[]{:S(2)}) async-start(bf16[16,1,2]{2,1,0:T(2,128)(2,1)} %all_to_all.12), calls=%async_computation.1 | async-start | bytes 16384 | tf_op jit(solution)/shard_map/all_to_all | solution.py:125
  39.9 8.1 %copy-start = (s32[2,1,32]{2,1,0:T(1,128)S(1)}, s32[2,1,32]{2,1,0:T(1,128)}, u32[]{:S(2)}) copy-start(s32[2,1,32]{2,1,0:T(1,128)} %param.11) | copy-start | bytes 772
  39.9 66.1 %all-to-all-start = ((bf16[16,2,256,256]{2,3,1,0:T(8,128)(2,1)}), bf16[16,2,256,256]{2,3,1,0:T(8,128)(2,1)}, u32[]{:S(2)}, u32[]{:S(2)}) async-start(bf16[16,2,256,256]{2,3,1,0:T(8,128)(2,1)} %copy.16), calls=%async_computation | async-start | bytes 8388608 | tf_op jit(solution)/shard_map/all_to_all | solution.py:124
  118.2 7.8 %collective-permute-start = (bf16[10,512]{1,0:T(8,128)(2,1)S(1)}, bf16[10,512]{1,0:T(8,128)(2,1)S(1)}, u32[]{:S(2)}, u32[]{:S(2)}) collective-permute-start(bf16[10,512]{1,0:T(8,128)(2,1)S(1)} %get-tuple-element.57), channel_id=1, source_target_pairs={{0,16},{16,32},{32,48},{48,64},{64,80},{80,96},{96,112},{1,17},{17... | collective-permute-start | bytes 30728 | tf_op jit(solution)/shard_map/ppermute | solution.py:24
  123.3 5.1 %collective-permute-start.1 = (bf16[10,512]{1,0:T(8,128)(2,1)S(1)}, bf16[10,512]{1,0:T(8,128)(2,1)S(1)}, u32[]{:S(2)}, u32[]{:S(2)}) collective-permute-start(bf16[10,512]{1,0:T(8,128)(2,1)S(1)} %get-tuple-element.58), channel_id=1, source_target_pairs={{16,0},{32,16},{48,32},{64,48},{80,64},{96,80},{112,96},{17,1},{33... | collective-permute-start | bytes 30728 | tf_op jit(solution)/shard_map/ppermute | solution.py:26
  128.5 6.8 %collective-permute-start.2 = (bf16[532,10]{1,0:T(8,128)(2,1)S(1)}, bf16[532,10]{1,0:T(8,128)(2,1)S(1)}, u32[]{:S(2)}, u32[]{:S(2)}) collective-permute-start(bf16[532,10]{1,0:T(8,128)(2,1)S(1)} %get-tuple-element.55), channel_id=1, source_target_pairs={{0,1},{1,2},{2,3},{3,4},{4,5},{5,6},{6,7},{7,8},{8,9},{9,10},{10,1... | collective-permute-start | bytes 31928 | tf_op jit(solution)/shard_map/ppermute | solution.py:24
  131.8 9.4 %collective-permute-start.3 = (bf16[532,10]{1,0:T(8,128)(2,1)S(1)}, bf16[532,10]{1,0:T(8,128)(2,1)S(1)}, u32[]{:S(2)}, u32[]{:S(2)}) collective-permute-start(bf16[532,10]{1,0:T(8,128)(2,1)S(1)} %get-tuple-element.56), channel_id=1, source_target_pairs={{1,0},{2,1},{3,2},{4,3},{5,4},{6,5},{7,6},{8,7},{9,8},{10,9},{11,1... | collective-permute-start | bytes 31928 | tf_op jit(solution)/shard_map/ppermute | solution.py:26
where the time goes:
time: 179 us; the launch traced here: 178 us
  waiting for transfers between devices  60.5 us (34%)
  other arithmetic  51.5 us (29%)
  starting transfers between devices  27 us (15%)
  matrix products  21.5 us (12%)
  local copies, waits for them, and re-layouts  16.2 us (9%)
    all_to_all x1, waiting for transfers between devices, body(): lax.all_to_all(send_matched, 'skyx', split_axis=0, concat_axis=0, tiled=T...  51.5 us
    add x1, other arithmetic, horizontal_pass(): result = result + kernel[step] * vert[:, step:step + out_cols]  19.4 us
    add x1, other arithmetic, vertical_pass(): vert = vert + kernel[step] * extended[step:step + out_rows, :]  16.4 us
    dot_general x1, matrix products, coadd_patch(): numer = jnp.dot(placed, col_place, preferred_element_type=jnp.float32)  10.5 us
    dot_general x4, matrix products, match_batch(): jnp.einsum('mbik,bjk->mbij', vert, basis, preferred_element_type=jnp.floa...  9.31 us
    ppermute x2, starting transfers between devices, padded(): lax.ppermute(tail, axis, [(i, (i + 1) % count) for i in range(ends)])  8.48 us
    ppermute x2, waiting for transfers between devices, padded(): lax.ppermute(head, axis, [((i + 1) % count, i) for i in range(ends)])  8.35 us
    all_to_all x1, starting transfers between devices, body(): lax.all_to_all(send_weight, 'skyx', split_axis=0, concat_axis=0, tiled=True)  7.62 us
  transfers between devices with their start and end apart: 6, of which 4 were waited for; matrix products, arithmetic and copies ran while one was open for 22% of the time, Pallas kernels for 0%

commit v1 on v0

v1 whole, which is shorter than its diff:
```python
import numpy as np
import jax
import jax.numpy as jnp
from jax import lax
from jax.sharding import PartitionSpec as P

NB = 5
REACH = 10
CAP = 2
PATCH = 512


basis_widths = (1.0, 1.8, 2.6, 3.6, 5.0)
detect_width = 2.5


def band_matrices(size):
    rows = np.arange(size, dtype=np.int32)[:, None]
    cols = np.arange(size, dtype=np.int32)[None, :]
    gap = (cols - rows).astype(np.float32)
    inside = np.abs(cols - rows) <= REACH
    taps = np.arange(-REACH, REACH + 1).astype(np.float32)
    mats = []
    for width in basis_widths:
        scale = np.float32(2.0 * width * width)
        total = np.sum(np.exp(-taps * taps / scale), dtype=np.float32)
        mats.append(np.where(inside, np.exp(-gap * gap / scale) / total, np.float32(0.0)))
    return np.stack(mats).astype(np.float32).astype(jnp.bfloat16)


def detect_band(out_size, in_size):
    taps = jnp.arange(-REACH, REACH + 1).astype(jnp.float32)
    kernel = jnp.exp(-taps * taps / (2.0 * detect_width * detect_width))
    kernel = kernel / jnp.sum(kernel)
    rows = jnp.arange(out_size, dtype=jnp.int32)[:, None]
    cols = jnp.arange(in_size, dtype=jnp.int32)[None, :]
    gap = cols - rows
    inside = (gap >= 0) & (gap <= 2 * REACH)
    return jnp.where(inside, kernel[jnp.clip(gap, 0, 2 * REACH)], 0.0)


def match_all(tiles, coeffs, basis):
    vert = jnp.einsum(
        "bij,mjk->mbik", basis, tiles, preferred_element_type=jnp.float32
    ).astype(jnp.bfloat16)
    horiz = jnp.einsum("mbik,bjk->mbij", vert, basis, preferred_element_type=jnp.float32)
    return jnp.sum(coeffs.astype(jnp.float32) * horiz, axis=1).astype(jnp.bfloat16)


def coadd_patch(matched, slot_weight, offsets, patch):
    slot_count = matched.shape[0]
    size = matched.shape[1]
    local = jnp.arange(size, dtype=jnp.int32)
    pixel = jnp.arange(patch, dtype=jnp.int32)
    row_hit = offsets[0][:, None, None] + local[None, :, None] == pixel[None, None, :]
    col_hit = offsets[1][:, None, None] + local[None, :, None] == pixel[None, None, :]
    row_place = row_hit.astype(jnp.bfloat16)
    placed = jnp.einsum("sip,sij->psj", row_place, matched, preferred_element_type=jnp.float32)
    placed = placed.astype(jnp.bfloat16).reshape(patch, slot_count * size)
    zero_weight = jnp.zeros((), jnp.bfloat16)
    col_place = jnp.where(col_hit, slot_weight[:, None, None], zero_weight).reshape(
        slot_count * size, patch
    )
    numer = jnp.dot(placed, col_place, preferred_element_type=jnp.float32)
    row_cover = jnp.any(row_hit, axis=1).astype(jnp.float32)
    col_cover = jnp.where(jnp.any(col_hit, axis=1), slot_weight[:, None].astype(jnp.float32), 0.0)
    cover = jnp.dot(
        row_cover.T, col_cover, precision=lax.Precision.HIGHEST, preferred_element_type=jnp.float32
    )
    return numer / (1.0 + cover)


def halo_extend(coadd):
    ny = lax.axis_size("skyy")
    nx = lax.axis_size("skyx")
    r = REACH
    both = ("skyy", "skyx")

    def flat(a, b):
        return a * nx + b

    down = [(i, i + 1) for i in range(ny - 1)]
    up = [(i + 1, i) for i in range(ny - 1)]
    right = [(j, j + 1) for j in range(nx - 1)]
    left = [(j + 1, j) for j in range(nx - 1)]
    top = lax.ppermute(coadd[-r:, :], "skyy", down)
    bottom = lax.ppermute(coadd[:r, :], "skyy", up)
    west = lax.ppermute(coadd[:, -r:], "skyx", right)
    east = lax.ppermute(coadd[:, :r], "skyx", left)
    tl = lax.ppermute(
        coadd[-r:, -r:], both,
        [(flat(a, b), flat(a + 1, b + 1)) for a in range(ny - 1) for b in range(nx - 1)],
    )
    tr = lax.ppermute(
        coadd[-r:, :r], both,
        [(flat(a, b + 1), flat(a + 1, b)) for a in range(ny - 1) for b in range(nx - 1)],
    )
    bl = lax.ppermute(
        coadd[:r, -r:], both,
        [(flat(a + 1, b), flat(a, b + 1)) for a in range(ny - 1) for b in range(nx - 1)],
    )
    br = lax.ppermute(
        coadd[:r, :r], both,
        [(flat(a + 1, b + 1), flat(a, b)) for a in range(ny - 1) for b in range(nx - 1)],
    )
    upper = jnp.concatenate([tl, top, tr], axis=1)
    middle = jnp.concatenate([west, coadd, east], axis=1)
    lower = jnp.concatenate([bl, bottom, br], axis=1)
    return jnp.concatenate([upper, middle, lower], axis=0)


def body(tiles, coeffs, weights, tile_slot, slot_offset):
    count = tiles.shape[1]
    size = tiles.shape[2]
    columns = lax.axis_size("skyx")
    slots = columns * CAP
    patch = PATCH
    basis = jnp.asarray(band_matrices(size))
    own_tiles = tiles[0]
    own_coeffs = coeffs[0]
    own_weight = weights[0]
    own_slot = tile_slot[0]
    offsets = slot_offset[:, 0, :]
    hits = own_slot[None, :] == jnp.arange(slots, dtype=jnp.int32)[:, None]
    present = jnp.any(hits, axis=1)
    which = jnp.sum(jnp.where(hits, jnp.arange(count, dtype=jnp.int32)[None, :], 0), axis=1)
    send_weight = jnp.where(present, own_weight[which], jnp.zeros((), jnp.bfloat16))
    send_weight = send_weight.reshape(columns, CAP)
    own_matched = match_all(own_tiles, own_coeffs, basis)
    send_matched = jnp.where(
        present[:, None, None], own_matched[which], jnp.zeros((), jnp.bfloat16)
    ).reshape(columns, CAP, size, size)
    matched, recv_weight = (
        lax.all_to_all(send_matched, "skyx", split_axis=0, concat_axis=0, tiled=True),
        lax.all_to_all(send_weight, "skyx", split_axis=0, concat_axis=0, tiled=True),
    )
    matched = matched.reshape(slots, size, size)
    recv_weight = recv_weight.reshape(slots)
    coadd = coadd_patch(matched, recv_weight, offsets, patch)
    extended = halo_extend(coadd)
    ext = patch + 2 * REACH
    band = detect_band(patch, ext)
    high = lax.Precision.HIGH
    vert = jnp.dot(band, extended, precision=high, preferred_element_type=jnp.float32)
    detection = jnp.dot(vert, band.T, precision=high, preferred_element_type=jnp.float32)
    return (coadd, detection)


def solution(mesh):
    in_specs = (
        P("skyy", "skyx", None, None),
        P("skyy", "skyx", None, None, None),
        P("skyy", "skyx"),
        P("skyy", "skyx"),
        P(None, "skyy", "skyx"),
    )
    out_specs = (P("skyy", "skyx"), P("skyy", "skyx"))
    return jax.shard_map(body, mesh=mesh, in_specs=in_specs, out_specs=out_specs, check_vma=False)
```

time: 179 us -> 175 us (0.978)
  other arithmetic: 51.5 us -> 12.8 us
  matrix products: 21.5 us -> 49.3 us
  starting transfers between devices: 27 us -> 42.9 us
  waiting for transfers between devices: 60.5 us -> 51.7 us
  local copies, waits for them, and re-layouts: 16.2 us -> 14.3 us
    add x2 -> x0, other arithmetic: 35.8 us -> none  [the longest x1 19.4 us: horizontal_pass(): result = result + kernel[step] * vert[:, step:step + out_cols]]
    dot_general x4, matrix products: 9.31 us -> 44 us  [the longest x1 17.9 us: body(): jnp.dot(vert, band.T, precision=high, preferred_element_type=jnp.float32)]
    ppermute x4 -> x8, starting transfers between devices: 12.6 us -> 28.5 us  [the longest x1 6.16 us: halo_extend(): west = lax.ppermute(coadd[:, -r:], 'skyx', right)]
    gather x0 -> x5, local copies, waits for them, and re-layouts: none -> 11.9 us  [the longest x2 9.16 us: body(): own_matched[which]]
    ppermute x4 -> x8, waiting for transfers between devices: 8.99 us -> 0.02 us  [the longest x1 0.01 us: halo_extend(): lax.ppermute(coadd[:r, :r], both, [(flat(a + 1, b + 1), flat(a, b)) for a...]
    reshape x1 -> x0, local copies, waits for them, and re-layouts: 6.39 us -> none  [body(): send_matched = send_matched.reshape(columns, CAP, size, size)]
    dot_general x1, matrix products: 10.5 us -> 4.51 us  [coadd_patch(): numer = jnp.dot(placed, col_place, preferred_element_type=jnp.float32)]
    select_n x1 -> x3, other arithmetic: 0.66 us -> 4.51 us  [the longest x1 4.49 us: body(): jnp.where(present[:, None, None], own_matched[which], jnp.zeros((), jnp.b...]
  transfers between devices with their start and end apart: 6 -> 10, of which waited for: 4 -> 1; matrix products, arithmetic and copies ran while one was open for 22% -> 17% of each run, Pallas kernels for 0% -> 0%
where the time goes in v1:
time: 175 us; the launch traced here: 172 us
  waiting for transfers between devices  51.7 us (30%)
  matrix products  49.3 us (28%)
  starting transfers between devices  42.9 us (25%)
  local copies, waits for them, and re-layouts  14.3 us (8%)
  other arithmetic  12.8 us (7%)
    all_to_all x1, waiting for transfers between devices, body(): lax.all_to_all(send_matched, 'skyx', split_axis=0, concat_axis=0, tiled=T...  51.6 us
    dot_general x1, matrix products, body(): jnp.dot(vert, band.T, precision=high, preferred_element_type=jnp.float32)  17.9 us
    dot_general x1, matrix products, body(): jnp.dot(band, extended, precision=high, preferred_element_type=jnp.float32)  15 us
    gather x2, local copies, waits for them, and re-layouts, body(): own_matched[which]  9.16 us
    all_to_all x1, starting transfers between devices, body(): lax.all_to_all(send_weight, 'skyx', split_axis=0, concat_axis=0, tiled=True)  7.62 us
    all_to_all x1, starting transfers between devices, body(): lax.all_to_all(send_matched, 'skyx', split_axis=0, concat_axis=0, tiled=T...  6.8 us
    ppermute x1, starting transfers between devices, halo_extend(): west = lax.ppermute(coadd[:, -r:], 'skyx', right)  6.16 us
    dot_general x1, matrix products, coadd_patch(): jnp.einsum('sip,sij->psj', row_place, matched, preferred_element_type=jnp...  5.75 us
  transfers between devices with their start and end apart: 10, of which 1 were waited for; matrix products, arithmetic and copies ran while one was open for 17% of the time, Pallas kernels for 0%

profile of v1, /device:TPU:29, one launch (start us, length us, event | category | flops | bytes accessed | tf_op | source)
XLA Modules:
  0.0 171.9 jit_solution(17830028522675865757)
XLA Ops:
  0.6 0.0 copy-start
  0.6 0.8 fusion.103
  1.5 0.7 select_reduce_fusion
  2.2 1.4 gather_fusion.1
  3.6 0.7 select_n.66
  4.3 7.6 %all-to-all-start.1 = ((bf16[16,1,2]{2,1,0:T(2,128)(2,1)}), bf16[16,1,2]{2,1,0:T(2,128)(2,1)S(1)}, u32[]{:S(2)}, u32[]{:S(2)}) async-start(bf16[16,1,2]{2,1,0:T(2,128)(2,1)} %select_n.66), calls=%async_computation.1 | async-start | bytes 16384 | tf_op jit(solution)/shard_map/all_to_all | solution.py:135
  11.9 0.1 broadcast_in_dim.72
  12.0 0.0 copy-done
  12.0 5.4 %fusion.4 = bf16[8,256,256]{2,1,0:T(8,128)(2,1)S(1)} fusion(bf16[1,8,5,256,256]{4,3,2,1,0:T(8,128)(2,1)} %param.7, bf16[5,256,256,1]{2,1,3,0:T(8,128)(2,1)} %constant.53, bf16[1,8,256,256]{3,2,1,0:T(8,128)(2,1)S(1)} %copy-done), kind=kOutput, calls=%fused_computation.9 | convolution fusion | flops 2694316032 | bytes 7995392 | tf_op jit(solution)/shard_map/mbik,bjk->mbij/dot_general | solution.py:46
  17.4 2.8 %gather_fusion = bf16[32,256,256]{2,1,0:T(8,128)(2,1)} fusion(bf16[8,256,256]{2,1,0:T(8,128)(2,1)S(1)} %fusion.4, s32[1024]{0:T(1024)S(1)} %pad_clamp_fusion), kind=kCustom, calls=%fused_computation | custom fusion | bytes 8388736 | tf_op jit(solution)/shard_map/gather | solution.py:131
  20.2 6.4 %copy.38 = bf16[16,2,256,256]{2,3,1,0:T(8,128)(2,1)} copy(bf16[16,2,256,256]{3,2,1,0:T(8,128)(2,1)} %bitcast.191) | data formatting | bytes 8388608 | tf_op jit(solution)/shard_map/gather | solution.py:131
  26.6 4.5 %broadcast_select_fusion = bf16[16,2,256,256]{2,3,1,0:T(8,128)(2,1)} fusion(bf16[16,2,256,256]{2,3,1,0:T(8,128)(2,1)} %copy.38, pred[16,2]{1,0:T(8,128)(4,1)S(1)} %broadcast_in_dim.72), kind=kLoop, calls=%fused_computation.20 | loop fusion | flops 2097152 | bytes 8388640 | tf_op jit(solution)/shard_map/jit(_where)/select_n | solution.py:130
  31.1 0.0 all-to-all-done.1
  31.1 6.8 %all-to-all-start = ((bf16[16,2,256,256]{2,3,1,0:T(8,128)(2,1)}), bf16[16,2,256,256]{2,3,1,0:T(8,128)(2,1)}, u32[]{:S(2)}, u32[]{:S(2)}) async-start(bf16[16,2,256,256]{2,3,1,0:T(8,128)(2,1)} %broadcast_select_fusion), calls=%async_computation | async-start | bytes 8388608 | tf_op jit(solution)/shard_map/all_to_all | solution.py:134
  37.9 0.6 fusion.107
  38.5 0.7 broadcast_divide_fusion
  39.2 0.7 fusion.160
  39.9 0.0 copy-done.1
  39.9 0.1 iota_add_fusion
  40.0 2.3 %fusion = pred[32,512]{1,0:T(8,128)(4,1)S(1)} fusion(s32[32,256]{1,0:T(8,128)S(1)} %get-tuple-element.43), kind=kLoop, calls=%fused_computation.3 | loop fusion | flops 8372224 | bytes 49152 | tf_op jit(solution)/shard_map/reduce_or | solution.py:66
  42.3 3.1 %fusion.2 = pred[32,512]{1,0:T(8,128)(4,1)S(1)} fusion(s32[32,256]{1,0:T(8,128)S(1)} %get-tuple-element.44), kind=kLoop, calls=%fused_computation.6 | loop fusion | flops 8372224 | bytes 49152 | tf_op jit(solution)/shard_map/reduce_or | solution.py:65
  45.4 0.1 broadcast_in_dim.78
  45.5 51.6 %all-to-all-done = bf16[16,2,256,256]{2,3,1,0:T(8,128)(2,1)} async-done(((bf16[16,2,256,256]{2,3,1,0:T(8,128)(2,1)}), bf16[16,2,256,256]{2,3,1,0:T(8,128)(2,1)}, u32[]{:S(2)}, u32[]{:S(2)}) %all-to-all-start) | async-done | bytes 4194336 | tf_op jit(solution)/shard_map/all_to_all | solution.py:134
  97.2 5.8 %fusion.177 = bf16[512,32,256]{0,2,1:T(8,128)(2,1)S(1)} fusion(bf16[32,256,256]{1,2,0:T(8,128)(2,1)} %bitcast.11, s32[32,256]{1,0:T(8,128)S(1)} %get-tuple-element.44), kind=kOutput, calls=%fused_computation.11.clone.clone.clone.2 | convolution fusion | flops 2155872256 | bytes 12615680 | tf_op jit(solution)/shard_map/sip,sij->psj/dot_general | solution.py:58
  102.9 4.5 %fusion.38 = f32[512,512]{0,1:T(8,128)S(1)} fusion(s32[32,256]{1,0:T(8,128)S(1)} %get-tuple-element.43, bf16[32]{0:T(256)(128)(2,1)S(1)} %broadcast_in_dim.78, bf16[512,32,256]{0,2,1:T(8,128)(2,1)S(1)} %fusion.177), kind=kOutput, calls=%fused_computation.41 | convolution fusion | flops 4303355904 | bytes 9470016 | tf_op jit(solution)/shard_map/dot_general | solution.py:64
  107.5 0.8 fusion.43
  108.2 0.1 fusion.157
  108.3 0.1 fusion.158
  108.5 1.9 %collective-permute-start.7 = (f32[10,10]{0,1:T(8,128)S(1)}, f32[10,10]{0,1:T(8,128)S(1)}, u32[]{:S(2)}, u32[]{:S(2)}) collective-permute-start(f32[10,10]{0,1:T(8,128)S(1)} %get-tuple-element.13), channel_id=1, source_target_pairs={{17,0},{18,1},{19,2},{20,3},{21,4},{22,5},{23,6},{24,7},{25,8},{26... | collective-permute-start | bytes 1208 | tf_op jit(solution)/shard_map/ppermute | solution.py:102
  110.4 5.7 %collective-permute-start.5 = (f32[10,10]{0,1:T(8,128)S(1)}, f32[10,10]{0,1:T(8,128)S(1)}, u32[]{:S(2)}, u32[]{:S(2)}) collective-permute-start(f32[10,10]{0,1:T(8,128)S(1)} %get-tuple-element.14), channel_id=1, source_target_pairs={{16,1},{17,2},{18,3},{19,4},{20,5},{21,6},{22,7},{23,8},{24,9},{25... | collective-permute-start | bytes 1208 | tf_op jit(solution)/shard_map/ppermute | solution.py:98
  116.1 4.2 %collective-permute-start.6 = (f32[10,512]{0,1:T(8,128)S(1)}, f32[10,512]{0,1:T(8,128)S(1)}, u32[]{:S(2)}, u32[]{:S(2)}) collective-permute-start(f32[10,512]{0,1:T(8,128)S(1)} %get-tuple-element.17), channel_id=1, source_target_pairs={{16,0},{32,16},{48,32},{64,48},{80,64},{96,80},{112,96},{17,1},{33... | collective-permute-start | bytes 61448 | tf_op jit(solution)/shard_map/ppermute | solution.py:87
  120.3 1.9 %collective-permute-start.2 = (f32[10,10]{0,1:T(8,128)S(1)}, f32[10,10]{0,1:T(8,128)S(1)}, u32[]{:S(2)}, u32[]{:S(2)}) collective-permute-start(f32[10,10]{0,1:T(8,128)S(1)} %get-tuple-element.15), channel_id=1, source_target_pairs={{1,16},{2,17},{3,18},{4,19},{5,20},{6,21},{7,22},{8,23},{9,24},{10... | collective-permute-start | bytes 1208 | tf_op jit(solution)/shard_map/ppermute | solution.py:94
  122.3 2.1 %collective-permute-start.4 = (f32[512,10]{0,1:T(8,128)S(1)}, f32[512,10]{0,1:T(8,128)S(1)}, u32[]{:S(2)}, u32[]{:S(2)}) collective-permute-start(f32[512,10]{0,1:T(8,128)S(1)} %get-tuple-element.19), channel_id=1, source_target_pairs={{1,0},{2,1},{3,2},{4,3},{5,4},{6,5},{7,6},{8,7},{9,8},{10,9},{11,1... | collective-permute-start | bytes 61448 | tf_op jit(solution)/shard_map/ppermute | solution.py:89
  124.4 0.0 collective-permute-done.7
  124.4 6.2 %collective-permute-start.3 = (f32[512,10]{0,1:T(8,128)S(1)}, f32[512,10]{0,1:T(8,128)S(1)}, u32[]{:S(2)}, u32[]{:S(2)}) collective-permute-start(f32[512,10]{0,1:T(8,128)S(1)} %get-tuple-element.18), channel_id=1, source_target_pairs={{0,1},{1,2},{2,3},{3,4},{4,5},{5,6},{6,7},{7,8},{8,9},{9,10},{10,1... | collective-permute-start | bytes 61448 | tf_op jit(solution)/shard_map/ppermute | solution.py:88
  130.5 0.0 collective-permute-done.5
  130.5 2.9 %collective-permute-start.1 = (f32[10,512]{0,1:T(8,128)S(1)}, f32[10,512]{0,1:T(8,128)S(1)}, u32[]{:S(2)}, u32[]{:S(2)}) collective-permute-start(f32[10,512]{0,1:T(8,128)S(1)} %get-tuple-element.16), channel_id=1, source_target_pairs={{0,16},{16,32},{32,48},{48,64},{64,80},{80,96},{96,112},{1,17},{17... | collective-permute-start | bytes 61448 | tf_op jit(solution)/shard_map/ppermute | solution.py:86
  133.4 0.0 collective-permute-done.2
  133.4 3.6 %collective-permute-start = (f32[10,10]{0,1:T(8,128)S(1)}, f32[10,10]{0,1:T(8,128)S(1)}, u32[]{:S(2)}, u32[]{:S(2)}) collective-permute-start(f32[10,10]{0,1:T(8,128)S(1)} %get-tuple-element.12), channel_id=1, source_target_pairs={{0,17},{1,18},{2,19},{3,20},{4,21},{5,22},{6,23},{7,24},{8,25},{9,... | collective-permute-start | bytes 1208 | tf_op jit(solution)/shard_map/ppermute | solution.py:90
  137.0 0.6 fusion.161
  137.6 1.3 copy.41
  138.9 0.0 collective-permute-done
  139.0 0.0 collective-permute-done.6
  139.0 0.0 collective-permute-done.4
  139.0 0.0 collective-permute-done.3
  139.0 0.0 collective-permute-done.1
  139.0 15.0 %fusion.20 = f32[512,532]{0,1:T(8,128)S(1)} fusion(f32[10,10]{0,1:T(8,128)S(1)} %collective-permute-done.7, f32[10,512]{0,1:T(8,128)S(1)} %collective-permute-done.6, f32[10,10]{0,1:T(8,128)S(1)} %collective-permute-done.5, f32[512,10]{0,1:T(8,128)S(1)} %collective-permute-done.4, f32[512,512]{0,1:T(8,128)S(1)} %fusion.43, ...), kind=kOutput, calls=%fused_computation.23 | convolution fusion | flops 885333120 | bytes 2221716 | tf_op jit(solution)/shard_map/dot_general | solution.py:144
  154.0 17.9 %fusion.97 = f32[512,512]{1,0:T(8,128)} fusion(f32[512,532]{0,1:T(8,128)S(1)} %fusion.20, f32[]{:T(128)} %bitcast.45, f32[]{:T(128)} %bitcast.46, f32[]{:T(128)} %bitcast.47, f32[]{:T(128)} %bitcast.48, f32[]{:T(128)} %bitcast.49, f32[]{:T(128)} %bitcast.51, f32[]{:T(128)} %bitcast.50, f32[]{:T(128)} %bitcast.18, f32[]{:T(128)} %bitcast.20, f32[]{:T(128)} %bitcast.22, ...), kind=kOutput, calls=%fused_computation.98 | convolution fusion | flops 850382848 | bytes 2138196 | tf_op jit(solution)/shard_map/dot_general | solution.py:145
  (8 shorter events, 0.1 us)
Async XLA Ops:
  0.6 11.4 %copy-start = (bf16[1,8,256,256]{3,2,1,0:T(8,128)(2,1)S(1)}, bf16[1,8,256,256]{3,2,1,0:T(8,128)(2,1)}, u32[]{:S(2)}) copy-start(bf16[1,8,256,256]{3,2,1,0:T(8,128)(2,1)} %param.6) | copy-start | bytes 3145732
  4.3 26.8 %all-to-all-start.1 = ((bf16[16,1,2]{2,1,0:T(2,128)(2,1)}), bf16[16,1,2]{2,1,0:T(2,128)(2,1)S(1)}, u32[]{:S(2)}, u32[]{:S(2)}) async-start(bf16[16,1,2]{2,1,0:T(2,128)(2,1)} %select_n.66), calls=%async_computation.1 | async-start | bytes 16384 | tf_op jit(solution)/shard_map/all_to_all | solution.py:135
  31.1 8.8 %copy-start.1 = (s32[2,1,32]{2,1,0:T(1,128)S(1)}, s32[2,1,32]{2,1,0:T(1,128)}, u32[]{:S(2)}) copy-start(s32[2,1,32]{2,1,0:T(1,128)} %param.10) | copy-start | bytes 772
  31.1 66.1 %all-to-all-start = ((bf16[16,2,256,256]{2,3,1,0:T(8,128)(2,1)}), bf16[16,2,256,256]{2,3,1,0:T(8,128)(2,1)}, u32[]{:S(2)}, u32[]{:S(2)}) async-start(bf16[16,2,256,256]{2,3,1,0:T(8,128)(2,1)} %broadcast_select_fusion), calls=%async_computation | async-start | bytes 8388608 | tf_op jit(solution)/shard_map/all_to_all | solution.py:134
  108.5 15.9 %collective-permute-start.7 = (f32[10,10]{0,1:T(8,128)S(1)}, f32[10,10]{0,1:T(8,128)S(1)}, u32[]{:S(2)}, u32[]{:S(2)}) collective-permute-start(f32[10,10]{0,1:T(8,128)S(1)} %get-tuple-element.13), channel_id=1, source_target_pairs={{17,0},{18,1},{19,2},{20,3},{21,4},{22,5},{23,6},{24,7},{25,8},{26... | collective-permute-start | bytes 1208 | tf_op jit(solution)/shard_map/ppermute | solution.py:102
  110.4 20.2 %collective-permute-start.5 = (f32[10,10]{0,1:T(8,128)S(1)}, f32[10,10]{0,1:T(8,128)S(1)}, u32[]{:S(2)}, u32[]{:S(2)}) collective-permute-start(f32[10,10]{0,1:T(8,128)S(1)} %get-tuple-element.14), channel_id=1, source_target_pairs={{16,1},{17,2},{18,3},{19,4},{20,5},{21,6},{22,7},{23,8},{24,9},{25... | collective-permute-start | bytes 1208 | tf_op jit(solution)/shard_map/ppermute | solution.py:98
  116.1 22.8 %collective-permute-start.6 = (f32[10,512]{0,1:T(8,128)S(1)}, f32[10,512]{0,1:T(8,128)S(1)}, u32[]{:S(2)}, u32[]{:S(2)}) collective-permute-start(f32[10,512]{0,1:T(8,128)S(1)} %get-tuple-element.17), channel_id=1, source_target_pairs={{16,0},{32,16},{48,32},{64,48},{80,64},{96,80},{112,96},{17,1},{33... | collective-permute-start | bytes 61448 | tf_op jit(solution)/shard_map/ppermute | solution.py:87
  120.3 13.1 %collective-permute-start.2 = (f32[10,10]{0,1:T(8,128)S(1)}, f32[10,10]{0,1:T(8,128)S(1)}, u32[]{:S(2)}, u32[]{:S(2)}) collective-permute-start(f32[10,10]{0,1:T(8,128)S(1)} %get-tuple-element.15), channel_id=1, source_target_pairs={{1,16},{2,17},{3,18},{4,19},{5,20},{6,21},{7,22},{8,23},{9,24},{10... | collective-permute-start | bytes 1208 | tf_op jit(solution)/shard_map/ppermute | solution.py:94
  122.3 16.7 %collective-permute-start.4 = (f32[512,10]{0,1:T(8,128)S(1)}, f32[512,10]{0,1:T(8,128)S(1)}, u32[]{:S(2)}, u32[]{:S(2)}) collective-permute-start(f32[512,10]{0,1:T(8,128)S(1)} %get-tuple-element.19), channel_id=1, source_target_pairs={{1,0},{2,1},{3,2},{4,3},{5,4},{6,5},{7,6},{8,7},{9,8},{10,9},{11,1... | collective-permute-start | bytes 61448 | tf_op jit(solution)/shard_map/ppermute | solution.py:89
  124.4 14.6 %collective-permute-start.3 = (f32[512,10]{0,1:T(8,128)S(1)}, f32[512,10]{0,1:T(8,128)S(1)}, u32[]{:S(2)}, u32[]{:S(2)}) collective-permute-start(f32[512,10]{0,1:T(8,128)S(1)} %get-tuple-element.18), channel_id=1, source_target_pairs={{0,1},{1,2},{2,3},{3,4},{4,5},{5,6},{6,7},{7,8},{8,9},{9,10},{10,1... | collective-permute-start | bytes 61448 | tf_op jit(solution)/shard_map/ppermute | solution.py:88
  130.5 8.4 %collective-permute-start.1 = (f32[10,512]{0,1:T(8,128)S(1)}, f32[10,512]{0,1:T(8,128)S(1)}, u32[]{:S(2)}, u32[]{:S(2)}) collective-permute-start(f32[10,512]{0,1:T(8,128)S(1)} %get-tuple-element.16), channel_id=1, source_target_pairs={{0,16},{16,32},{32,48},{48,64},{64,80},{80,96},{96,112},{1,17},{17... | collective-permute-start | bytes 61448 | tf_op jit(solution)/shard_map/ppermute | solution.py:86
  133.4 5.5 %collective-permute-start = (f32[10,10]{0,1:T(8,128)S(1)}, f32[10,10]{0,1:T(8,128)S(1)}, u32[]{:S(2)}, u32[]{:S(2)}) collective-permute-start(f32[10,10]{0,1:T(8,128)S(1)} %get-tuple-element.12), channel_id=1, source_target_pairs={{0,17},{1,18},{2,19},{3,20},{4,21},{5,22},{6,23},{7,24},{8,25},{9,... | collective-permute-start | bytes 1208 | tf_op jit(solution)/shard_map/ppermute | solution.py:90

commit v2 on v1

v2 whole, which is shorter than its diff:
```python
import numpy as np
import jax
import jax.numpy as jnp
from jax import lax
from jax.sharding import PartitionSpec as P

NB = 5
REACH = 10
CAP = 2
PATCH = 512


basis_widths = (1.0, 1.8, 2.6, 3.6, 5.0)
detect_width = 2.5


def band_matrices(size):
    rows = np.arange(size, dtype=np.int32)[:, None]
    cols = np.arange(size, dtype=np.int32)[None, :]
    gap = (cols - rows).astype(np.float32)
    inside = np.abs(cols - rows) <= REACH
    taps = np.arange(-REACH, REACH + 1).astype(np.float32)
    mats = []
    for width in basis_widths:
        scale = np.float32(2.0 * width * width)
        total = np.sum(np.exp(-taps * taps / scale), dtype=np.float32)
        mats.append(np.where(inside, np.exp(-gap * gap / scale) / total, np.float32(0.0)))
    return np.stack(mats).astype(np.float32).astype(jnp.bfloat16)


def detect_band(out_size, in_size):
    taps = jnp.arange(-REACH, REACH + 1).astype(jnp.float32)
    kernel = jnp.exp(-taps * taps / (2.0 * detect_width * detect_width))
    kernel = kernel / jnp.sum(kernel)
    rows = jnp.arange(out_size, dtype=jnp.int32)[:, None]
    cols = jnp.arange(in_size, dtype=jnp.int32)[None, :]
    gap = cols - rows
    inside = (gap >= 0) & (gap <= 2 * REACH)
    return jnp.where(inside, kernel[jnp.clip(gap, 0, 2 * REACH)], 0.0)


def match_all(tiles, coeffs, basis):
    vert = jnp.einsum(
        "bij,mjk->mbik", basis, tiles, preferred_element_type=jnp.float32
    ).astype(jnp.bfloat16)
    horiz = jnp.einsum("mbik,bjk->mbij", vert, basis, preferred_element_type=jnp.float32)
    return jnp.sum(coeffs.astype(jnp.float32) * horiz, axis=1).astype(jnp.bfloat16)


def coadd_patch(matched, slot_weight, offsets, patch):
    slot_count = matched.shape[0]
    size = matched.shape[1]
    local = jnp.arange(size, dtype=jnp.int32)
    pixel = jnp.arange(patch, dtype=jnp.int32)
    col_hit = offsets[1][:, None, None] + local[None, :, None] == pixel[None, None, :]
    row_hit = offsets[0][None, :, None] + local[None, None, :] == pixel[:, None, None]
    col_place = col_hit.astype(jnp.bfloat16)
    shifted = jnp.einsum(
        "sij,sjq->siq", matched, col_place, preferred_element_type=jnp.float32
    ).astype(jnp.bfloat16)
    zero_weight = jnp.zeros((), jnp.bfloat16)
    row_place = jnp.where(row_hit, slot_weight[None, :, None], zero_weight)
    numer = jnp.dot(
        row_place.reshape(patch, slot_count * size),
        shifted.reshape(slot_count * size, patch),
        preferred_element_type=jnp.float32,
    )
    row_cover = jnp.where(jnp.any(row_hit, axis=2), slot_weight[None, :], zero_weight)
    col_cover = jnp.any(col_hit, axis=1).astype(jnp.bfloat16)
    cover = jnp.dot(row_cover, col_cover, preferred_element_type=jnp.float32)
    return numer / (1.0 + cover)


def split(x):
    hi = lax.reduce_precision(x, exponent_bits=8, mantissa_bits=7)
    return hi.astype(jnp.bfloat16), (x - hi).astype(jnp.bfloat16)


def mm3(a, b, dims=(((1,), (0,)), ((), ()))):
    ah, al = a
    bh, bl = b

    def one(x, y):
        return lax.dot_general(x, y, dims, preferred_element_type=jnp.float32)

    return one(ah, bh) + (one(al, bh) + one(ah, bl))


def detect(coadd):
    ny = lax.axis_size("skyy")
    nx = lax.axis_size("skyx")
    r = REACH
    patch = coadd.shape[0]
    band = detect_band(patch, patch + 2 * r)
    g_head = split(band[:, :r])
    g_mid = split(band[:, r:patch + r])
    g_tail = split(band[:, patch + r:])
    down = [(i, i + 1) for i in range(ny - 1)]
    up = [(i + 1, i) for i in range(ny - 1)]
    right = [(j, j + 1) for j in range(nx - 1)]
    left = [(j + 1, j) for j in range(nx - 1)]
    top = lax.ppermute(coadd[-r:, :], "skyy", down)
    bottom = lax.ppermute(coadd[:r, :], "skyy", up)
    vert = mm3(g_mid, split(coadd))
    vert = vert + (mm3(g_head, split(top)) + mm3(g_tail, split(bottom)))
    west = lax.ppermute(vert[:, -r:].T, "skyx", right)
    east = lax.ppermute(vert[:, :r].T, "skyx", left)
    on_cols = (((1,), (1,)), ((), ()))
    by_rows = (((0,), (1,)), ((), ()))
    result = mm3(split(vert), g_mid, on_cols)
    return result + (mm3(split(west), g_head, by_rows) + mm3(split(east), g_tail, by_rows))


def body(tiles, coeffs, weights, tile_slot, slot_offset):
    count = tiles.shape[1]
    size = tiles.shape[2]
    columns = lax.axis_size("skyx")
    slots = columns * CAP
    patch = PATCH
    basis = jnp.asarray(band_matrices(size))
    own_tiles = tiles[0]
    own_coeffs = coeffs[0]
    own_weight = weights[0]
    own_slot = tile_slot[0]
    offsets = slot_offset[:, 0, :]
    hits = own_slot[None, :] == jnp.arange(slots, dtype=jnp.int32)[:, None]
    present = jnp.any(hits, axis=1)
    which = jnp.sum(jnp.where(hits, jnp.arange(count, dtype=jnp.int32)[None, :], 0), axis=1)
    which = jnp.where(present, which, count)
    own_matched = match_all(own_tiles, own_coeffs, basis)
    extra = 16
    line = jnp.arange(extra, dtype=jnp.int32)[None, :, None] == 0
    weight_rows = jnp.where(
        line, own_weight[:, None, None], jnp.zeros((), jnp.bfloat16)
    ) * jnp.ones((1, 1, size), jnp.bfloat16)
    carry = jnp.concatenate([own_matched, weight_rows], axis=1)
    carry = jnp.concatenate([carry, jnp.zeros((1, size + extra, size), jnp.bfloat16)], axis=0)
    send = carry[which].reshape(columns, CAP, size + extra, size)
    recv = lax.all_to_all(send, "skyx", split_axis=0, concat_axis=0, tiled=True)
    recv = recv.reshape(slots, size + extra, size)
    matched = recv[:, :size, :]
    recv_weight = recv[:, size, 0]
    coadd = coadd_patch(matched, recv_weight, offsets, patch)
    detection = detect(coadd)
    return (coadd, detection)


def solution(mesh):
    in_specs = (
        P("skyy", "skyx", None, None),
        P("skyy", "skyx", None, None, None),
        P("skyy", "skyx"),
        P("skyy", "skyx"),
        P(None, "skyy", "skyx"),
    )
    out_specs = (P("skyy", "skyx"), P("skyy", "skyx"))
    return jax.shard_map(body, mesh=mesh, in_specs=in_specs, out_specs=out_specs, check_vma=False)
```

time: 175 us -> 122 us (0.70)
  the two profiles are of different devices: /device:TPU:29 before, /device:TPU:36 now
where the time goes in v2:
time: 122 us
  waiting for transfers between devices  48.6 us (40%)
  matrix products  24.9 us (20%)
  other arithmetic  22.9 us (19%)
  starting transfers between devices  18.8 us (15%)
  local copies, waits for them, and re-layouts  5.6 us (5%)
    all_to_all x1, waiting for transfers between devices, body(): recv = lax.all_to_all(send, 'skyx', split_axis=0, concat_axis=0, tiled=True)  43.6 us
    select_n x1, other arithmetic, detect_band(): return jnp.where(inside, kernel[jnp.clip(gap, 0, 2 * REACH)], 0.0)  13.4 us
    dot_general x18, matrix products, one(): return lax.dot_general(x, y, dims, preferred_element_type=jnp.float32)  8.85 us
    all_to_all x1, starting transfers between devices, body(): recv = lax.all_to_all(send, 'skyx', split_axis=0, concat_axis=0, tiled=True)  8.2 us
    dot_general x1, matrix products, coadd_patch(): jnp.einsum('sij,sjq->siq', matched, col_place, preferred_element_type=jnp...  5.76 us
    dot_general x1, matrix products, match_all(): jnp.einsum('mbik,bjk->mbij', vert, basis, preferred_element_type=jnp.floa...  5.4 us
    dot_general x1, matrix products, coadd_patch(): jnp.dot(row_place.reshape(patch, slot_count * size), shifted.reshape(slot...  4.52 us
    ppermute x1, starting transfers between devices, detect(): east = lax.ppermute(vert[:, :r].T, 'skyx', left)  4.13 us
  transfers between devices with their start and end apart: 5, of which 3 were waited for; matrix products, arithmetic and copies ran while one was open for 21% of the time, Pallas kernels for 0%

profile of v2, /device:TPU:36, one launch (start us, length us, event | category | flops | bytes accessed | tf_op | source)
XLA Modules:
  0.0 121.7 jit_solution(9239235668819078128)
XLA Ops:
  0.6 0.0 copy-start
  0.7 0.8 fusion.123
  1.5 0.7 select_reduce_fusion
  2.2 0.7 broadcast_select_fusion
  3.0 5.4 %fusion.4 = bf16[8,256,256]{2,1,0:T(8,128)(2,1)S(1)} fusion(bf16[1,8,5,256,256]{4,3,2,1,0:T(8,128)(2,1)} %param.7, bf16[5,256,256,1]{2,1,3,0:T(8,128)(2,1)} %constant.59, bf16[1,8,256,256]{3,2,1,0:T(8,128)(2,1)S(1)} %copy-done), kind=kOutput, calls=%fused_computation.8 | convolution fusion | flops 2694316032 | bytes 7995392 | tf_op jit(solution)/shard_map/mbik,bjk->mbij/dot_general | solution.py:46
  8.4 0.1 mul.14
  8.5 0.1 fusion.88
  8.6 2.9 %gather_fusion = bf16[32,272,256]{2,1,0:T(8,128)(2,1)} fusion(bf16[9,272,256]{2,1,0:T(8,128)(2,1)S(1)} %fusion.88, s32[1024]{0:T(1024)S(1)} %pad_clamp_fusion), kind=kCustom, calls=%fused_computation | custom fusion | bytes 8913024 | tf_op jit(solution)/shard_map/gather | solution.py:138
  11.5 8.2 %all-to-all-start = ((bf16[16,2,272,256]{3,2,1,0:T(8,128)(2,1)}), bf16[16,2,272,256]{3,2,1,0:T(8,128)(2,1)}, u32[]{:S(2)}, u32[]{:S(2)}) async-start(bf16[16,2,272,256]{3,2,1,0:T(8,128)(2,1)} %bitcast.161), calls=%async_computation | async-start | bytes 8912896 | tf_op jit(solution)/shard_map/all_to_all | solution.py:139
  19.7 0.6 fusion.127
  20.3 0.7 broadcast_divide_fusion
  21.0 0.7 fusion.132
  21.6 0.7 fusion.131
  22.4 0.1 iota_add_fusion
  22.4 13.4 %fusion.50 = f32[512,532]{1,0:T(8,128)S(1)} fusion(f32[]{:T(128)} %bitcast.44, f32[]{:T(128)} %bitcast.45, f32[]{:T(128)} %bitcast.46, f32[]{:T(128)} %bitcast.47, f32[]{:T(128)} %bitcast.48, f32[]{:T(128)} %bitcast.50, f32[]{:T(128)} %bitcast.49, f32[]{:T(128)} %bitcast.17, f32[]{:T(128)} %bitcast.19, f32[]{:T(128)} %bitcast.21, f32[]{:T(128)} %bitcast.23, ...), kind=kLoop, calls=%fused_computation.63 | loop fusion | flops 13619200 | bytes 1089620 | tf_op jit(solution)/shard_map/jit(_where)/select_n | solution.py:39
  35.9 0.1 reduce-precision_convert_fusion.4
  36.0 0.2 reduce-precision_convert_fusion.2
  36.3 2.3 %fusion.2 = pred[512,32]{0,1:T(8,128)(4,1)S(1)} fusion(s32[32,256]{1,0:T(8,128)S(1)} %get-tuple-element.32), kind=kLoop, calls=%fused_computation.5 | loop fusion | flops 8372224 | bytes 49152 | tf_op jit(solution)/shard_map/reduce_or | solution.py:68
  38.5 3.1 %fusion = pred[32,512]{1,0:T(8,128)(4,1)S(1)} fusion(s32[32,256]{1,0:T(8,128)S(1)} %get-tuple-element.31), kind=kLoop, calls=%fused_computation.2 | loop fusion | flops 8372224 | bytes 49152 | tf_op jit(solution)/shard_map/reduce_or | solution.py:69
  41.6 43.6 %all-to-all-done = bf16[16,2,272,256]{3,2,1,0:T(8,128)(2,1)} async-done(((bf16[16,2,272,256]{3,2,1,0:T(8,128)(2,1)}), bf16[16,2,272,256]{3,2,1,0:T(8,128)(2,1)}, u32[]{:S(2)}, u32[]{:S(2)}) %all-to-all-start) | async-done | bytes 4456480 | tf_op jit(solution)/shard_map/all_to_all | solution.py:139
  85.2 1.2 slice_reduce_fusion
  86.4 5.8 %fusion.158 = bf16[32,256,512]{2,1,0:T(8,128)(2,1)S(1)} fusion(s32[32,256]{1,0:T(8,128)S(1)} %get-tuple-element.31, bf16[32,272,256]{2,1,0:T(8,128)(2,1)} %bitcast.13), kind=kOutput, calls=%fused_computation.10.clone.clone.clone.2 | convolution fusion | flops 2155872256 | bytes 12615680 | tf_op jit(solution)/shard_map/sij,sjq->siq/dot_general | solution.py:58
  92.2 4.5 %fusion.30 = f32[512,512]{1,0:T(8,128)S(1)} fusion(s32[32,256]{1,0:T(8,128)S(1)} %get-tuple-element.32, bf16[32]{0:T(256)(128)(2,1)S(1)} %slice_reduce_fusion, bf16[32,256,512]{2,1,0:T(8,128)(2,1)S(1)} %fusion.158), kind=kOutput, calls=%fused_computation.48 | convolution fusion | flops 4303355904 | bytes 9470016 | tf_op jit(solution)/shard_map/dot_general | solution.py:63
  96.7 0.4 fusion.27
  97.1 0.8 fusion.99
  97.9 0.5 fusion.100
  98.4 1.9 %collective-permute-start.1 = (f32[10,512]{1,0:T(8,128)S(1)}, f32[10,512]{1,0:T(8,128)S(1)}, u32[]{:S(2)}, u32[]{:S(2)}) collective-permute-start(f32[10,512]{1,0:T(8,128)S(1)} %get-tuple-element.7), channel_id=1, source_target_pairs={{16,0},{32,16},{48,32},{64,48},{80,64},{96,80},{112,96},{17,1},{33... | collective-permute-start | bytes 61448 | tf_op jit(solution)/shard_map/ppermute | solution.py:103
  100.3 2.6 %collective-permute-start = (f32[10,512]{1,0:T(8,128)S(1)}, f32[10,512]{1,0:T(8,128)S(1)}, u32[]{:S(2)}, u32[]{:S(2)}) collective-permute-start(f32[10,512]{1,0:T(8,128)S(1)} %get-tuple-element.6), channel_id=1, source_target_pairs={{0,16},{16,32},{32,48},{48,64},{64,80},{80,96},{96,112},{1,17},{17... | collective-permute-start | bytes 61448 | tf_op jit(solution)/shard_map/ppermute | solution.py:102
  102.9 0.5 fusion.26
  103.4 0.3 fusion.117
  103.8 0.4 convolution_add_fusion.5
  104.2 0.3 convolution_add_fusion.6
  104.6 0.9 collective-permute-done
  105.5 0.3 fusion.119
  105.9 0.3 convolution_add_fusion.7
  106.2 0.4 fusion.28
  106.6 0.5 fusion.101
  107.1 0.5 fusion.94
  107.7 4.1 %collective-permute-start.3 = (f32[10,512]{1,0:T(8,128)S(1)}, f32[10,512]{1,0:T(8,128)S(1)}, u32[]{:S(2)}, u32[]{:S(2)}) collective-permute-start(f32[10,512]{1,0:T(8,128)S(1)} %get-tuple-element.5), channel_id=1, source_target_pairs={{1,0},{2,1},{3,2},{4,3},{5,4},{6,5},{7,6},{8,7},{9,8},{10,9},{11,1... | collective-permute-start | bytes 61448 | tf_op jit(solution)/shard_map/ppermute | solution.py:107
  111.8 1.9 %collective-permute-start.2 = (f32[10,512]{1,0:T(8,128)S(1)}, f32[10,512]{1,0:T(8,128)S(1)}, u32[]{:S(2)}, u32[]{:S(2)}) collective-permute-start(f32[10,512]{1,0:T(8,128)S(1)} %get-tuple-element.4), channel_id=1, source_target_pairs={{0,1},{1,2},{2,3},{3,4},{4,5},{5,6},{6,7},{7,8},{8,9},{9,10},{10,1... | collective-permute-start | bytes 61448 | tf_op jit(solution)/shard_map/ppermute | solution.py:106
  113.7 0.8 fusion.24
  114.5 0.4 fusion.109
  115.0 0.3 convolution_add_fusion
  115.3 0.3 convolution_add_fusion.1
  115.6 4.1 %collective-permute-done.2 = f32[10,512]{1,0:T(8,128)S(1)} collective-permute-done((f32[10,512]{1,0:T(8,128)S(1)}, f32[10,512]{1,0:T(8,128)S(1)}, u32[]{:S(2)}, u32[]{:S(2)}) %collective-permute-start.2) | collective-permute-done | bytes 20512 | tf_op jit(solution)/shard_map/ppermute | solution.py:106
  119.7 0.3 fusion.112
  120.0 0.3 convolution_add_fusion.2
  120.4 1.4 %fusion.29 = f32[512,512]{1,0:T(8,128)} fusion(f32[512,512]{1,0:T(8,128)S(1)} %fusion.24, f32[512,512]{1,0:T(8,128)S(1)} %convolution_add_fusion.1, f32[512,512]{1,0:T(8,128)S(1)} %convolution_add_fusion.2, bf16[512,10]{1,0:T(8,128)(2,1)S(1)} %get-tuple-element.2, f32[10,512]{1,0:T(8,128)S(1)} %collective-permute-done.2), kind=kOutput, calls=%fused_computation.47 | convolution fusion | flops 6039552 | bytes 4225024 | tf_op jit(solution)/shard_map/dot_general | solution.py:84
  (13 shorter events, 0.1 us)
Async XLA Ops:
  0.6 2.3 %copy-start = (bf16[1,8,256,256]{3,2,1,0:T(8,128)(2,1)S(1)}, bf16[1,8,256,256]{3,2,1,0:T(8,128)(2,1)}, u32[]{:S(2)}) copy-start(bf16[1,8,256,256]{3,2,1,0:T(8,128)(2,1)} %param.6) | copy-start | bytes 3145732
  11.5 10.9 %copy-start.2 = (s32[2,1,32]{2,1,0:T(1,128)S(1)}, s32[2,1,32]{2,1,0:T(1,128)}, u32[]{:S(2)}) copy-start(s32[2,1,32]{2,1,0:T(1,128)} %param.10) | copy-start | bytes 772
  11.5 73.7 %all-to-all-start = ((bf16[16,2,272,256]{3,2,1,0:T(8,128)(2,1)}), bf16[16,2,272,256]{3,2,1,0:T(8,128)(2,1)}, u32[]{:S(2)}, u32[]{:S(2)}) async-start(bf16[16,2,272,256]{3,2,1,0:T(8,128)(2,1)} %bitcast.161), calls=%async_computation | async-start | bytes 8912896 | tf_op jit(solution)/shard_map/all_to_all | solution.py:139
  97.1 5.8 %copy-start.1 = (f32[512,512]{1,0:T(8,128)}, f32[512,512]{1,0:T(8,128)S(1)}, u32[]{:S(2)}) copy-start(f32[512,512]{1,0:T(8,128)S(1)} %fusion.27) | copy-start | bytes 3145732
  98.4 5.1 %collective-permute-start.1 = (f32[10,512]{1,0:T(8,128)S(1)}, f32[10,512]{1,0:T(8,128)S(1)}, u32[]{:S(2)}, u32[]{:S(2)}) collective-permute-start(f32[10,512]{1,0:T(8,128)S(1)} %get-tuple-element.7), channel_id=1, source_target_pairs={{16,0},{32,16},{48,32},{64,48},{80,64},{96,80},{112,96},{17,1},{33... | collective-permute-start | bytes 61448 | tf_op jit(solution)/shard_map/ppermute | solution.py:103
  100.3 5.2 %collective-permute-start = (f32[10,512]{1,0:T(8,128)S(1)}, f32[10,512]{1,0:T(8,128)S(1)}, u32[]{:S(2)}, u32[]{:S(2)}) collective-permute-start(f32[10,512]{1,0:T(8,128)S(1)} %get-tuple-element.6), channel_id=1, source_target_pairs={{0,16},{16,32},{32,48},{48,64},{64,80},{80,96},{96,112},{1,17},{17... | collective-permute-start | bytes 61448 | tf_op jit(solution)/shard_map/ppermute | solution.py:102
  107.7 6.9 %collective-permute-start.3 = (f32[10,512]{1,0:T(8,128)S(1)}, f32[10,512]{1,0:T(8,128)S(1)}, u32[]{:S(2)}, u32[]{:S(2)}) collective-permute-start(f32[10,512]{1,0:T(8,128)S(1)} %get-tuple-element.5), channel_id=1, source_target_pairs={{1,0},{2,1},{3,2},{4,3},{5,4},{6,5},{7,6},{8,7},{9,8},{10,9},{11,1... | collective-permute-start | bytes 61448 | tf_op jit(solution)/shard_map/ppermute | solution.py:107
  111.8 7.9 %collective-permute-start.2 = (f32[10,512]{1,0:T(8,128)S(1)}, f32[10,512]{1,0:T(8,128)S(1)}, u32[]{:S(2)}, u32[]{:S(2)}) collective-permute-start(f32[10,512]{1,0:T(8,128)S(1)} %get-tuple-element.4), channel_id=1, source_target_pairs={{0,1},{1,2},{2,3},{3,4},{4,5},{5,6},{6,7},{7,8},{8,9},{9,10},{10,1... | collective-permute-start | bytes 61448 | tf_op jit(solution)/shard_map/ppermute | solution.py:106

commit v3 on v2

--- a/solution.py
+++ b/solution.py
@@ -30,13 +30,14 @@
 
 def detect_band(out_size, in_size):
     taps = jnp.arange(-REACH, REACH + 1).astype(jnp.float32)
-    kernel = jnp.exp(-taps * taps / (2.0 * detect_width * detect_width))
-    kernel = kernel / jnp.sum(kernel)
+    scale = 2.0 * detect_width * detect_width
+    total = jnp.sum(jnp.exp(-taps * taps / scale))
     rows = jnp.arange(out_size, dtype=jnp.int32)[:, None]
     cols = jnp.arange(in_size, dtype=jnp.int32)[None, :]
     gap = cols - rows
     inside = (gap >= 0) & (gap <= 2 * REACH)
-    return jnp.where(inside, kernel[jnp.clip(gap, 0, 2 * REACH)], 0.0)
+    tap = (gap - REACH).astype(jnp.float32)
+    return jnp.where(inside, jnp.exp(-tap * tap / scale) / total, 0.0)
 
 
 def match_all(tiles, coeffs, basis):
@@ -47,7 +48,7 @@
     return jnp.sum(coeffs.astype(jnp.float32) * horiz, axis=1).astype(jnp.bfloat16)
 
 
-def coadd_patch(matched, slot_weight, offsets, patch):
+def coadd_parts(matched, slot_weight, offsets, patch):
     slot_count = matched.shape[0]
     size = matched.shape[1]
     local = jnp.arange(size, dtype=jnp.int32)
@@ -60,13 +61,25 @@
     ).astype(jnp.bfloat16)
     zero_weight = jnp.zeros((), jnp.bfloat16)
     row_place = jnp.where(row_hit, slot_weight[None, :, None], zero_weight)
-    numer = jnp.dot(
+    row_cover = jnp.where(jnp.any(row_hit, axis=2), slot_weight[None, :], zero_weight)
+    col_cover = jnp.any(col_hit, axis=1).astype(jnp.bfloat16)
+    return (
         row_place.reshape(patch, slot_count * size),
         shifted.reshape(slot_count * size, patch),
-        preferred_element_type=jnp.float32,
+        row_cover,
+        col_cover,
     )
-    row_cover = jnp.where(jnp.any(row_hit, axis=2), slot_weight[None, :], zero_weight)
-    col_cover = jnp.any(col_hit, axis=1).astype(jnp.bfloat16)
+
+
+def coadd_block(parts, rows=None, cols=None):
+    row_place, shifted, row_cover, col_cover = parts
+    if rows is not None:
+        row_place = row_place[rows]
+        row_cover = row_cover[rows]
+    if cols is not None:
+        shifted = shifted[:, cols]
+        col_cover = col_cover[:, cols]
+    numer = jnp.dot(row_place, shifted, preferred_element_type=jnp.float32)
     cover = jnp.dot(row_cover, col_cover, preferred_element_type=jnp.float32)
     return numer / (1.0 + cover)
 
@@ -86,11 +99,10 @@
     return one(ah, bh) + (one(al, bh) + one(ah, bl))
 
 
-def detect(coadd):
+def detect(parts, patch):
     ny = lax.axis_size("skyy")
     nx = lax.axis_size("skyx")
     r = REACH
-    patch = coadd.shape[0]
     band = detect_band(patch, patch + 2 * r)
     g_head = split(band[:, :r])
     g_mid = split(band[:, r:patch + r])
@@ -99,16 +111,26 @@
     up = [(i + 1, i) for i in range(ny - 1)]
     right = [(j, j + 1) for j in range(nx - 1)]
     left = [(j + 1, j) for j in range(nx - 1)]
-    top = lax.ppermute(coadd[-r:, :], "skyy", down)
-    bottom = lax.ppermute(coadd[:r, :], "skyy", up)
-    vert = mm3(g_mid, split(coadd))
-    vert = vert + (mm3(g_head, split(top)) + mm3(g_tail, split(bottom)))
-    west = lax.ppermute(vert[:, -r:].T, "skyx", right)
-    east = lax.ppermute(vert[:, :r].T, "skyx", left)
+    top = lax.ppermute(coadd_block(parts, rows=slice(patch - r, patch)), "skyy", down)
+    bottom = lax.ppermute(coadd_block(parts, rows=slice(0, r)), "skyy", up)
     on_cols = (((1,), (1,)), ((), ()))
     by_rows = (((0,), (1,)), ((), ()))
+
+    def vertical(own, above, below):
+        inner = mm3(g_mid, split(own))
+        return inner + (mm3(g_head, split(above)) + mm3(g_tail, split(below)))
+
+    first = vertical(coadd_block(parts, cols=slice(0, r)), top[:, :r], bottom[:, :r])
+    last = vertical(
+        coadd_block(parts, cols=slice(patch - r, patch)), top[:, patch - r:], bottom[:, patch - r:]
+    )
+    west = lax.ppermute(last.T, "skyx", right)
+    east = lax.ppermute(first.T, "skyx", left)
+    coadd = coadd_block(parts)
+    vert = vertical(coadd, top, bottom)
     result = mm3(split(vert), g_mid, on_cols)
-    return result + (mm3(split(west), g_head, by_rows) + mm3(split(east), g_tail, by_rows))
+    result = result + (mm3(split(west), g_head, by_rows) + mm3(split(east), g_tail, by_rows))
+    return coadd, result
 
 
 def body(tiles, coeffs, weights, tile_slot, slot_offset):
@@ -140,8 +162,8 @@
     recv = recv.reshape(slots, size + extra, size)
     matched = recv[:, :size, :]
     recv_weight = recv[:, size, 0]
-    coadd = coadd_patch(matched, recv_weight, offsets, patch)
-    detection = detect(coadd)
+    parts = coadd_parts(matched, recv_weight, offsets, patch)
+    coadd, detection = detect(parts, patch)
     return (coadd, detection)
 
 

time: 122 us -> 144 us (1.18)
  the two profiles are of different devices: /device:TPU:36 before, /device:TPU:37 now
where the time goes in v3:
time: 144 us
  waiting for transfers between devices  64 us (44%)
  matrix products  38.3 us (27%)
  starting transfers between devices  19.8 us (14%)
  other arithmetic  16.1 us (11%)
  local copies, waits for them, and re-layouts  4.43 us (3%)
    all_to_all x1, waiting for transfers between devices, body(): recv = lax.all_to_all(send, 'skyx', split_axis=0, concat_axis=0, tiled=True)  56.7 us
    dot_general x36, matrix products, one(): return lax.dot_general(x, y, dims, preferred_element_type=jnp.float32)  12.5 us
    dot_general x5, matrix products, coadd_block(): numer = jnp.dot(row_place, shifted, preferred_element_type=jnp.float32)  12.1 us
    all_to_all x1, starting transfers between devices, body(): recv = lax.all_to_all(send, 'skyx', split_axis=0, concat_axis=0, tiled=True)  7.64 us
    dot_general x1, matrix products, match_all(): jnp.einsum('mbik,bjk->mbij', vert, basis, preferred_element_type=jnp.floa...  6.36 us
    dot_general x1, matrix products, coadd_parts(): jnp.einsum('sij,sjq->siq', matched, col_place, preferred_element_type=jnp...  5.94 us
    ppermute x1, waiting for transfers between devices, detect(): west = lax.ppermute(last.T, 'skyx', right)  4.88 us
    ppermute x1, starting transfers between devices, detect(): lax.ppermute(coadd_block(parts, rows=slice(patch - r, patch)), 'skyy', down)  4.49 us
  transfers between devices with their start and end apart: 5, of which 3 were waited for; matrix products, arithmetic and copies ran while one was open for 9% of the time, Pallas kernels for 0%

profile of v3, /device:TPU:37, one launch (start us, length us, event | category | flops | bytes accessed | tf_op | source)
XLA Modules:
  0.0 143.6 jit_solution(1572136514736036740)
XLA Ops:
  0.6 0.8 select_reduce_fusion
  1.5 0.7 fusion.107
  2.2 0.7 broadcast_select_fusion.1
  3.0 6.4 %fusion.9 = bf16[8,256,256]{2,1,0:T(8,128)(2,1)} fusion(bf16[1,8,5,256,256]{4,3,2,1,0:T(8,128)(2,1)} %param.7, bf16[5,256,256,1]{2,1,3,0:T(8,128)(2,1)} %constant.41, bf16[1,8,256,256]{3,2,1,0:T(8,128)(2,1)S(1)} %copy-done), kind=kOutput, calls=%fused_computation.12 | convolution fusion | flops 2694316032 | bytes 7995392 | tf_op jit(solution)/shard_map/mbik,bjk->mbij/dot_general | solution.py:47
  9.4 1.3 fusion.44
  10.7 2.9 %gather_fusion = bf16[32,272,256]{2,1,0:T(8,128)(2,1)} fusion(bf16[9,272,256]{2,1,0:T(8,128)(2,1)S(1)} %fusion.44, s32[1024]{0:T(1024)S(1)} %pad_clamp_fusion), kind=kCustom, calls=%fused_computation | custom fusion | bytes 8913024 | tf_op jit(solution)/shard_map/gather | solution.py:160
  13.7 7.6 %all-to-all-start = ((bf16[16,2,272,256]{3,2,1,0:T(8,128)(2,1)}), bf16[16,2,272,256]{3,2,1,0:T(8,128)(2,1)}, u32[]{:S(2)}, u32[]{:S(2)}) async-start(bf16[16,2,272,256]{3,2,1,0:T(8,128)(2,1)} %bitcast.90), calls=%async_computation | async-start | bytes 8912896 | tf_op jit(solution)/shard_map/all_to_all | solution.py:161
  21.5 0.6 fusion.110
  22.1 0.8 fusion.40
  23.0 0.8 fusion.64
  23.8 0.3 fusion.56
  24.2 2.3 %fusion.2 = pred[512,32]{0,1:T(8,128)(4,1)S(1)} fusion(s32[32,256]{1,0:T(8,128)S(1)} %get-tuple-element.11), kind=kLoop, calls=%fused_computation.6 | loop fusion | flops 8372224 | bytes 49152 | tf_op jit(solution)/shard_map/reduce_or | solution.py:64
  26.4 3.1 %fusion = pred[32,512]{1,0:T(8,128)(4,1)S(1)} fusion(s32[32,256]{1,0:T(8,128)S(1)} %get-tuple-element.10), kind=kLoop, calls=%fused_computation.3 | loop fusion | flops 8372224 | bytes 49152 | tf_op jit(solution)/shard_map/reduce_or | solution.py:65
  29.5 56.7 %all-to-all-done = bf16[16,2,272,256]{3,2,1,0:T(8,128)(2,1)} async-done(((bf16[16,2,272,256]{3,2,1,0:T(8,128)(2,1)}), bf16[16,2,272,256]{3,2,1,0:T(8,128)(2,1)}, u32[]{:S(2)}, u32[]{:S(2)}) %all-to-all-start) | async-done | bytes 4456480 | tf_op jit(solution)/shard_map/all_to_all | solution.py:161
  86.3 1.2 slice_reduce_fusion
  87.5 5.9 %fusion.13 = bf16[32,256,512]{2,1,0:T(8,128)(2,1)S(1)} fusion(s32[32,256]{1,0:T(8,128)S(1)} %get-tuple-element.10, bf16[32,272,256]{2,1,0:T(8,128)(2,1)} %bitcast.13), kind=kOutput, calls=%fused_computation.16 | convolution fusion | flops 2155872256 | bytes 12615680 | tf_op jit(solution)/shard_map/sij,sjq->siq/dot_general | solution.py:59
  93.5 2.3 %fusion.5 = f32[512,10]{0,1:T(8,128)S(1)} fusion(s32[8192]{0:T(1024)S(1)} %add.229, bf16[8192]{0:T(1024)(128)(2,1)S(1)} %bitcast.93, bf16[8192,512]{1,0:T(8,128)(2,1)S(1)} %bitcast.88), kind=kOutput, calls=%fused_computation.9 | convolution fusion | flops 92274688 | bytes 2166784 | tf_op jit(solution)/shard_map/dot_general | solution.py:82
  95.8 2.8 %fusion.7 = f32[512,10]{0,1:T(8,128)S(1)} fusion(s32[8192]{0:T(1024)S(1)} %add.229, bf16[8192]{0:T(1024)(128)(2,1)S(1)} %bitcast.94, bf16[8192,512]{1,0:T(8,128)(2,1)S(1)} %bitcast.89), kind=kOutput, calls=%fused_computation.10 | convolution fusion | flops 92274688 | bytes 2166784 | tf_op jit(solution)/shard_map/dot_general | solution.py:82
  98.5 0.7 broadcast_select_fusion
  100.2 0.9 fusion.93
  101.1 0.9 fusion.94
  101.9 4.5 %convolution_bitcast_fusion = f32[512,512]{1,0:T(8,128)S(1)} fusion(bf16[32,256,512]{2,1,0:T(8,128)(2,1)S(1)} %fusion.13, s32[32,256]{1,0:T(8,128)S(1)} %get-tuple-element.11, bf16[32]{0:T(256)(128)(2,1)S(1)} %slice_reduce_fusion), kind=kOutput, calls=%fused_computation.56 | convolution fusion | flops 4303355904 | bytes 9470016 | tf_op jit(solution)/shard_map/dot_general | solution.py:82
  106.5 0.4 fusion.34
  106.9 0.4 fusion.68
  107.3 0.5 fusion.69
  107.8 3.7 %fusion.3 = bf16[512,32,256]{2,0,1:T(8,128)(2,1)S(1)} fusion(s32[32,256]{1,0:T(8,128)S(1)} %get-tuple-element.11, bf16[32]{0:T(256)(128)(2,1)S(1)} %slice_reduce_fusion), kind=kLoop, calls=%fused_computation.7 | loop fusion | flops 8388608 | bytes 8421440 | tf_op jit(solution)/shard_map/jit(_where)/select_n | solution.py:63
  111.5 1.4 convolution_bitcast_fusion.2
  112.9 1.2 convolution_bitcast_fusion.1
  114.5 4.5 %collective-permute-start = (f32[10,512]{1,0:T(8,128)S(1)}, f32[10,512]{1,0:T(8,128)S(1)}, u32[]{:S(2)}, u32[]{:S(2)}) collective-permute-start(f32[10,512]{1,0:T(8,128)S(1)} %fusion.53), channel_id=1, source_target_pairs={{0,16},{16,32},{32,48},{48,64},{64,80},{80,96},{96,112},{1,17},{17... | collective-permute-start | bytes 61448 | tf_op jit(solution)/shard_map/ppermute | solution.py:114
  119.0 1.9 %collective-permute-start.1 = (f32[10,512]{1,0:T(8,128)S(1)}, f32[10,512]{1,0:T(8,128)S(1)}, u32[]{:S(2)}, u32[]{:S(2)}) collective-permute-start(f32[10,512]{1,0:T(8,128)S(1)} %fusion.52), channel_id=1, source_target_pairs={{16,0},{32,16},{48,32},{64,48},{80,64},{96,80},{112,96},{17,1},{33... | collective-permute-start | bytes 61448 | tf_op jit(solution)/shard_map/ppermute | solution.py:115
  121.2 0.5 fusion.33
  121.9 2.3 %collective-permute-done.1 = f32[10,512]{1,0:T(8,128)S(1)} collective-permute-done((f32[10,512]{1,0:T(8,128)S(1)}, f32[10,512]{1,0:T(8,128)S(1)}, u32[]{:S(2)}, u32[]{:S(2)}) %collective-permute-start.1) | collective-permute-done | bytes 20512 | tf_op jit(solution)/shard_map/ppermute | solution.py:115
  124.3 0.3 fusion.81
  124.5 0.3 convolution_add_fusion.5
  125.1 0.3 fusion.83
  125.6 0.3 fusion.35
  125.9 0.5 fusion.61
  126.4 0.5 fusion.70
  127.9 3.9 %collective-permute-start.3 = (f32[10,512]{1,0:T(8,128)S(1)}, f32[10,512]{1,0:T(8,128)S(1)}, u32[]{:S(2)}, u32[]{:S(2)}) collective-permute-start(f32[10,512]{1,0:T(8,128)S(1)} %fusion.47), channel_id=1, source_target_pairs={{1,0},{2,1},{3,2},{4,3},{5,4},{6,5},{7,6},{8,7},{9,8},{10,9},{11,1... | collective-permute-start | bytes 61448 | tf_op jit(solution)/shard_map/ppermute | solution.py:128
  133.2 1.9 %collective-permute-start.2 = (f32[10,512]{1,0:T(8,128)S(1)}, f32[10,512]{1,0:T(8,128)S(1)}, u32[]{:S(2)}, u32[]{:S(2)}) collective-permute-start(f32[10,512]{1,0:T(8,128)S(1)} %fusion.50), channel_id=1, source_target_pairs={{0,1},{1,2},{2,3},{3,4},{4,5},{5,6},{6,7},{7,8},{8,9},{9,10},{10,1... | collective-permute-start | bytes 61448 | tf_op jit(solution)/shard_map/ppermute | solution.py:127
  135.2 0.5 fusion.31
  135.7 4.9 %collective-permute-done.2 = f32[10,512]{1,0:T(8,128)S(1)} collective-permute-done((f32[10,512]{1,0:T(8,128)S(1)}, f32[10,512]{1,0:T(8,128)S(1)}, u32[]{:S(2)}, u32[]{:S(2)}) %collective-permute-start.2) | collective-permute-done | bytes 20512 | tf_op jit(solution)/shard_map/ppermute | solution.py:127
  140.5 0.3 fusion.95
  140.9 0.3 convolution_add_fusion.2
  141.2 0.3 fusion.98
  141.6 0.3 convolution_add_fusion
  141.9 0.3 convolution_add_fusion.1
  142.3 1.3 fusion.36
  (50 shorter events, 5.3 us)
Async XLA Ops:
  0.6 2.3 %copy-start = (bf16[1,8,256,256]{3,2,1,0:T(8,128)(2,1)S(1)}, bf16[1,8,256,256]{3,2,1,0:T(8,128)(2,1)}, u32[]{:S(2)}) copy-start(bf16[1,8,256,256]{3,2,1,0:T(8,128)(2,1)} %param.6) | copy-start | bytes 3145732
  13.7 7.7 %copy-start.6 = (s32[2,1,32]{2,1,0:T(1,128)S(1)}, s32[2,1,32]{2,1,0:T(1,128)}, u32[]{:S(2)}) copy-start(s32[2,1,32]{2,1,0:T(1,128)} %param.10) | copy-start | bytes 772
  13.7 72.6 %all-to-all-start = ((bf16[16,2,272,256]{3,2,1,0:T(8,128)(2,1)}), bf16[16,2,272,256]{3,2,1,0:T(8,128)(2,1)}, u32[]{:S(2)}, u32[]{:S(2)}) async-start(bf16[16,2,272,256]{3,2,1,0:T(8,128)(2,1)} %bitcast.90), calls=%async_computation | async-start | bytes 8912896 | tf_op jit(solution)/shard_map/all_to_all | solution.py:161
  106.9 14.3 %copy-start.1 = (f32[512,512]{1,0:T(8,128)}, f32[512,512]{1,0:T(8,128)S(1)}, u32[]{:S(2)}) copy-start(f32[512,512]{1,0:T(8,128)S(1)} %fusion.34) | copy-start | bytes 3145732
  112.9 1.2 copy-start.5
  114.1 7.6 %copy-start.3 = (f32[10,512]{1,0:T(8,128)S(1)}, f32[10,512]{1,0:T(8,128)}, u32[]{:S(2)}) copy-start(f32[10,512]{1,0:T(8,128)} %fusion.93) | copy-start | bytes 61444
  114.1 7.6 %copy-start.4 = (f32[10,512]{1,0:T(8,128)S(1)}, f32[10,512]{1,0:T(8,128)}, u32[]{:S(2)}) copy-start(f32[10,512]{1,0:T(8,128)} %fusion.94) | copy-start | bytes 61444
  114.5 10.6 %collective-permute-start = (f32[10,512]{1,0:T(8,128)S(1)}, f32[10,512]{1,0:T(8,128)S(1)}, u32[]{:S(2)}, u32[]{:S(2)}) collective-permute-start(f32[10,512]{1,0:T(8,128)S(1)} %fusion.53), channel_id=1, source_target_pairs={{0,16},{16,32},{32,48},{48,64},{64,80},{80,96},{96,112},{1,17},{17... | collective-permute-start | bytes 61448 | tf_op jit(solution)/shard_map/ppermute | solution.py:114
  119.0 5.2 %collective-permute-start.1 = (f32[10,512]{1,0:T(8,128)S(1)}, f32[10,512]{1,0:T(8,128)S(1)}, u32[]{:S(2)}, u32[]{:S(2)}) collective-permute-start(f32[10,512]{1,0:T(8,128)S(1)} %fusion.52), channel_id=1, source_target_pairs={{16,0},{32,16},{48,32},{64,48},{80,64},{96,80},{112,96},{17,1},{33... | collective-permute-start | bytes 61448 | tf_op jit(solution)/shard_map/ppermute | solution.py:115
  121.2 4.2 %copy-start.2 = (bf16[512,10]{1,0:T(8,128)(2,1)S(1)}, bf16[512,10]{1,0:T(8,128)(2,1)}, u32[]{:S(2)}) copy-start(bf16[512,10]{1,0:T(8,128)(2,1)} %get-tuple-element.2) | copy-start | bytes 30724
  127.9 13.3 %collective-permute-start.3 = (f32[10,512]{1,0:T(8,128)S(1)}, f32[10,512]{1,0:T(8,128)S(1)}, u32[]{:S(2)}, u32[]{:S(2)}) collective-permute-start(f32[10,512]{1,0:T(8,128)S(1)} %fusion.47), channel_id=1, source_target_pairs={{1,0},{2,1},{3,2},{4,3},{5,4},{6,5},{7,6},{8,7},{9,8},{10,9},{11,1... | collective-permute-start | bytes 61448 | tf_op jit(solution)/shard_map/ppermute | solution.py:128
  133.2 7.3 %collective-permute-start.2 = (f32[10,512]{1,0:T(8,128)S(1)}, f32[10,512]{1,0:T(8,128)S(1)}, u32[]{:S(2)}, u32[]{:S(2)}) collective-permute-start(f32[10,512]{1,0:T(8,128)S(1)} %fusion.50), channel_id=1, source_target_pairs={{0,1},{1,2},{2,3},{3,4},{4,5},{5,6},{6,7},{7,8},{8,9},{9,10},{10,1... | collective-permute-start | bytes 61448 | tf_op jit(solution)/shard_map/ppermute | solution.py:127

commit v4 on v2

--- a/solution.py
+++ b/solution.py
@@ -2,6 +2,8 @@
 import jax
 import jax.numpy as jnp
 from jax import lax
+from jax.experimental import pallas as pl
+from jax.experimental.pallas import tpu as pltpu
 from jax.sharding import PartitionSpec as P
 
 NB = 5
@@ -30,21 +32,58 @@
 
 def detect_band(out_size, in_size):
     taps = jnp.arange(-REACH, REACH + 1).astype(jnp.float32)
-    kernel = jnp.exp(-taps * taps / (2.0 * detect_width * detect_width))
-    kernel = kernel / jnp.sum(kernel)
+    scale = 2.0 * detect_width * detect_width
+    total = jnp.sum(jnp.exp(-taps * taps / scale))
     rows = jnp.arange(out_size, dtype=jnp.int32)[:, None]
     cols = jnp.arange(in_size, dtype=jnp.int32)[None, :]
     gap = cols - rows
     inside = (gap >= 0) & (gap <= 2 * REACH)
-    return jnp.where(inside, kernel[jnp.clip(gap, 0, 2 * REACH)], 0.0)
+    tap = (gap - REACH).astype(jnp.float32)
+    return jnp.where(inside, jnp.exp(-tap * tap / scale) / total, 0.0)
 
 
-def match_all(tiles, coeffs, basis):
-    vert = jnp.einsum(
-        "bij,mjk->mbik", basis, tiles, preferred_element_type=jnp.float32
-    ).astype(jnp.bfloat16)
-    horiz = jnp.einsum("mbik,bjk->mbij", vert, basis, preferred_element_type=jnp.float32)
-    return jnp.sum(coeffs.astype(jnp.float32) * horiz, axis=1).astype(jnp.bfloat16)
+def match_kernel(slot_ref, weight_ref, tile_ref, coeff_ref, basis_ref, zero_ref, out_ref):
+    j = pl.program_id(0)
+    size = tile_ref.shape[-1]
+    tile = tile_ref[0, 0]
+    total = jnp.zeros((size, size), jnp.float32)
+    for b in range(NB):
+        band = basis_ref[b]
+        vert = jnp.dot(band, tile, preferred_element_type=jnp.float32).astype(jnp.bfloat16)
+        horiz = lax.dot_general(
+            vert, band, (((1,), (1,)), ((), ())), preferred_element_type=jnp.float32
+        )
+        total = total + coeff_ref[0, 0, b].astype(jnp.float32) * horiz
+    out_ref[0, :size, :] = total.astype(jnp.bfloat16)
+    extra = out_ref.shape[1] - size
+    line = lax.broadcasted_iota(jnp.int32, (extra, size), 0)
+    out_ref[0, size:, :] = jnp.where(line == 0, weight_ref[j], 0.0).astype(jnp.bfloat16)
+
+
+def match_into_slots(tiles, coeffs, weights, own_slot, basis, slots, extra):
+    count = tiles.shape[1]
+    size = tiles.shape[2]
+    zeros = jnp.zeros((slots, size + extra, size), jnp.bfloat16)
+    grid_spec = pltpu.PrefetchScalarGridSpec(
+        num_scalar_prefetch=2,
+        grid=(count,),
+        in_specs=[
+            pl.BlockSpec((1, 1, size, size), lambda j, slot, w: (0, j, 0, 0)),
+            pl.BlockSpec((1, 1, NB, size, size), lambda j, slot, w: (0, j, 0, 0, 0)),
+            pl.BlockSpec((NB, size, size), lambda j, slot, w: (0, 0, 0)),
+            pl.BlockSpec(memory_space=pl.ANY),
+        ],
+        out_specs=pl.BlockSpec((1, size + extra, size), lambda j, slot, w: (slot[j], 0, 0)),
+    )
+    flops = count * NB * 4 * size * size * size
+    moved = count * (NB + 1) * size * size * 2 + count * (size + extra) * size * 2
+    return pl.pallas_call(
+        match_kernel,
+        out_shape=jax.ShapeDtypeStruct((slots, size + extra, size), jnp.bfloat16),
+        grid_spec=grid_spec,
+        input_output_aliases={5: 0},
+        cost_estimate=pl.CostEstimate(flops=flops, bytes_accessed=moved, transcendentals=0),
+    )(own_slot, weights, tiles, coeffs, basis, zeros)
 
 
 def coadd_patch(matched, slot_weight, offsets, patch):
@@ -123,19 +162,10 @@
     own_weight = weights[0]
     own_slot = tile_slot[0]
     offsets = slot_offset[:, 0, :]
-    hits = own_slot[None, :] == jnp.arange(slots, dtype=jnp.int32)[:, None]
-    present = jnp.any(hits, axis=1)
-    which = jnp.sum(jnp.where(hits, jnp.arange(count, dtype=jnp.int32)[None, :], 0), axis=1)
-    which = jnp.where(present, which, count)
-    own_matched = match_all(own_tiles, own_coeffs, basis)
     extra = 16
-    line = jnp.arange(extra, dtype=jnp.int32)[None, :, None] == 0
-    weight_rows = jnp.where(
-        line, own_weight[:, None, None], jnp.zeros((), jnp.bfloat16)
-    ) * jnp.ones((1, 1, size), jnp.bfloat16)
-    carry = jnp.concatenate([own_matched, weight_rows], axis=1)
-    carry = jnp.concatenate([carry, jnp.zeros((1, size + extra, size), jnp.bfloat16)], axis=0)
-    send = carry[which].reshape(columns, CAP, size + extra, size)
+    send = match_into_slots(
+        tiles, coeffs, own_weight.astype(jnp.float32), own_slot, basis, slots, extra
+    ).reshape(columns, CAP, size + extra, size)
     recv = lax.all_to_all(send, "skyx", split_axis=0, concat_axis=0, tiled=True)
     recv = recv.reshape(slots, size + extra, size)
     matched = recv[:, :size, :]

time: 122 us -> 125 us (1.025)
  the two profiles are of different devices: /device:TPU:36 before, /device:TPU:29 now
where the time goes in v4:
time: 125 us; the launch traced here: 124 us
  waiting for transfers between devices  62.4 us (50%)
  starting transfers between devices  19.8 us (16%)
  matrix products  19.5 us (16%)
  Pallas kernels  9.57 us (8%)
  other arithmetic  8.42 us (7%)
  local copies, waits for them, and re-layouts  3.59 us (3%)
    all_to_all x1, waiting for transfers between devices, body(): recv = lax.all_to_all(send, 'skyx', split_axis=0, concat_axis=0, tiled=True)  57.2 us
    pallas_call x1, Pallas kernels, match_into_slots(): pl.pallas_call(match_kernel, out_shape=jax.ShapeDtypeStruct((slots, size...  9.57 us
    dot_general x18, matrix products, one(): return lax.dot_general(x, y, dims, preferred_element_type=jnp.float32)  8.8 us
    all_to_all x1, starting transfers between devices, body(): recv = lax.all_to_all(send, 'skyx', split_axis=0, concat_axis=0, tiled=True)  7.75 us
    dot_general x1, matrix products, coadd_patch(): jnp.einsum('sij,sjq->siq', matched, col_place, preferred_element_type=jnp...  5.76 us
    dot_general x1, matrix products, coadd_patch(): jnp.dot(row_place.reshape(patch, slot_count * size), shifted.reshape(slot...  4.52 us
    ppermute x1, starting transfers between devices, detect(): top = lax.ppermute(coadd[-r:, :], 'skyy', down)  4.5 us
    ppermute x1, waiting for transfers between devices, detect(): east = lax.ppermute(vert[:, :r].T, 'skyx', left)  3.78 us
  transfers between devices with their start and end apart: 5, of which 3 were waited for; matrix products, arithmetic and copies ran while one was open for 8% of the time, Pallas kernels for 0%

profile of v4, /device:TPU:29, one launch (start us, length us, event | category | flops | bytes accessed | tf_op | source)
XLA Modules:
  0.0 124.2 jit_solution(11177829167839649386)
XLA Ops:
  0.6 1.2 bitcast_convert_fusion.weight_ref
  1.8 2.4 %broadcast_in_dim.39.zero_ref = bf16[32,272,256]{2,1,0:T(8,128)(2,1)} broadcast(bf16[]{:T(256)} %constant.9.clone.1), dimensions={} | broadcast | bytes 4456450 | tf_op jit(solution)/shard_map/broadcast_in_dim | solution.py:66
  4.2 9.6 %shard_map.77 = bf16[32,272,256]{2,1,0:T(8,128)(2,1)} custom-call(s32[8]{0:T(128)} %bitcast.33, f32[8]{0:T(128)} %bitcast_convert_fusion.weight_ref, bf16[1,8,256,256]{3,2,1,0:T(8,128)(2,1)} %tile_ref.1, bf16[1,8,5,256,256]{4,3,2,1,0:T(8,128)(2,1)} %coeff_ref.1, bf16[5,256,256]{2,1,0:T(8,128)(2,1)} %constant.24.clone.basis_ref, ...), custom_call_target="tpu_custom_call", output_to_operand_aliasing={{}: (5, {})} | custom-call | flops 2684354560 | bytes 7405568 | tf_op jit(solution)/shard_map/pallas_call | solution.py:80
  13.8 0.0 copy-start.1
  13.8 7.8 %all-to-all-start = ((bf16[16,2,272,256]{3,2,1,0:T(8,128)(2,1)}), bf16[16,2,272,256]{3,2,1,0:T(8,128)(2,1)}, u32[]{:S(2)}, u32[]{:S(2)}) async-start(bf16[16,2,272,256]{3,2,1,0:T(8,128)(2,1)} %bitcast.32), calls=%async_computation | async-start | bytes 8912896 | tf_op jit(solution)/shard_map/all_to_all | solution.py:169
  21.5 0.6 fusion.68
  22.1 0.8 fusion.30
  23.0 0.0 copy-done.1
  23.0 0.1 iota_add_fusion
  23.1 0.1 reduce-precision_convert_fusion.4
  23.2 0.2 reduce-precision_convert_fusion.2
  23.4 2.3 %fusion.2 = pred[512,32]{0,1:T(8,128)(4,1)S(1)} fusion(s32[32,256]{1,0:T(8,128)S(1)} %get-tuple-element.11), kind=kLoop, calls=%fused_computation.4 | loop fusion | flops 8372224 | bytes 49152 | tf_op jit(solution)/shard_map/reduce_or | solution.py:107
  25.7 3.1 %fusion = pred[32,512]{1,0:T(8,128)(4,1)S(1)} fusion(s32[32,256]{1,0:T(8,128)S(1)} %get-tuple-element.10), kind=kLoop, calls=%fused_computation.1 | loop fusion | flops 8372224 | bytes 49152 | tf_op jit(solution)/shard_map/reduce_or | solution.py:108
  28.8 57.2 %all-to-all-done = bf16[16,2,272,256]{3,2,1,0:T(8,128)(2,1)} async-done(((bf16[16,2,272,256]{3,2,1,0:T(8,128)(2,1)}), bf16[16,2,272,256]{3,2,1,0:T(8,128)(2,1)}, u32[]{:S(2)}, u32[]{:S(2)}) %all-to-all-start) | async-done | bytes 4456480 | tf_op jit(solution)/shard_map/all_to_all | solution.py:169
  86.1 5.8 %fusion.95 = bf16[32,256,512]{2,1,0:T(8,128)(2,1)S(1)} fusion(s32[32,256]{1,0:T(8,128)S(1)} %get-tuple-element.10, bf16[32,272,256]{2,1,0:T(8,128)(2,1)} %bitcast.4), kind=kOutput, calls=%fused_computation.7.clone.clone.clone.2 | convolution fusion | flops 2155872256 | bytes 12615680 | tf_op jit(solution)/shard_map/sij,sjq->siq/dot_general | solution.py:97
  91.8 1.2 slice_reduce_fusion
  93.0 4.5 %fusion.20 = f32[512,512]{1,0:T(8,128)S(1)} fusion(s32[32,256]{1,0:T(8,128)S(1)} %get-tuple-element.11, bf16[32]{0:T(256)(128)(2,1)S(1)} %slice_reduce_fusion, bf16[32,256,512]{2,1,0:T(8,128)(2,1)S(1)} %fusion.95), kind=kOutput, calls=%fused_computation.38 | convolution fusion | flops 4303355904 | bytes 9470016 | tf_op jit(solution)/shard_map/dot_general | solution.py:102
  97.5 0.4 fusion.17
  97.9 0.0 copy-start
  97.9 0.8 fusion.42
  98.7 4.5 %collective-permute-start = (f32[10,512]{1,0:T(8,128)S(1)}, f32[10,512]{1,0:T(8,128)S(1)}, u32[]{:S(2)}, u32[]{:S(2)}) collective-permute-start(f32[10,512]{1,0:T(8,128)S(1)} %get-tuple-element.6), channel_id=1, source_target_pairs={{0,16},{16,32},{32,48},{48,64},{64,80},{80,96},{96,112},{1,17},{17... | collective-permute-start | bytes 61448 | tf_op jit(solution)/shard_map/ppermute | solution.py:141
  103.2 2.1 %collective-permute-start.1 = (f32[10,512]{1,0:T(8,128)S(1)}, f32[10,512]{1,0:T(8,128)S(1)}, u32[]{:S(2)}, u32[]{:S(2)}) collective-permute-start(f32[10,512]{1,0:T(8,128)S(1)} %get-tuple-element.7), channel_id=1, source_target_pairs={{16,0},{32,16},{48,32},{64,48},{80,64},{96,80},{112,96},{17,1},{33... | collective-permute-start | bytes 61448 | tf_op jit(solution)/shard_map/ppermute | solution.py:142
  105.3 0.5 fusion.43
  105.8 0.5 fusion.16
  106.3 0.0 copy-done
  106.3 0.0 collective-permute-done
  106.3 0.3 fusion.62
  106.7 0.3 convolution_add_fusion.7
  107.0 1.4 %collective-permute-done.1 = f32[10,512]{1,0:T(8,128)S(1)} collective-permute-done((f32[10,512]{1,0:T(8,128)S(1)}, f32[10,512]{1,0:T(8,128)S(1)}, u32[]{:S(2)}, u32[]{:S(2)}) %collective-permute-start.1) | collective-permute-done | bytes 20512 | tf_op jit(solution)/shard_map/ppermute | solution.py:142
  108.4 0.3 fusion.60
  108.8 0.4 convolution_add_fusion.5
  109.2 0.3 convolution_add_fusion.6
  109.6 0.4 fusion.18
  110.0 0.5 fusion.37
  110.5 0.5 fusion.44
  111.0 3.6 %collective-permute-start.2 = (f32[10,512]{1,0:T(8,128)S(1)}, f32[10,512]{1,0:T(8,128)S(1)}, u32[]{:S(2)}, u32[]{:S(2)}) collective-permute-start(f32[10,512]{1,0:T(8,128)S(1)} %get-tuple-element.4), channel_id=1, source_target_pairs={{0,1},{1,2},{2,3},{3,4},{4,5},{5,6},{6,7},{7,8},{8,9},{9,10},{10,1... | collective-permute-start | bytes 61448 | tf_op jit(solution)/shard_map/ppermute | solution.py:145
  114.6 1.9 %collective-permute-start.3 = (f32[10,512]{1,0:T(8,128)S(1)}, f32[10,512]{1,0:T(8,128)S(1)}, u32[]{:S(2)}, u32[]{:S(2)}) collective-permute-start(f32[10,512]{1,0:T(8,128)S(1)} %get-tuple-element.5), channel_id=1, source_target_pairs={{1,0},{2,1},{3,2},{4,3},{5,4},{6,5},{7,6},{8,7},{9,8},{10,9},{11,1... | collective-permute-start | bytes 61448 | tf_op jit(solution)/shard_map/ppermute | solution.py:146
  116.5 0.8 fusion.14
  117.3 0.0 collective-permute-done.2
  117.3 0.3 fusion.55
  117.6 0.3 convolution_add_fusion.2
  118.0 3.8 %collective-permute-done.3 = f32[10,512]{1,0:T(8,128)S(1)} collective-permute-done((f32[10,512]{1,0:T(8,128)S(1)}, f32[10,512]{1,0:T(8,128)S(1)}, u32[]{:S(2)}, u32[]{:S(2)}) %collective-permute-start.3) | collective-permute-done | bytes 20512 | tf_op jit(solution)/shard_map/ppermute | solution.py:146
  121.8 0.4 fusion.52
  122.2 0.3 convolution_add_fusion
  122.5 0.3 convolution_add_fusion.1
  122.9 1.3 %fusion.19 = f32[512,512]{1,0:T(8,128)} fusion(f32[512,512]{1,0:T(8,128)S(1)} %fusion.14, f32[512,512]{1,0:T(8,128)S(1)} %convolution_add_fusion.1, f32[512,512]{1,0:T(8,128)S(1)} %convolution_add_fusion.2, bf16[512,10]{1,0:T(8,128)(2,1)S(1)} %get-tuple-element.2, f32[10,512]{1,0:T(8,128)S(1)} %collective-permute-done.2), kind=kOutput, calls=%fused_computation.37 | convolution fusion | flops 6039552 | bytes 4225024 | tf_op jit(solution)/shard_map/dot_general | solution.py:123
  (3 shorter events, 0.0 us)
Async XLA Ops:
  13.8 9.2 %copy-start.1 = (s32[2,1,32]{2,1,0:T(1,128)S(1)}, s32[2,1,32]{2,1,0:T(1,128)}, u32[]{:S(2)}) copy-start(s32[2,1,32]{2,1,0:T(1,128)} %param.10) | copy-start | bytes 772
  13.8 72.3 %all-to-all-start = ((bf16[16,2,272,256]{3,2,1,0:T(8,128)(2,1)}), bf16[16,2,272,256]{3,2,1,0:T(8,128)(2,1)}, u32[]{:S(2)}, u32[]{:S(2)}) async-start(bf16[16,2,272,256]{3,2,1,0:T(8,128)(2,1)} %bitcast.32), calls=%async_computation | async-start | bytes 8912896 | tf_op jit(solution)/shard_map/all_to_all | solution.py:169
  97.9 8.4 %copy-start = (f32[512,512]{1,0:T(8,128)}, f32[512,512]{1,0:T(8,128)S(1)}, u32[]{:S(2)}) copy-start(f32[512,512]{1,0:T(8,128)S(1)} %fusion.17) | copy-start | bytes 3145732
  98.7 7.6 %collective-permute-start = (f32[10,512]{1,0:T(8,128)S(1)}, f32[10,512]{1,0:T(8,128)S(1)}, u32[]{:S(2)}, u32[]{:S(2)}) collective-permute-start(f32[10,512]{1,0:T(8,128)S(1)} %get-tuple-element.6), channel_id=1, source_target_pairs={{0,16},{16,32},{32,48},{48,64},{64,80},{80,96},{96,112},{1,17},{17... | collective-permute-start | bytes 61448 | tf_op jit(solution)/shard_map/ppermute | solution.py:141
  103.2 5.2 %collective-permute-start.1 = (f32[10,512]{1,0:T(8,128)S(1)}, f32[10,512]{1,0:T(8,128)S(1)}, u32[]{:S(2)}, u32[]{:S(2)}) collective-permute-start(f32[10,512]{1,0:T(8,128)S(1)} %get-tuple-element.7), channel_id=1, source_target_pairs={{16,0},{32,16},{48,32},{64,48},{80,64},{96,80},{112,96},{17,1},{33... | collective-permute-start | bytes 61448 | tf_op jit(solution)/shard_map/ppermute | solution.py:142
  111.0 6.3 %collective-permute-start.2 = (f32[10,512]{1,0:T(8,128)S(1)}, f32[10,512]{1,0:T(8,128)S(1)}, u32[]{:S(2)}, u32[]{:S(2)}) collective-permute-start(f32[10,512]{1,0:T(8,128)S(1)} %get-tuple-element.4), channel_id=1, source_target_pairs={{0,1},{1,2},{2,3},{3,4},{4,5},{5,6},{6,7},{7,8},{8,9},{9,10},{10,1... | collective-permute-start | bytes 61448 | tf_op jit(solution)/shard_map/ppermute | solution.py:145
  114.6 7.2 %collective-permute-start.3 = (f32[10,512]{1,0:T(8,128)S(1)}, f32[10,512]{1,0:T(8,128)S(1)}, u32[]{:S(2)}, u32[]{:S(2)}) collective-permute-start(f32[10,512]{1,0:T(8,128)S(1)} %get-tuple-element.5), channel_id=1, source_target_pairs={{1,0},{2,1},{3,2},{4,3},{5,4},{6,5},{7,6},{8,7},{9,8},{10,9},{11,1... | collective-permute-start | bytes 61448 | tf_op jit(solution)/shard_map/ppermute | solution.py:146

commit v5 on v2

--- a/solution.py
+++ b/solution.py
@@ -30,13 +30,14 @@
 
 def detect_band(out_size, in_size):
     taps = jnp.arange(-REACH, REACH + 1).astype(jnp.float32)
-    kernel = jnp.exp(-taps * taps / (2.0 * detect_width * detect_width))
-    kernel = kernel / jnp.sum(kernel)
+    scale = 2.0 * detect_width * detect_width
+    total = jnp.sum(jnp.exp(-taps * taps / scale))
     rows = jnp.arange(out_size, dtype=jnp.int32)[:, None]
     cols = jnp.arange(in_size, dtype=jnp.int32)[None, :]
     gap = cols - rows
     inside = (gap >= 0) & (gap <= 2 * REACH)
-    return jnp.where(inside, kernel[jnp.clip(gap, 0, 2 * REACH)], 0.0)
+    tap = (gap - REACH).astype(jnp.float32)
+    return jnp.where(inside, jnp.exp(-tap * tap / scale) / total, 0.0)
 
 
 def match_all(tiles, coeffs, basis):
@@ -91,24 +92,19 @@
     nx = lax.axis_size("skyx")
     r = REACH
     patch = coadd.shape[0]
-    band = detect_band(patch, patch + 2 * r)
-    g_head = split(band[:, :r])
-    g_mid = split(band[:, r:patch + r])
-    g_tail = split(band[:, patch + r:])
+    band = split(detect_band(patch, patch + 2 * r))
     down = [(i, i + 1) for i in range(ny - 1)]
     up = [(i + 1, i) for i in range(ny - 1)]
     right = [(j, j + 1) for j in range(nx - 1)]
     left = [(j + 1, j) for j in range(nx - 1)]
     top = lax.ppermute(coadd[-r:, :], "skyy", down)
     bottom = lax.ppermute(coadd[:r, :], "skyy", up)
-    vert = mm3(g_mid, split(coadd))
-    vert = vert + (mm3(g_head, split(top)) + mm3(g_tail, split(bottom)))
+    rows = jnp.concatenate([top, coadd, bottom], axis=0)
+    vert = mm3(band, split(rows))
     west = lax.ppermute(vert[:, -r:].T, "skyx", right)
     east = lax.ppermute(vert[:, :r].T, "skyx", left)
-    on_cols = (((1,), (1,)), ((), ()))
-    by_rows = (((0,), (1,)), ((), ()))
-    result = mm3(split(vert), g_mid, on_cols)
-    return result + (mm3(split(west), g_head, by_rows) + mm3(split(east), g_tail, by_rows))
+    cols = jnp.concatenate([west.T, vert, east.T], axis=1)
+    return mm3(split(cols), band, (((1,), (1,)), ((), ())))
 
 
 def body(tiles, coeffs, weights, tile_slot, slot_offset):

time: 122 us -> 126 us (1.033)
  waiting for transfers between devices: 48.6 us -> 68 us
  other arithmetic: 22.9 us -> 8.55 us
  local copies, waits for them, and re-layouts: 5.6 us -> 4.21 us
    all_to_all x1, waiting for transfers between devices: 43.6 us -> 60.1 us  [body(): recv = lax.all_to_all(send, 'skyx', split_axis=0, concat_axis=0, tiled=True)]
    select_n x1 -> x0, other arithmetic: 13.4 us -> none  [detect_band(): return jnp.where(inside, kernel[jnp.clip(gap, 0, 2 * REACH)], 0.0)]
    ppermute x1, waiting for transfers between devices: 4.07 us -> 5.98 us  [detect(): west = lax.ppermute(vert[:, -r:].T, 'skyx', right)]
    gather x2 -> x0, local copies, waits for them, and re-layouts: 1.39 us -> none  [detect_band(): return jnp.where(inside, kernel[jnp.clip(gap, 0, 2 * REACH)], 0.0)]
    dot_general x18 -> x6, matrix products: 8.85 us -> 9.19 us  [one(): return lax.dot_general(x, y, dims, preferred_element_type=jnp.float32)]
  transfers between devices with their start and end apart: 5 -> 5, of which waited for: 3 -> 3; matrix products, arithmetic and copies ran while one was open for 21% -> 5% of each run, Pallas kernels for 0% -> 0%
where the time goes in v5:
time: 126 us
  waiting for transfers between devices  68 us (54%)
  matrix products  25.3 us (20%)
  starting transfers between devices  18.7 us (15%)
  other arithmetic  8.55 us (7%)
  local copies, waits for them, and re-layouts  4.21 us (3%)
    all_to_all x1, waiting for transfers between devices, body(): recv = lax.all_to_all(send, 'skyx', split_axis=0, concat_axis=0, tiled=True)  60.1 us
    dot_general x6, matrix products, one(): return lax.dot_general(x, y, dims, preferred_element_type=jnp.float32)  9.19 us
    all_to_all x1, starting transfers between devices, body(): recv = lax.all_to_all(send, 'skyx', split_axis=0, concat_axis=0, tiled=True)  8.2 us
    ppermute x1, waiting for transfers between devices, detect(): west = lax.ppermute(vert[:, -r:].T, 'skyx', right)  5.98 us
    dot_general x1, matrix products, coadd_patch(): jnp.einsum('sij,sjq->siq', matched, col_place, preferred_element_type=jnp...  5.76 us
    dot_general x1, matrix products, match_all(): jnp.einsum('mbik,bjk->mbij', vert, basis, preferred_element_type=jnp.floa...  5.39 us
    dot_general x1, matrix products, coadd_patch(): jnp.dot(row_place.reshape(patch, slot_count * size), shifted.reshape(slot...  4.52 us
    ppermute x1, starting transfers between devices, detect(): east = lax.ppermute(vert[:, :r].T, 'skyx', left)  4.12 us
  transfers between devices with their start and end apart: 5, of which 3 were waited for; matrix products, arithmetic and copies ran while one was open for 5% of the time, Pallas kernels for 0%

profile of v5, /device:TPU:36, one launch (start us, length us, event | category | flops | bytes accessed | tf_op | source)
XLA Modules:
  0.0 125.6 jit_solution(13704366829003329642)
XLA Ops:
  0.6 0.0 copy-start
  0.7 0.8 fusion.53
  1.5 0.7 select_reduce_fusion
  2.2 0.7 broadcast_select_fusion
  3.0 0.0 copy-done
  3.0 5.4 %fusion.4 = bf16[8,256,256]{2,1,0:T(8,128)(2,1)S(1)} fusion(bf16[1,8,5,256,256]{4,3,2,1,0:T(8,128)(2,1)} %param.7, bf16[5,256,256,1]{2,1,3,0:T(8,128)(2,1)} %constant.39, bf16[1,8,256,256]{3,2,1,0:T(8,128)(2,1)S(1)} %copy-done), kind=kOutput, calls=%fused_computation.8 | convolution fusion | flops 2694316032 | bytes 7995392 | tf_op jit(solution)/shard_map/mbik,bjk->mbij/dot_general | solution.py:47
  8.4 0.1 mul.15
  8.5 0.1 fusion.39
  8.5 2.9 %gather_fusion = bf16[32,272,256]{2,1,0:T(8,128)(2,1)} fusion(bf16[9,272,256]{2,1,0:T(8,128)(2,1)S(1)} %fusion.39, s32[1024]{0:T(1024)S(1)} %pad_clamp_fusion), kind=kCustom, calls=%fused_computation | custom fusion | bytes 8913024 | tf_op jit(solution)/shard_map/gather | solution.py:134
  11.5 0.0 copy-start.2
  11.5 8.2 %all-to-all-start = ((bf16[16,2,272,256]{3,2,1,0:T(8,128)(2,1)}), bf16[16,2,272,256]{3,2,1,0:T(8,128)(2,1)}, u32[]{:S(2)}, u32[]{:S(2)}) async-start(bf16[16,2,272,256]{3,2,1,0:T(8,128)(2,1)} %bitcast.44), calls=%async_computation | async-start | bytes 8912896 | tf_op jit(solution)/shard_map/all_to_all | solution.py:135
  19.7 0.0 copy-done.2
  19.7 0.1 iota_add_fusion
  19.8 2.3 %fusion.2 = pred[512,32]{0,1:T(8,128)(4,1)S(1)} fusion(s32[32,256]{1,0:T(8,128)S(1)} %get-tuple-element.9), kind=kLoop, calls=%fused_computation.5 | loop fusion | flops 8372224 | bytes 49152 | tf_op jit(solution)/shard_map/reduce_or | solution.py:69
  22.0 3.1 %fusion = pred[32,512]{1,0:T(8,128)(4,1)S(1)} fusion(s32[32,256]{1,0:T(8,128)S(1)} %get-tuple-element.8), kind=kLoop, calls=%fused_computation.2 | loop fusion | flops 8372224 | bytes 49152 | tf_op jit(solution)/shard_map/reduce_or | solution.py:70
  25.2 60.1 %all-to-all-done = bf16[16,2,272,256]{3,2,1,0:T(8,128)(2,1)} async-done(((bf16[16,2,272,256]{3,2,1,0:T(8,128)(2,1)}), bf16[16,2,272,256]{3,2,1,0:T(8,128)(2,1)}, u32[]{:S(2)}, u32[]{:S(2)}) %all-to-all-start) | async-done | bytes 4456480 | tf_op jit(solution)/shard_map/all_to_all | solution.py:135
  85.2 1.2 slice_reduce_fusion
  86.4 5.8 %fusion.106 = bf16[32,256,512]{2,1,0:T(8,128)(2,1)S(1)} fusion(s32[32,256]{1,0:T(8,128)S(1)} %get-tuple-element.8, bf16[32,272,256]{2,1,0:T(8,128)(2,1)} %bitcast.13), kind=kOutput, calls=%fused_computation.10.clone.clone.clone.2 | convolution fusion | flops 2155872256 | bytes 12615680 | tf_op jit(solution)/shard_map/sij,sjq->siq/dot_general | solution.py:59
  92.2 4.5 %fusion.24 = f32[512,512]{1,0:T(8,128)S(1)} fusion(s32[32,256]{1,0:T(8,128)S(1)} %get-tuple-element.9, bf16[32]{0:T(256)(128)(2,1)S(1)} %slice_reduce_fusion, bf16[32,256,512]{2,1,0:T(8,128)(2,1)S(1)} %fusion.106), kind=kOutput, calls=%fused_computation.36 | convolution fusion | flops 4303355904 | bytes 9470016 | tf_op jit(solution)/shard_map/dot_general | solution.py:64
  96.7 0.4 fusion.23
  97.1 0.0 copy-start.1
  97.1 1.9 %collective-permute-start.1 = (f32[10,512]{1,0:T(8,128)S(1)}, f32[10,512]{1,0:T(8,128)S(1)}, u32[]{:S(2)}, u32[]{:S(2)}) collective-permute-start(f32[10,512]{1,0:T(8,128)S(1)} %get-tuple-element.5), channel_id=1, source_target_pairs={{16,0},{32,16},{48,32},{64,48},{80,64},{96,80},{112,96},{17,1},{33... | collective-permute-start | bytes 61448 | tf_op jit(solution)/shard_map/ppermute | solution.py:101
  99.0 2.6 %collective-permute-start = (f32[10,512]{1,0:T(8,128)S(1)}, f32[10,512]{1,0:T(8,128)S(1)}, u32[]{:S(2)}, u32[]{:S(2)}) collective-permute-start(f32[10,512]{1,0:T(8,128)S(1)} %get-tuple-element.4), channel_id=1, source_target_pairs={{0,16},{16,32},{32,48},{48,64},{64,80},{80,96},{96,112},{1,17},{17... | collective-permute-start | bytes 61448 | tf_op jit(solution)/shard_map/ppermute | solution.py:100
  101.6 0.7 fusion.56
  102.3 0.0 collective-permute-done.1
  102.3 1.9 %collective-permute-done = f32[10,512]{1,0:T(8,128)S(1)} collective-permute-done((f32[10,512]{1,0:T(8,128)S(1)}, f32[10,512]{1,0:T(8,128)S(1)}, u32[]{:S(2)}, u32[]{:S(2)}) %collective-permute-start) | collective-permute-done | bytes 20512 | tf_op jit(solution)/shard_map/ppermute | solution.py:100
  104.3 1.4 %fusion.45 = f32[512,512]{0,1:T(8,128)S(1)} fusion(f32[]{:T(128)} %fusion.56, f32[10,512]{1,0:T(8,128)S(1)} %collective-permute-done.1, f32[512,512]{1,0:T(8,128)S(1)} %fusion.23, f32[10,512]{1,0:T(8,128)S(1)} %collective-permute-done), kind=kOutput, calls=%fused_computation.53 | convolution fusion | flops 283824128 | bytes 2138116 | tf_op jit(solution)/shard_map/dot_general | solution.py:85
  105.7 1.4 %convolution_add_fusion.2 = f32[512,512]{0,1:T(8,128)S(1)} fusion(f32[512,512]{0,1:T(8,128)S(1)} %fusion.45, f32[]{:T(128)} %fusion.56, f32[10,512]{1,0:T(8,128)S(1)} %collective-permute-done.1, f32[512,512]{1,0:T(8,128)S(1)} %fusion.23, f32[10,512]{1,0:T(8,128)S(1)} %collective-permute-done), kind=kOutput, calls=%fused_computation.32 | convolution fusion | flops 284086272 | bytes 3186692 | tf_op jit(solution)/shard_map/dot_general | solution.py:85
  107.1 0.0 copy-done.1
  107.1 1.4 %convolution_add_fusion.3 = f32[512,512]{0,1:T(8,128)S(1)} fusion(f32[512,512]{0,1:T(8,128)S(1)} %convolution_add_fusion.2, f32[]{:T(128)} %fusion.56, f32[10,512]{1,0:T(8,128)S(1)} %collective-permute-done.1, f32[512,512]{1,0:T(8,128)S(1)} %fusion.23, f32[10,512]{1,0:T(8,128)S(1)} %collective-permute-done), kind=kOutput, calls=%fused_computation.33 | convolution fusion | flops 283813888 | bytes 3186692 | tf_op jit(solution)/shard_map/dot_general | solution.py:85
  108.5 4.1 %collective-permute-start.3 = (f32[10,512]{1,0:T(8,128)S(1)}, f32[10,512]{1,0:T(8,128)S(1)}, u32[]{:S(2)}, u32[]{:S(2)}) collective-permute-start(f32[10,512]{1,0:T(8,128)S(1)} %get-tuple-element.3), channel_id=1, source_target_pairs={{1,0},{2,1},{3,2},{4,3},{5,4},{6,5},{7,6},{8,7},{9,8},{10,9},{11,1... | collective-permute-start | bytes 61448 | tf_op jit(solution)/shard_map/ppermute | solution.py:105
  112.6 1.9 %collective-permute-start.2 = (f32[10,512]{1,0:T(8,128)S(1)}, f32[10,512]{1,0:T(8,128)S(1)}, u32[]{:S(2)}, u32[]{:S(2)}) collective-permute-start(f32[10,512]{1,0:T(8,128)S(1)} %get-tuple-element.2), channel_id=1, source_target_pairs={{0,1},{1,2},{2,3},{3,4},{4,5},{5,6},{6,7},{7,8},{8,9},{9,10},{10,1... | collective-permute-start | bytes 61448 | tf_op jit(solution)/shard_map/ppermute | solution.py:104
  114.6 0.0 collective-permute-done.3
  114.6 6.0 %collective-permute-done.2 = f32[10,512]{1,0:T(8,128)S(1)} collective-permute-done((f32[10,512]{1,0:T(8,128)S(1)}, f32[10,512]{1,0:T(8,128)S(1)}, u32[]{:S(2)}, u32[]{:S(2)}) %collective-permute-start.2) | collective-permute-done | bytes 20512 | tf_op jit(solution)/shard_map/ppermute | solution.py:104
  120.6 1.4 %fusion.44 = f32[512,512]{1,0:T(8,128)S(1)} fusion(f32[]{:T(128)} %fusion.56, f32[512,10]{0,1:T(8,128)S(1)} %bitcast.46, f32[512,512]{0,1:T(8,128)S(1)} %convolution_add_fusion.3, f32[512,10]{0,1:T(8,128)S(1)} %bitcast.49), kind=kOutput, calls=%fused_computation.52 | convolution fusion | flops 283824128 | bytes 2138116 | tf_op jit(solution)/shard_map/dot_general | solution.py:85
  121.9 1.3 %convolution_add_fusion = f32[512,512]{1,0:T(8,128)S(1)} fusion(f32[512,512]{1,0:T(8,128)S(1)} %fusion.44, f32[]{:T(128)} %fusion.56, f32[512,10]{0,1:T(8,128)S(1)} %bitcast.47, f32[512,512]{0,1:T(8,128)S(1)} %convolution_add_fusion.3, f32[512,10]{0,1:T(8,128)S(1)} %bitcast.50), kind=kOutput, calls=%fused_computation.30 | convolution fusion | flops 284086272 | bytes 3186692 | tf_op jit(solution)/shard_map/dot_general | solution.py:85
  123.3 2.3 %convolution_add_fusion.1 = f32[512,512]{1,0:T(8,128)} fusion(f32[512,512]{1,0:T(8,128)S(1)} %convolution_add_fusion, f32[]{:T(128)} %fusion.56, f32[512,10]{0,1:T(8,128)S(1)} %bitcast.48, f32[512,512]{0,1:T(8,128)S(1)} %convolution_add_fusion.3, f32[512,10]{0,1:T(8,128)S(1)} %bitcast.51), kind=kOutput, calls=%fused_computation.31 | convolution fusion | flops 283813888 | bytes 3186692 | tf_op jit(solution)/shard_map/dot_general | solution.py:85
  (6 shorter events, 0.0 us)
Async XLA Ops:
  0.6 2.3 %copy-start = (bf16[1,8,256,256]{3,2,1,0:T(8,128)(2,1)S(1)}, bf16[1,8,256,256]{3,2,1,0:T(8,128)(2,1)}, u32[]{:S(2)}) copy-start(bf16[1,8,256,256]{3,2,1,0:T(8,128)(2,1)} %param.6) | copy-start | bytes 3145732
  11.5 8.2 %copy-start.2 = (s32[2,1,32]{2,1,0:T(1,128)S(1)}, s32[2,1,32]{2,1,0:T(1,128)}, u32[]{:S(2)}) copy-start(s32[2,1,32]{2,1,0:T(1,128)} %param.10) | copy-start | bytes 772
  11.5 73.7 %all-to-all-start = ((bf16[16,2,272,256]{3,2,1,0:T(8,128)(2,1)}), bf16[16,2,272,256]{3,2,1,0:T(8,128)(2,1)}, u32[]{:S(2)}, u32[]{:S(2)}) async-start(bf16[16,2,272,256]{3,2,1,0:T(8,128)(2,1)} %bitcast.44), calls=%async_computation | async-start | bytes 8912896 | tf_op jit(solution)/shard_map/all_to_all | solution.py:135
  97.1 10.0 %copy-start.1 = (f32[512,512]{1,0:T(8,128)}, f32[512,512]{1,0:T(8,128)S(1)}, u32[]{:S(2)}) copy-start(f32[512,512]{1,0:T(8,128)S(1)} %fusion.23) | copy-start | bytes 3145732
  97.1 5.2 %collective-permute-start.1 = (f32[10,512]{1,0:T(8,128)S(1)}, f32[10,512]{1,0:T(8,128)S(1)}, u32[]{:S(2)}, u32[]{:S(2)}) collective-permute-start(f32[10,512]{1,0:T(8,128)S(1)} %get-tuple-element.5), channel_id=1, source_target_pairs={{16,0},{32,16},{48,32},{64,48},{80,64},{96,80},{112,96},{17,1},{33... | collective-permute-start | bytes 61448 | tf_op jit(solution)/shard_map/ppermute | solution.py:101
  99.0 5.2 %collective-permute-start = (f32[10,512]{1,0:T(8,128)S(1)}, f32[10,512]{1,0:T(8,128)S(1)}, u32[]{:S(2)}, u32[]{:S(2)}) collective-permute-start(f32[10,512]{1,0:T(8,128)S(1)} %get-tuple-element.4), channel_id=1, source_target_pairs={{0,16},{16,32},{32,48},{48,64},{64,80},{80,96},{96,112},{1,17},{17... | collective-permute-start | bytes 61448 | tf_op jit(solution)/shard_map/ppermute | solution.py:100
  108.5 6.1 %collective-permute-start.3 = (f32[10,512]{1,0:T(8,128)S(1)}, f32[10,512]{1,0:T(8,128)S(1)}, u32[]{:S(2)}, u32[]{:S(2)}) collective-permute-start(f32[10,512]{1,0:T(8,128)S(1)} %get-tuple-element.3), channel_id=1, source_target_pairs={{1,0},{2,1},{3,2},{4,3},{5,4},{6,5},{7,6},{8,7},{9,8},{10,9},{11,1... | collective-permute-start | bytes 61448 | tf_op jit(solution)/shard_map/ppermute | solution.py:105
  112.6 7.9 %collective-permute-start.2 = (f32[10,512]{1,0:T(8,128)S(1)}, f32[10,512]{1,0:T(8,128)S(1)}, u32[]{:S(2)}, u32[]{:S(2)}) collective-permute-start(f32[10,512]{1,0:T(8,128)S(1)} %get-tuple-element.2), channel_id=1, source_target_pairs={{0,1},{1,2},{2,3},{3,4},{4,5},{5,6},{6,7},{7,8},{8,9},{9,10},{10,1... | collective-permute-start | bytes 61448 | tf_op jit(solution)/shard_map/ppermute | solution.py:104

commit v6 on v5

--- a/solution.py
+++ b/solution.py
@@ -92,19 +92,32 @@
     nx = lax.axis_size("skyx")
     r = REACH
     patch = coadd.shape[0]
-    band = split(detect_band(patch, patch + 2 * r))
+    hi, lo = split(detect_band(patch, patch + 2 * r))
+    mid = jnp.concatenate([hi[:, r:patch + r], lo[:, r:patch + r]], axis=1)
+    edge = jnp.concatenate(
+        [hi[:, :r], hi[:, patch + r:], lo[:, :r], lo[:, patch + r:]], axis=1
+    )
     down = [(i, i + 1) for i in range(ny - 1)]
     up = [(i + 1, i) for i in range(ny - 1)]
     right = [(j, j + 1) for j in range(nx - 1)]
     left = [(j + 1, j) for j in range(nx - 1)]
-    top = lax.ppermute(coadd[-r:, :], "skyy", down)
-    bottom = lax.ppermute(coadd[:r, :], "skyy", up)
-    rows = jnp.concatenate([top, coadd, bottom], axis=0)
-    vert = mm3(band, split(rows))
-    west = lax.ppermute(vert[:, -r:].T, "skyx", right)
-    east = lax.ppermute(vert[:, :r].T, "skyx", left)
-    cols = jnp.concatenate([west.T, vert, east.T], axis=1)
-    return mm3(split(cols), band, (((1,), (1,)), ((), ())))
+    f32 = jnp.float32
+    own = coadd.astype(jnp.bfloat16)
+    top = lax.ppermute(own[-r:, :], "skyy", down)
+    bottom = lax.ppermute(own[:r, :], "skyy", up)
+    vert = jnp.dot(mid, jnp.concatenate([own, own], axis=0), preferred_element_type=f32)
+    rim = jnp.concatenate([top, bottom, top, bottom], axis=0)
+    vert = vert + jnp.dot(edge, rim, preferred_element_type=f32)
+    vown = vert.astype(jnp.bfloat16)
+    west = lax.ppermute(vown[:, -r:].T, "skyx", right)
+    east = lax.ppermute(vown[:, :r].T, "skyx", left)
+    on_cols = (((1,), (1,)), ((), ()))
+    by_rows = (((0,), (1,)), ((), ()))
+    result = lax.dot_general(
+        jnp.concatenate([vown, vown], axis=1), mid, on_cols, preferred_element_type=f32
+    )
+    side = jnp.concatenate([west, east, west, east], axis=0)
+    return result + lax.dot_general(side, edge, by_rows, preferred_element_type=f32)
 
 
 def body(tiles, coeffs, weights, tile_slot, slot_offset):

time: 126 us -> 119 us (0.944)
  the two profiles are of different devices: /device:TPU:36 before, /device:TPU:34 now
where the time goes in v6:
time: 119 us; the launch traced here: 118 us
  waiting for transfers between devices  65.2 us (55%)
  matrix products  20.2 us (17%)
  starting transfers between devices  18.4 us (15%)
  other arithmetic  9.32 us (8%)
  local copies, waits for them, and re-layouts  4.47 us (4%)
    all_to_all x1, waiting for transfers between devices, body(): recv = lax.all_to_all(send, 'skyx', split_axis=0, concat_axis=0, tiled=True)  58.3 us
    all_to_all x1, starting transfers between devices, body(): recv = lax.all_to_all(send, 'skyx', split_axis=0, concat_axis=0, tiled=True)  8.07 us
    dot_general x1, matrix products, coadd_patch(): jnp.einsum('sij,sjq->siq', matched, col_place, preferred_element_type=jnp...  5.76 us
    dot_general x1, matrix products, match_all(): jnp.einsum('mbik,bjk->mbij', vert, basis, preferred_element_type=jnp.floa...  5.39 us
    ppermute x1, waiting for transfers between devices, detect(): west = lax.ppermute(vown[:, -r:].T, 'skyx', right)  5.07 us
    dot_general x1, matrix products, coadd_patch(): jnp.dot(row_place.reshape(patch, slot_count * size), shifted.reshape(slot...  4.52 us
    ppermute x1, starting transfers between devices, detect(): east = lax.ppermute(vown[:, :r].T, 'skyx', left)  4.14 us
    reduce_or x1, other arithmetic, coadd_patch(): col_cover = jnp.any(col_hit, axis=1).astype(jnp.bfloat16)  3.11 us
  transfers between devices with their start and end apart: 5, of which 3 were waited for; matrix products, arithmetic and copies ran while one was open for 7% of the time, Pallas kernels for 0%

profile of v6, /device:TPU:34, one launch (start us, length us, event | category | flops | bytes accessed | tf_op | source)
XLA Modules:
  0.0 118.4 jit_solution(10142933031846742295)
XLA Ops:
  0.6 0.0 copy-start
  0.7 0.8 fusion.68
  1.5 0.7 select_reduce_fusion
  2.2 0.7 broadcast_select_fusion
  3.0 0.0 copy-done
  3.0 5.4 %fusion.4 = bf16[8,256,256]{2,1,0:T(8,128)(2,1)S(1)} fusion(bf16[1,8,5,256,256]{4,3,2,1,0:T(8,128)(2,1)} %param.7, bf16[5,256,256,1]{2,1,3,0:T(8,128)(2,1)} %constant.39, bf16[1,8,256,256]{3,2,1,0:T(8,128)(2,1)S(1)} %copy-done), kind=kOutput, calls=%fused_computation.8 | convolution fusion | flops 2694316032 | bytes 7995392 | tf_op jit(solution)/shard_map/mbik,bjk->mbij/dot_general | solution.py:47
  8.4 0.1 mul.15
  8.5 0.1 fusion.32
  8.5 2.9 %gather_fusion = bf16[32,272,256]{2,1,0:T(8,128)(2,1)} fusion(bf16[9,272,256]{2,1,0:T(8,128)(2,1)S(1)} %fusion.32, s32[1024]{0:T(1024)S(1)} %pad_clamp_fusion), kind=kCustom, calls=%fused_computation | custom fusion | bytes 8913024 | tf_op jit(solution)/shard_map/gather | solution.py:147
  11.5 8.1 %all-to-all-start = ((bf16[16,2,272,256]{3,2,1,0:T(8,128)(2,1)}), bf16[16,2,272,256]{3,2,1,0:T(8,128)(2,1)}, u32[]{:S(2)}, u32[]{:S(2)}) async-start(bf16[16,2,272,256]{3,2,1,0:T(8,128)(2,1)} %bitcast.42), calls=%async_computation | async-start | bytes 8912896 | tf_op jit(solution)/shard_map/all_to_all | solution.py:148
  19.5 0.0 copy-start.1
  19.6 0.6 fusion.71
  20.2 0.9 reduce-precision_convert_fusion
  21.0 0.1 slice.63
  21.2 0.1 slice.62
  21.3 0.0 copy-done.1
  21.3 0.1 iota_add_fusion
  21.4 2.3 %fusion.2 = pred[512,32]{0,1:T(8,128)(4,1)S(1)} fusion(s32[32,256]{1,0:T(8,128)S(1)} %get-tuple-element.15), kind=kLoop, calls=%fused_computation.5 | loop fusion | flops 8372224 | bytes 49152 | tf_op jit(solution)/shard_map/reduce_or | solution.py:69
  23.7 3.1 %fusion = pred[32,512]{1,0:T(8,128)(4,1)S(1)} fusion(s32[32,256]{1,0:T(8,128)S(1)} %get-tuple-element.14), kind=kLoop, calls=%fused_computation.2 | loop fusion | flops 8372224 | bytes 49152 | tf_op jit(solution)/shard_map/reduce_or | solution.py:70
  26.8 58.3 %all-to-all-done = bf16[16,2,272,256]{3,2,1,0:T(8,128)(2,1)} async-done(((bf16[16,2,272,256]{3,2,1,0:T(8,128)(2,1)}), bf16[16,2,272,256]{3,2,1,0:T(8,128)(2,1)}, u32[]{:S(2)}, u32[]{:S(2)}) %all-to-all-start) | async-done | bytes 4456480 | tf_op jit(solution)/shard_map/all_to_all | solution.py:148
  85.1 1.2 slice_reduce_fusion
  86.2 5.8 %fusion.96 = bf16[32,256,512]{2,1,0:T(8,128)(2,1)S(1)} fusion(s32[32,256]{1,0:T(8,128)S(1)} %get-tuple-element.14, bf16[32,272,256]{2,1,0:T(8,128)(2,1)} %bitcast.13), kind=kOutput, calls=%fused_computation.10.clone.clone.clone.2 | convolution fusion | flops 2155872256 | bytes 12615680 | tf_op jit(solution)/shard_map/sij,sjq->siq/dot_general | solution.py:59
  92.0 4.5 %fusion.24 = f32[512,512]{1,0:T(8,128)S(1)} fusion(s32[32,256]{1,0:T(8,128)S(1)} %get-tuple-element.15, bf16[32]{0:T(256)(128)(2,1)S(1)} %slice_reduce_fusion, bf16[32,256,512]{2,1,0:T(8,128)(2,1)S(1)} %fusion.96), kind=kOutput, calls=%fused_computation.30 | convolution fusion | flops 4303355904 | bytes 9470016 | tf_op jit(solution)/shard_map/dot_general | solution.py:64
  96.5 1.4 %fusion.82 = (bf16[512,512]{1,0:T(8,128)(2,1)S(1)}, f32[512,512]{1,0:T(8,128)}) fusion(f32[512,512]{1,0:T(8,128)S(1)} %fusion.24, pred[32,512]{1,0:T(8,128)(4,1)S(1)} %fusion, pred[512,32]{0,1:T(8,128)(4,1)S(1)} %fusion.2, bf16[32]{0:T(256)(128)(2,1)S(1)} %slice_reduce_fusion), kind=kOutput, calls=%fused_computation.98 | convolution fusion | flops 17580032 | bytes 2654272 | tf_op jit(solution)/shard_map/dot_general | solution.py:71
  97.9 1.9 %collective-permute-start.1 = (bf16[10,512]{1,0:T(8,128)(2,1)S(1)}, bf16[10,512]{1,0:T(8,128)(2,1)S(1)}, u32[]{:S(2)}, u32[]{:S(2)}) collective-permute-start(bf16[10,512]{1,0:T(8,128)(2,1)S(1)} %get-tuple-element.9), channel_id=1, source_target_pairs={{16,0},{32,16},{48,32},{64,48},{80,64},{96,80},{112,96},{17,1},{33... | collective-permute-start | bytes 30728 | tf_op jit(solution)/shard_map/ppermute | solution.py:107
  99.8 2.4 %collective-permute-start = (bf16[10,512]{1,0:T(8,128)(2,1)S(1)}, bf16[10,512]{1,0:T(8,128)(2,1)S(1)}, u32[]{:S(2)}, u32[]{:S(2)}) collective-permute-start(bf16[10,512]{1,0:T(8,128)(2,1)S(1)} %get-tuple-element.8), channel_id=1, source_target_pairs={{0,16},{16,32},{32,48},{48,64},{64,80},{80,96},{96,112},{1,17},{17... | collective-permute-start | bytes 30728 | tf_op jit(solution)/shard_map/ppermute | solution.py:106
  102.2 0.8 fusion.41
  103.0 0.0 collective-permute-done.1
  103.0 1.9 %collective-permute-done = bf16[10,512]{1,0:T(8,128)(2,1)S(1)} collective-permute-done((bf16[10,512]{1,0:T(8,128)(2,1)S(1)}, bf16[10,512]{1,0:T(8,128)(2,1)S(1)}, u32[]{:S(2)}, u32[]{:S(2)}) %collective-permute-start) | collective-permute-done | bytes 10272 | tf_op jit(solution)/shard_map/ppermute | solution.py:106
  104.9 0.3 fusion.31
  105.2 4.1 %collective-permute-start.3 = (bf16[10,512]{1,0:T(8,128)(2,1)S(1)}, bf16[10,512]{1,0:T(8,128)(2,1)S(1)}, u32[]{:S(2)}, u32[]{:S(2)}) collective-permute-start(bf16[10,512]{1,0:T(8,128)(2,1)S(1)} %get-tuple-element.7), channel_id=1, source_target_pairs={{1,0},{2,1},{3,2},{4,3},{5,4},{6,5},{7,6},{8,7},{9,8},{10,9},{11,1... | collective-permute-start | bytes 30728 | tf_op jit(solution)/shard_map/ppermute | solution.py:113
  109.4 1.9 %collective-permute-start.2 = (bf16[10,512]{1,0:T(8,128)(2,1)S(1)}, bf16[10,512]{1,0:T(8,128)(2,1)S(1)}, u32[]{:S(2)}, u32[]{:S(2)}) collective-permute-start(bf16[10,512]{1,0:T(8,128)(2,1)S(1)} %get-tuple-element.6), channel_id=1, source_target_pairs={{0,1},{1,2},{2,3},{3,4},{4,5},{5,6},{6,7},{7,8},{8,9},{9,10},{10,1... | collective-permute-start | bytes 30728 | tf_op jit(solution)/shard_map/ppermute | solution.py:112
  111.3 0.7 fusion.45
  112.0 0.0 collective-permute-done.3
  112.0 5.1 %collective-permute-done.2 = bf16[10,512]{1,0:T(8,128)(2,1)S(1)} collective-permute-done((bf16[10,512]{1,0:T(8,128)(2,1)S(1)}, bf16[10,512]{1,0:T(8,128)(2,1)S(1)}, u32[]{:S(2)}, u32[]{:S(2)}) %collective-permute-start.2) | collective-permute-done | bytes 10272 | tf_op jit(solution)/shard_map/ppermute | solution.py:112
  117.1 1.3 %convolution_add_fusion = f32[512,512]{1,0:T(8,128)} fusion(f32[512,512]{1,0:T(8,128)S(1)} %fusion.45, bf16[10,512]{1,0:T(8,128)(2,1)S(1)} %collective-permute-done.3, bf16[10,512]{1,0:T(8,128)(2,1)S(1)} %collective-permute-done.2, bf16[512,10]{0,1:T(8,128)(2,1)S(1)} %get-tuple-element.5, bf16[512,10]{0,1:T(8,128)(2,1)S(1)} %get-tuple-element.4, ...), kind=kOutput, calls=%fused_computation.26 | convolution fusion | flops 21561344 | bytes 2158592 | tf_op jit(solution)/shard_map/dot_general | solution.py:120
  (8 shorter events, 0.1 us)
Async XLA Ops:
  0.6 2.3 %copy-start = (bf16[1,8,256,256]{3,2,1,0:T(8,128)(2,1)S(1)}, bf16[1,8,256,256]{3,2,1,0:T(8,128)(2,1)}, u32[]{:S(2)}) copy-start(bf16[1,8,256,256]{3,2,1,0:T(8,128)(2,1)} %param.6) | copy-start | bytes 3145732
  11.5 73.6 %all-to-all-start = ((bf16[16,2,272,256]{3,2,1,0:T(8,128)(2,1)}), bf16[16,2,272,256]{3,2,1,0:T(8,128)(2,1)}, u32[]{:S(2)}, u32[]{:S(2)}) async-start(bf16[16,2,272,256]{3,2,1,0:T(8,128)(2,1)} %bitcast.42), calls=%async_computation | async-start | bytes 8912896 | tf_op jit(solution)/shard_map/all_to_all | solution.py:148
  19.5 1.7 %copy-start.1 = (s32[2,1,32]{2,1,0:T(1,128)S(1)}, s32[2,1,32]{2,1,0:T(1,128)}, u32[]{:S(2)}) copy-start(s32[2,1,32]{2,1,0:T(1,128)} %param.10) | copy-start | bytes 772
  97.9 5.1 %collective-permute-start.1 = (bf16[10,512]{1,0:T(8,128)(2,1)S(1)}, bf16[10,512]{1,0:T(8,128)(2,1)S(1)}, u32[]{:S(2)}, u32[]{:S(2)}) collective-permute-start(bf16[10,512]{1,0:T(8,128)(2,1)S(1)} %get-tuple-element.9), channel_id=1, source_target_pairs={{16,0},{32,16},{48,32},{64,48},{80,64},{96,80},{112,96},{17,1},{33... | collective-permute-start | bytes 30728 | tf_op jit(solution)/shard_map/ppermute | solution.py:107
  99.8 5.1 %collective-permute-start = (bf16[10,512]{1,0:T(8,128)(2,1)S(1)}, bf16[10,512]{1,0:T(8,128)(2,1)S(1)}, u32[]{:S(2)}, u32[]{:S(2)}) collective-permute-start(bf16[10,512]{1,0:T(8,128)(2,1)S(1)} %get-tuple-element.8), channel_id=1, source_target_pairs={{0,16},{16,32},{32,48},{48,64},{64,80},{80,96},{96,112},{1,17},{17... | collective-permute-start | bytes 30728 | tf_op jit(solution)/shard_map/ppermute | solution.py:106
  105.2 6.8 %collective-permute-start.3 = (bf16[10,512]{1,0:T(8,128)(2,1)S(1)}, bf16[10,512]{1,0:T(8,128)(2,1)S(1)}, u32[]{:S(2)}, u32[]{:S(2)}) collective-permute-start(bf16[10,512]{1,0:T(8,128)(2,1)S(1)} %get-tuple-element.7), channel_id=1, source_target_pairs={{1,0},{2,1},{3,2},{4,3},{5,4},{6,5},{7,6},{8,7},{9,8},{10,9},{11,1... | collective-permute-start | bytes 30728 | tf_op jit(solution)/shard_map/ppermute | solution.py:113
  109.4 7.7 %collective-permute-start.2 = (bf16[10,512]{1,0:T(8,128)(2,1)S(1)}, bf16[10,512]{1,0:T(8,128)(2,1)S(1)}, u32[]{:S(2)}, u32[]{:S(2)}) collective-permute-start(bf16[10,512]{1,0:T(8,128)(2,1)S(1)} %get-tuple-element.6), channel_id=1, source_target_pairs={{0,1},{1,2},{2,3},{3,4},{4,5},{5,6},{6,7},{7,8},{8,9},{9,10},{10,1... | collective-permute-start | bytes 30728 | tf_op jit(solution)/shard_map/ppermute | solution.py:112

commit v7 on v6

--- a/solution.py
+++ b/solution.py
@@ -66,8 +66,12 @@
         shifted.reshape(slot_count * size, patch),
         preferred_element_type=jnp.float32,
     )
-    row_cover = jnp.where(jnp.any(row_hit, axis=2), slot_weight[None, :], zero_weight)
-    col_cover = jnp.any(col_hit, axis=1).astype(jnp.bfloat16)
+    row_gap = pixel[:, None] - offsets[0][None, :]
+    col_gap = pixel[None, :] - offsets[1][:, None]
+    row_in = (row_gap >= 0) & (row_gap < size)
+    col_in = (col_gap >= 0) & (col_gap < size)
+    row_cover = jnp.where(row_in, slot_weight[None, :], zero_weight)
+    col_cover = col_in.astype(jnp.bfloat16)
     cover = jnp.dot(row_cover, col_cover, preferred_element_type=jnp.float32)
     return numer / (1.0 + cover)
 
@@ -87,16 +91,21 @@
     return one(ah, bh) + (one(al, bh) + one(ah, bl))
 
 
-def detect(coadd):
-    ny = lax.axis_size("skyy")
-    nx = lax.axis_size("skyx")
+def detect_filters(patch):
     r = REACH
-    patch = coadd.shape[0]
     hi, lo = split(detect_band(patch, patch + 2 * r))
     mid = jnp.concatenate([hi[:, r:patch + r], lo[:, r:patch + r]], axis=1)
     edge = jnp.concatenate(
         [hi[:, :r], hi[:, patch + r:], lo[:, :r], lo[:, patch + r:]], axis=1
     )
+    return mid, edge
+
+
+def detect(coadd, mid, edge):
+    ny = lax.axis_size("skyy")
+    nx = lax.axis_size("skyx")
+    r = REACH
+    patch = coadd.shape[0]
     down = [(i, i + 1) for i in range(ny - 1)]
     up = [(i + 1, i) for i in range(ny - 1)]
     right = [(j, j + 1) for j in range(nx - 1)]
@@ -145,12 +154,15 @@
     carry = jnp.concatenate([own_matched, weight_rows], axis=1)
     carry = jnp.concatenate([carry, jnp.zeros((1, size + extra, size), jnp.bfloat16)], axis=0)
     send = carry[which].reshape(columns, CAP, size + extra, size)
+    filters = detect_filters(patch)
+    send, filters = lax.optimization_barrier((send, filters))
     recv = lax.all_to_all(send, "skyx", split_axis=0, concat_axis=0, tiled=True)
+    recv, offsets, filters = lax.optimization_barrier((recv, offsets, filters))
     recv = recv.reshape(slots, size + extra, size)
     matched = recv[:, :size, :]
     recv_weight = recv[:, size, 0]
     coadd = coadd_patch(matched, recv_weight, offsets, patch)
-    detection = detect(coadd)
+    detection = detect(coadd, *filters)
     return (coadd, detection)
 
 

time: 119 us -> 105 us (0.88)
  the two profiles are of different devices: /device:TPU:34 before, /device:TPU:29 now
where the time goes in v7:
time: 105 us; the launch traced here: 104 us
  blocking collectives  58.4 us (56%)
  matrix products  19.6 us (19%)
  starting transfers between devices  11.9 us (11%)
  waiting for transfers between devices  6.7 us (6%)
  local copies, waits for them, and re-layouts  3.58 us (3%)
  other arithmetic  3.35 us (3%)
    all_to_all x1, blocking collectives, body(): recv = lax.all_to_all(send, 'skyx', split_axis=0, concat_axis=0, tiled=True)  58.4 us
    dot_general x1, matrix products, match_all(): jnp.einsum('mbik,bjk->mbij', vert, basis, preferred_element_type=jnp.floa...  6.26 us
    dot_general x1, matrix products, coadd_patch(): jnp.dot(row_place.reshape(patch, slot_count * size), shifted.reshape(slot...  4.51 us
    ppermute x1, starting transfers between devices, detect(): top = lax.ppermute(own[-r:, :], 'skyy', down)  4.48 us
    dot_general x1, matrix products, coadd_patch(): jnp.einsum('sij,sjq->siq', matched, col_place, preferred_element_type=jnp...  4.39 us
    ppermute x1, waiting for transfers between devices, detect(): east = lax.ppermute(vown[:, :r].T, 'skyx', left)  4.33 us
    ppermute x1, starting transfers between devices, detect(): west = lax.ppermute(vown[:, -r:].T, 'skyx', right)  3.54 us
    gather x1, local copies, waits for them, and re-layouts, body(): send = carry[which].reshape(columns, CAP, size + extra, size)  2.87 us
  transfers between devices with their start and end apart: 4, of which 2 were waited for; matrix products, arithmetic and copies ran while one was open for 1% of the time, Pallas kernels for 0%

profile of v7, /device:TPU:29, one launch (start us, length us, event | category | flops | bytes accessed | tf_op | source)
XLA Modules:
  0.0 104.3 jit_solution(13611416770787900364)
XLA Ops:
  0.6 0.0 copy-start
  0.6 0.0 copy-start.3
  0.7 0.6 fusion.84
  1.3 0.0 copy-start.2
  1.3 0.0 copy-start.4
  1.3 0.9 reduce-precision_convert_fusion
  2.2 0.1 slice.60
  2.4 0.1 slice.61
  2.5 0.0 copy-done.3
  2.5 0.1 fusion.81
  2.6 0.1 select_reduce_fusion
  2.7 0.1 pad_maximum_fusion
  2.8 0.0 copy-done.2
  2.8 0.1 broadcast_select_fusion
  2.9 0.0 copy-done
  2.9 0.0 copy-done.4
  2.9 6.3 %fusion.2 = bf16[8,256,256]{2,1,0:T(8,128)(2,1)} fusion(bf16[1,8,5,256,256]{4,3,2,1,0:T(8,128)(2,1)} %param.7, bf16[5,256,256,1]{2,1,3,0:T(8,128)(2,1)S(1)} %copy-done.4, bf16[1,8,256,256]{3,2,1,0:T(8,128)(2,1)S(1)} %copy-done), kind=kOutput, calls=%fused_computation.6 | convolution fusion | flops 2694316032 | bytes 7995392 | tf_op jit(solution)/shard_map/mbik,bjk->mbij/dot_general | solution.py:47
  9.1 0.1 mul.15
  9.2 1.3 %fusion.30 = bf16[9,272,256]{2,1,0:T(8,128)(2,1)S(1)} fusion(bf16[8,16,256]{2,1,0:T(8,128)(2,1)S(1)} %mul.15, bf16[8,256,256]{2,1,0:T(8,128)(2,1)} %fusion.2), kind=kLoop, calls=%fused_computation.30 | loop fusion | flops 4386816 | bytes 2367488 | tf_op jit(solution)/shard_map/concatenate | solution.py:154
  10.5 2.9 %gather_fusion = bf16[32,272,256]{2,1,0:T(8,128)(2,1)} fusion(bf16[9,272,256]{2,1,0:T(8,128)(2,1)S(1)} %fusion.30, s32[1024]{0:T(1024)S(1)} %pad_clamp_fusion), kind=kCustom, calls=%fused_computation | custom fusion | bytes 8913024 | tf_op jit(solution)/shard_map/gather | solution.py:156
  13.4 0.0 copy-start.1
  13.4 58.4 %all_to_all.5 = bf16[16,2,272,256]{3,2,1,0:T(8,128)(2,1)S(1)} all-to-all(bf16[16,2,272,256]{3,2,1,0:T(8,128)(2,1)} %bitcast.46), channel_id=1, replica_groups=mesh['skyy'=8,'skyx'=16] {'skyx'}, dimensions={0} | all-to-all | bytes 8912896 | tf_op jit(solution)/shard_map/all_to_all | solution.py:159
  71.8 0.0 copy-done.1
  71.8 0.1 iota_add_fusion
  71.9 0.3 slice_reduce_fusion
  72.2 4.4 %fusion.114 = bf16[32,256,512]{2,1,0:T(8,128)(2,1)S(1)} fusion(s32[32,256]{1,0:T(8,128)S(1)} %iota_add_fusion, bf16[32,272,256]{2,1,0:T(8,128)(2,1)S(1)} %bitcast.48), kind=kOutput, calls=%fused_computation.8.clone.clone.clone.2 | convolution fusion | flops 2155872256 | bytes 12615680 | tf_op jit(solution)/shard_map/sij,sjq->siq/dot_general | solution.py:59
  76.6 0.1 iota_add_fusion.1
  76.7 4.5 %fusion.22 = f32[512,512]{1,0:T(8,128)S(1)} fusion(s32[32,256]{1,0:T(8,128)S(1)} %iota_add_fusion.1, bf16[32]{0:T(256)(128)(2,1)S(1)} %slice_reduce_fusion, bf16[32,256,512]{2,1,0:T(8,128)(2,1)S(1)} %fusion.114), kind=kOutput, calls=%fused_computation.28 | convolution fusion | flops 4303355904 | bytes 9470016 | tf_op jit(solution)/shard_map/dot_general | solution.py:64
  81.2 1.3 %fusion.97 = (bf16[512,512]{1,0:T(8,128)(2,1)S(1)}, f32[512,512]{1,0:T(8,128)}) fusion(f32[512,512]{1,0:T(8,128)S(1)} %fusion.22, s32[32]{0:T(128)S(1)} %get-tuple-element.25, s32[32]{0:T(128)S(1)} %get-tuple-element.24, bf16[32]{0:T(256)(128)(2,1)S(1)} %slice_reduce_fusion), kind=kOutput, calls=%fused_computation.112 | convolution fusion | flops 17711104 | bytes 2621760 | tf_op jit(solution)/shard_map/dot_general | solution.py:75
  82.5 4.5 %collective-permute-start = (bf16[10,512]{1,0:T(8,128)(2,1)S(1)}, bf16[10,512]{1,0:T(8,128)(2,1)S(1)}, u32[]{:S(2)}, u32[]{:S(2)}) collective-permute-start(bf16[10,512]{1,0:T(8,128)(2,1)S(1)} %get-tuple-element.22), channel_id=1, source_target_pairs={{0,16},{16,32},{32,48},{48,64},{64,80},{80,96},{96,112},{1,17},{17... | collective-permute-start | bytes 30728 | tf_op jit(solution)/shard_map/ppermute | solution.py:115
  87.0 1.9 %collective-permute-start.1 = (bf16[10,512]{1,0:T(8,128)(2,1)S(1)}, bf16[10,512]{1,0:T(8,128)(2,1)S(1)}, u32[]{:S(2)}, u32[]{:S(2)}) collective-permute-start(bf16[10,512]{1,0:T(8,128)(2,1)S(1)} %get-tuple-element.23), channel_id=1, source_target_pairs={{16,0},{32,16},{48,32},{64,48},{80,64},{96,80},{112,96},{17,1},{33... | collective-permute-start | bytes 30728 | tf_op jit(solution)/shard_map/ppermute | solution.py:116
  89.0 0.8 fusion.39
  89.7 0.0 collective-permute-done
  89.7 2.4 %collective-permute-done.1 = bf16[10,512]{1,0:T(8,128)(2,1)S(1)} collective-permute-done((bf16[10,512]{1,0:T(8,128)(2,1)S(1)}, bf16[10,512]{1,0:T(8,128)(2,1)S(1)}, u32[]{:S(2)}, u32[]{:S(2)}) %collective-permute-start.1) | collective-permute-done | bytes 10272 | tf_op jit(solution)/shard_map/ppermute | solution.py:116
  92.1 0.3 fusion.29
  92.5 3.5 %collective-permute-start.2 = (bf16[10,512]{1,0:T(8,128)(2,1)S(1)}, bf16[10,512]{1,0:T(8,128)(2,1)S(1)}, u32[]{:S(2)}, u32[]{:S(2)}) collective-permute-start(bf16[10,512]{1,0:T(8,128)(2,1)S(1)} %get-tuple-element.20), channel_id=1, source_target_pairs={{0,1},{1,2},{2,3},{3,4},{4,5},{5,6},{6,7},{7,8},{8,9},{9,10},{10,1... | collective-permute-start | bytes 30728 | tf_op jit(solution)/shard_map/ppermute | solution.py:121
  96.0 1.9 %collective-permute-start.3 = (bf16[10,512]{1,0:T(8,128)(2,1)S(1)}, bf16[10,512]{1,0:T(8,128)(2,1)S(1)}, u32[]{:S(2)}, u32[]{:S(2)}) collective-permute-start(bf16[10,512]{1,0:T(8,128)(2,1)S(1)} %get-tuple-element.21), channel_id=1, source_target_pairs={{1,0},{2,1},{3,2},{4,3},{5,4},{6,5},{7,6},{8,7},{9,8},{10,9},{11,1... | collective-permute-start | bytes 30728 | tf_op jit(solution)/shard_map/ppermute | solution.py:122
  97.9 0.7 fusion.43
  98.7 0.0 collective-permute-done.2
  98.7 4.3 %collective-permute-done.3 = bf16[10,512]{1,0:T(8,128)(2,1)S(1)} collective-permute-done((bf16[10,512]{1,0:T(8,128)(2,1)S(1)}, bf16[10,512]{1,0:T(8,128)(2,1)S(1)}, u32[]{:S(2)}, u32[]{:S(2)}) %collective-permute-start.3) | collective-permute-done | bytes 10272 | tf_op jit(solution)/shard_map/ppermute | solution.py:122
  103.0 1.3 %convolution_add_fusion = f32[512,512]{1,0:T(8,128)} fusion(f32[512,512]{1,0:T(8,128)S(1)} %fusion.43, bf16[512,40]{0,1:T(8,128)(2,1)S(1)} %pad_maximum_fusion.1, bf16[10,512]{1,0:T(8,128)(2,1)S(1)} %collective-permute-done.3, bf16[10,512]{1,0:T(8,128)(2,1)S(1)} %collective-permute-done.2), kind=kOutput, calls=%fused_computation.24 | convolution fusion | flops 21397504 | bytes 2158592 | tf_op jit(solution)/shard_map/dot_general | solution.py:129
  (9 shorter events, 0.1 us)
Async XLA Ops:
  0.6 2.2 %copy-start = (bf16[1,8,256,256]{3,2,1,0:T(8,128)(2,1)S(1)}, bf16[1,8,256,256]{3,2,1,0:T(8,128)(2,1)}, u32[]{:S(2)}) copy-start(bf16[1,8,256,256]{3,2,1,0:T(8,128)(2,1)} %param.6) | copy-start | bytes 3145732
  0.6 1.9 %copy-start.3 = (s32[1,8]{1,0:T(1,128)S(1)}, s32[1,8]{1,0:T(1,128)}, u32[]{:S(2)}) copy-start(s32[1,8]{1,0:T(1,128)} %param.9) | copy-start | bytes 100
  1.3 1.5 %copy-start.2 = (bf16[1,8]{1,0:T(2,128)(2,1)S(1)}, bf16[1,8]{1,0:T(2,128)(2,1)}, u32[]{:S(2)}) copy-start(bf16[1,8]{1,0:T(2,128)(2,1)} %param.8) | copy-start | bytes 52
  1.3 1.6 %copy-start.4 = (bf16[5,256,256,1]{2,1,3,0:T(8,128)(2,1)S(1)}, bf16[5,256,256,1]{2,1,3,0:T(8,128)(2,1)}, u32[]{:S(2)}) copy-start(bf16[5,256,256,1]{2,1,3,0:T(8,128)(2,1)} %constant.44) | copy-start | bytes 1966084
  13.4 58.4 %copy-start.1 = (s32[2,1,32]{2,1,0:T(1,128)S(1)}, s32[2,1,32]{2,1,0:T(1,128)}, u32[]{:S(2)}) copy-start(s32[2,1,32]{2,1,0:T(1,128)} %param.10) | copy-start | bytes 772
  82.5 7.2 %collective-permute-start = (bf16[10,512]{1,0:T(8,128)(2,1)S(1)}, bf16[10,512]{1,0:T(8,128)(2,1)S(1)}, u32[]{:S(2)}, u32[]{:S(2)}) collective-permute-start(bf16[10,512]{1,0:T(8,128)(2,1)S(1)} %get-tuple-element.22), channel_id=1, source_target_pairs={{0,16},{16,32},{32,48},{48,64},{64,80},{80,96},{96,112},{1,17},{17... | collective-permute-start | bytes 30728 | tf_op jit(solution)/shard_map/ppermute | solution.py:115
  87.0 5.1 %collective-permute-start.1 = (bf16[10,512]{1,0:T(8,128)(2,1)S(1)}, bf16[10,512]{1,0:T(8,128)(2,1)S(1)}, u32[]{:S(2)}, u32[]{:S(2)}) collective-permute-start(bf16[10,512]{1,0:T(8,128)(2,1)S(1)} %get-tuple-element.23), channel_id=1, source_target_pairs={{16,0},{32,16},{48,32},{64,48},{80,64},{96,80},{112,96},{17,1},{33... | collective-permute-start | bytes 30728 | tf_op jit(solution)/shard_map/ppermute | solution.py:116
  92.5 6.2 %collective-permute-start.2 = (bf16[10,512]{1,0:T(8,128)(2,1)S(1)}, bf16[10,512]{1,0:T(8,128)(2,1)S(1)}, u32[]{:S(2)}, u32[]{:S(2)}) collective-permute-start(bf16[10,512]{1,0:T(8,128)(2,1)S(1)} %get-tuple-element.20), channel_id=1, source_target_pairs={{0,1},{1,2},{2,3},{3,4},{4,5},{5,6},{6,7},{7,8},{8,9},{9,10},{10,1... | collective-permute-start | bytes 30728 | tf_op jit(solution)/shard_map/ppermute | solution.py:121
  96.0 7.0 %collective-permute-start.3 = (bf16[10,512]{1,0:T(8,128)(2,1)S(1)}, bf16[10,512]{1,0:T(8,128)(2,1)S(1)}, u32[]{:S(2)}, u32[]{:S(2)}) collective-permute-start(bf16[10,512]{1,0:T(8,128)(2,1)S(1)} %get-tuple-element.21), channel_id=1, source_target_pairs={{1,0},{2,1},{3,2},{4,3},{5,4},{6,5},{7,6},{8,7},{9,8},{10,9},{11,1... | collective-permute-start | bytes 30728 | tf_op jit(solution)/shard_map/ppermute | solution.py:122

commit v8 on v7

--- a/solution.py
+++ b/solution.py
@@ -26,18 +26,6 @@
         total = np.sum(np.exp(-taps * taps / scale), dtype=np.float32)
         mats.append(np.where(inside, np.exp(-gap * gap / scale) / total, np.float32(0.0)))
     return np.stack(mats).astype(np.float32).astype(jnp.bfloat16)
-
-
-def detect_band(out_size, in_size):
-    taps = jnp.arange(-REACH, REACH + 1).astype(jnp.float32)
-    scale = 2.0 * detect_width * detect_width
-    total = jnp.sum(jnp.exp(-taps * taps / scale))
-    rows = jnp.arange(out_size, dtype=jnp.int32)[:, None]
-    cols = jnp.arange(in_size, dtype=jnp.int32)[None, :]
-    gap = cols - rows
-    inside = (gap >= 0) & (gap <= 2 * REACH)
-    tap = (gap - REACH).astype(jnp.float32)
-    return jnp.where(inside, jnp.exp(-tap * tap / scale) / total, 0.0)
 
 
 def match_all(tiles, coeffs, basis):
@@ -93,12 +81,20 @@
 
 def detect_filters(patch):
     r = REACH
-    hi, lo = split(detect_band(patch, patch + 2 * r))
-    mid = jnp.concatenate([hi[:, r:patch + r], lo[:, r:patch + r]], axis=1)
-    edge = jnp.concatenate(
-        [hi[:, :r], hi[:, patch + r:], lo[:, :r], lo[:, patch + r:]], axis=1
-    )
-    return mid, edge
+    taps = np.arange(-r, r + 1).astype(np.float32)
+    scale = np.float32(2.0 * detect_width * detect_width)
+    total = np.sum(np.exp(-taps * taps / scale), dtype=np.float32)
+    rows = np.arange(patch, dtype=np.int32)[:, None]
+    cols = np.arange(patch + 2 * r, dtype=np.int32)[None, :]
+    gap = cols - rows
+    inside = (gap >= 0) & (gap <= 2 * r)
+    tap = (gap - r).astype(np.float32)
+    band = np.where(inside, np.exp(-tap * tap / scale) / total, np.float32(0.0)).astype(np.float32)
+    hi = band.astype(jnp.bfloat16)
+    lo = (band - hi.astype(np.float32)).astype(jnp.bfloat16)
+    mid = np.concatenate([hi[:, r:patch + r], lo[:, r:patch + r]], axis=1)
+    edge = np.concatenate([hi[:, :r], hi[:, patch + r:], lo[:, :r], lo[:, patch + r:]], axis=1)
+    return jnp.asarray(mid), jnp.asarray(edge)
 
 
 def detect(coadd, mid, edge):
@@ -155,7 +151,6 @@
     carry = jnp.concatenate([carry, jnp.zeros((1, size + extra, size), jnp.bfloat16)], axis=0)
     send = carry[which].reshape(columns, CAP, size + extra, size)
     filters = detect_filters(patch)
-    send, filters = lax.optimization_barrier((send, filters))
     recv = lax.all_to_all(send, "skyx", split_axis=0, concat_axis=0, tiled=True)
     recv, offsets, filters = lax.optimization_barrier((recv, offsets, filters))
     recv = recv.reshape(slots, size + extra, size)

time: 105 us -> 103 us (0.981)
    concatenate x1, other arithmetic: 1.31 us -> 0.08 us  [body(): carry = jnp.concatenate([own_matched, weight_rows], axis=1)]
where the time goes in v8:
time: 103 us; the launch traced here: 102 us
  blocking collectives  58.5 us (57%)
  matrix products  18.8 us (18%)
  starting transfers between devices  11.9 us (12%)
  waiting for transfers between devices  6.61 us (6%)
  local copies, waits for them, and re-layouts  3.32 us (3%)
  other arithmetic  2.47 us (2%)
    all_to_all x1, blocking collectives, body(): recv = lax.all_to_all(send, 'skyx', split_axis=0, concat_axis=0, tiled=True)  58.5 us
    dot_general x1, matrix products, match_all(): jnp.einsum('mbik,bjk->mbij', vert, basis, preferred_element_type=jnp.floa...  5.39 us
    dot_general x1, matrix products, coadd_patch(): jnp.dot(row_place.reshape(patch, slot_count * size), shifted.reshape(slot...  4.51 us
    ppermute x1, starting transfers between devices, detect(): top = lax.ppermute(own[-r:, :], 'skyy', down)  4.48 us
    dot_general x1, matrix products, coadd_patch(): jnp.einsum('sij,sjq->siq', matched, col_place, preferred_element_type=jnp...  4.39 us
    ppermute x1, waiting for transfers between devices, detect(): east = lax.ppermute(vown[:, :r].T, 'skyx', left)  4.26 us
    ppermute x1, starting transfers between devices, detect(): west = lax.ppermute(vown[:, -r:].T, 'skyx', right)  3.55 us
    gather x1, local copies, waits for them, and re-layouts, body(): send = carry[which].reshape(columns, CAP, size + extra, size)  2.87 us
  transfers between devices with their start and end apart: 4, of which 2 were waited for; matrix products, arithmetic and copies ran while one was open for 1% of the time, Pallas kernels for 0%

profile of v8, /device:TPU:29, one launch (start us, length us, event | category | flops | bytes accessed | tf_op | source)
XLA Modules:
  0.0 102.3 jit_solution(16055647200846960223)
XLA Ops:
  0.6 0.0 copy-start
  0.6 0.8 fusion.73
  1.5 0.7 select_reduce_fusion
  2.2 0.7 broadcast_select_fusion
  3.0 0.0 copy-done
  3.0 5.4 %fusion.2 = bf16[8,256,256]{2,1,0:T(8,128)(2,1)S(1)} fusion(bf16[1,8,5,256,256]{4,3,2,1,0:T(8,128)(2,1)} %param.9, bf16[5,256,256,1]{2,1,3,0:T(8,128)(2,1)} %constant.38, bf16[1,8,256,256]{3,2,1,0:T(8,128)(2,1)S(1)} %copy-done), kind=kOutput, calls=%fused_computation.6 | convolution fusion | flops 2694316032 | bytes 7995392 | tf_op jit(solution)/shard_map/mbik,bjk->mbij/dot_general | solution.py:35
  8.4 0.1 mul.9
  8.5 0.1 fusion.30
  8.6 2.9 %gather_fusion = bf16[32,272,256]{2,1,0:T(8,128)(2,1)} fusion(bf16[9,272,256]{2,1,0:T(8,128)(2,1)S(1)} %fusion.30, s32[1024]{0:T(1024)S(1)} %pad_clamp_fusion), kind=kCustom, calls=%fused_computation | custom fusion | bytes 8913024 | tf_op jit(solution)/shard_map/gather | solution.py:152
  11.4 0.0 copy-start.2
  11.4 58.5 %all_to_all.5 = bf16[16,2,272,256]{3,2,1,0:T(8,128)(2,1)S(1)} all-to-all(bf16[16,2,272,256]{3,2,1,0:T(8,128)(2,1)} %bitcast.46), channel_id=1, replica_groups=mesh['skyy'=8,'skyx'=16] {'skyx'}, dimensions={0} | all-to-all | bytes 8912896 | tf_op jit(solution)/shard_map/all_to_all | solution.py:154
  69.9 0.0 copy-done.2
  69.9 0.3 slice_reduce_fusion
  70.2 0.1 iota_add_fusion
  70.3 4.4 %fusion.101 = bf16[32,256,512]{2,1,0:T(8,128)(2,1)S(1)} fusion(s32[32,256]{1,0:T(8,128)S(1)} %get-tuple-element.18, bf16[32,272,256]{2,1,0:T(8,128)(2,1)S(1)} %bitcast.48), kind=kOutput, calls=%fused_computation.8.clone.clone.clone.2 | convolution fusion | flops 2155872256 | bytes 12615680 | tf_op jit(solution)/shard_map/sij,sjq->siq/dot_general | solution.py:47
  74.7 0.0 copy-start.3
  74.7 4.5 %fusion.22 = f32[512,512]{1,0:T(8,128)S(1)} fusion(s32[32,256]{1,0:T(8,128)S(1)} %get-tuple-element.19, bf16[32]{0:T(256)(128)(2,1)S(1)} %slice_reduce_fusion, bf16[32,256,512]{2,1,0:T(8,128)(2,1)S(1)} %fusion.101), kind=kOutput, calls=%fused_computation.25 | convolution fusion | flops 4303355904 | bytes 9470016 | tf_op jit(solution)/shard_map/dot_general | solution.py:52
  79.2 0.0 copy-start.1
  79.2 1.3 %fusion.84 = (bf16[512,512]{1,0:T(8,128)(2,1)S(1)}, f32[512,512]{1,0:T(8,128)}) fusion(f32[512,512]{1,0:T(8,128)S(1)} %fusion.22, s32[32]{0:T(128)S(1)} %get-tuple-element.15, s32[32]{0:T(128)S(1)} %get-tuple-element.14, bf16[32]{0:T(256)(128)(2,1)S(1)} %slice_reduce_fusion), kind=kOutput, calls=%fused_computation.92 | convolution fusion | flops 17711104 | bytes 2621760 | tf_op jit(solution)/shard_map/dot_general | solution.py:63
  80.6 4.5 %collective-permute-start = (bf16[10,512]{1,0:T(8,128)(2,1)S(1)}, bf16[10,512]{1,0:T(8,128)(2,1)S(1)}, u32[]{:S(2)}, u32[]{:S(2)}) collective-permute-start(bf16[10,512]{1,0:T(8,128)(2,1)S(1)} %get-tuple-element.12), channel_id=1, source_target_pairs={{0,16},{16,32},{32,48},{48,64},{64,80},{80,96},{96,112},{1,17},{17... | collective-permute-start | bytes 30728 | tf_op jit(solution)/shard_map/ppermute | solution.py:111
  85.1 1.9 %collective-permute-start.1 = (bf16[10,512]{1,0:T(8,128)(2,1)S(1)}, bf16[10,512]{1,0:T(8,128)(2,1)S(1)}, u32[]{:S(2)}, u32[]{:S(2)}) collective-permute-start(bf16[10,512]{1,0:T(8,128)(2,1)S(1)} %get-tuple-element.13), channel_id=1, source_target_pairs={{16,0},{32,16},{48,32},{64,48},{80,64},{96,80},{112,96},{17,1},{33... | collective-permute-start | bytes 30728 | tf_op jit(solution)/shard_map/ppermute | solution.py:112
  87.0 0.0 copy-done.3
  87.0 0.8 fusion.31
  87.8 0.0 collective-permute-done
  87.8 2.3 %collective-permute-done.1 = bf16[10,512]{1,0:T(8,128)(2,1)S(1)} collective-permute-done((bf16[10,512]{1,0:T(8,128)(2,1)S(1)}, bf16[10,512]{1,0:T(8,128)(2,1)S(1)}, u32[]{:S(2)}, u32[]{:S(2)}) %collective-permute-start.1) | collective-permute-done | bytes 10272 | tf_op jit(solution)/shard_map/ppermute | solution.py:112
  90.1 0.0 copy-done.1
  90.1 0.3 fusion.29
  90.5 3.6 %collective-permute-start.2 = (bf16[10,512]{1,0:T(8,128)(2,1)S(1)}, bf16[10,512]{1,0:T(8,128)(2,1)S(1)}, u32[]{:S(2)}, u32[]{:S(2)}) collective-permute-start(bf16[10,512]{1,0:T(8,128)(2,1)S(1)} %get-tuple-element.10), channel_id=1, source_target_pairs={{0,1},{1,2},{2,3},{3,4},{4,5},{5,6},{6,7},{7,8},{8,9},{9,10},{10,1... | collective-permute-start | bytes 30728 | tf_op jit(solution)/shard_map/ppermute | solution.py:117
  94.1 1.9 %collective-permute-start.3 = (bf16[10,512]{1,0:T(8,128)(2,1)S(1)}, bf16[10,512]{1,0:T(8,128)(2,1)S(1)}, u32[]{:S(2)}, u32[]{:S(2)}) collective-permute-start(bf16[10,512]{1,0:T(8,128)(2,1)S(1)} %get-tuple-element.11), channel_id=1, source_target_pairs={{1,0},{2,1},{3,2},{4,3},{5,4},{6,5},{7,6},{8,7},{9,8},{10,9},{11,1... | collective-permute-start | bytes 30728 | tf_op jit(solution)/shard_map/ppermute | solution.py:118
  96.0 0.8 fusion.35
  96.7 0.0 collective-permute-done.2
  96.8 4.3 %collective-permute-done.3 = bf16[10,512]{1,0:T(8,128)(2,1)S(1)} collective-permute-done((bf16[10,512]{1,0:T(8,128)(2,1)S(1)}, bf16[10,512]{1,0:T(8,128)(2,1)S(1)}, u32[]{:S(2)}, u32[]{:S(2)}) %collective-permute-start.3) | collective-permute-done | bytes 10272 | tf_op jit(solution)/shard_map/ppermute | solution.py:118
  101.0 1.3 %convolution_add_fusion = f32[512,512]{1,0:T(8,128)} fusion(f32[512,512]{1,0:T(8,128)S(1)} %fusion.35, bf16[512,40]{1,0:T(8,128)(2,1)S(1)} %copy-done.1, bf16[10,512]{1,0:T(8,128)(2,1)S(1)} %collective-permute-done.3, bf16[10,512]{1,0:T(8,128)(2,1)S(1)} %collective-permute-done.2), kind=kOutput, calls=%fused_computation.21 | convolution fusion | flops 21397504 | bytes 2158592 | tf_op jit(solution)/shard_map/dot_general | solution.py:125
  (6 shorter events, 0.0 us)
Async XLA Ops:
  0.6 2.3 %copy-start = (bf16[1,8,256,256]{3,2,1,0:T(8,128)(2,1)S(1)}, bf16[1,8,256,256]{3,2,1,0:T(8,128)(2,1)}, u32[]{:S(2)}) copy-start(bf16[1,8,256,256]{3,2,1,0:T(8,128)(2,1)} %param.8) | copy-start | bytes 3145732
  11.4 58.5 %copy-start.2 = (s32[2,1,32]{2,1,0:T(1,128)S(1)}, s32[2,1,32]{2,1,0:T(1,128)}, u32[]{:S(2)}) copy-start(s32[2,1,32]{2,1,0:T(1,128)} %param.12) | copy-start | bytes 772
  74.7 12.3 %copy-start.3 = (bf16[512,1024]{1,0:T(8,128)(2,1)S(1)}, bf16[512,1024]{1,0:T(8,128)(2,1)}, u32[]{:S(2)}) copy-start(bf16[512,1024]{1,0:T(8,128)(2,1)} %constant.6.clone) | copy-start | bytes 3145732
  79.2 10.9 %copy-start.1 = (bf16[512,40]{1,0:T(8,128)(2,1)S(1)}, bf16[512,40]{1,0:T(8,128)(2,1)}, u32[]{:S(2)}) copy-start(bf16[512,40]{1,0:T(8,128)(2,1)} %constant.7.clone) | copy-start | bytes 122884
  80.6 7.2 %collective-permute-start = (bf16[10,512]{1,0:T(8,128)(2,1)S(1)}, bf16[10,512]{1,0:T(8,128)(2,1)S(1)}, u32[]{:S(2)}, u32[]{:S(2)}) collective-permute-start(bf16[10,512]{1,0:T(8,128)(2,1)S(1)} %get-tuple-element.12), channel_id=1, source_target_pairs={{0,16},{16,32},{32,48},{48,64},{64,80},{80,96},{96,112},{1,17},{17... | collective-permute-start | bytes 30728 | tf_op jit(solution)/shard_map/ppermute | solution.py:111
  85.1 5.1 %collective-permute-start.1 = (bf16[10,512]{1,0:T(8,128)(2,1)S(1)}, bf16[10,512]{1,0:T(8,128)(2,1)S(1)}, u32[]{:S(2)}, u32[]{:S(2)}) collective-permute-start(bf16[10,512]{1,0:T(8,128)(2,1)S(1)} %get-tuple-element.13), channel_id=1, source_target_pairs={{16,0},{32,16},{48,32},{64,48},{80,64},{96,80},{112,96},{17,1},{33... | collective-permute-start | bytes 30728 | tf_op jit(solution)/shard_map/ppermute | solution.py:112
  90.5 6.3 %collective-permute-start.2 = (bf16[10,512]{1,0:T(8,128)(2,1)S(1)}, bf16[10,512]{1,0:T(8,128)(2,1)S(1)}, u32[]{:S(2)}, u32[]{:S(2)}) collective-permute-start(bf16[10,512]{1,0:T(8,128)(2,1)S(1)} %get-tuple-element.10), channel_id=1, source_target_pairs={{0,1},{1,2},{2,3},{3,4},{4,5},{5,6},{6,7},{7,8},{8,9},{9,10},{10,1... | collective-permute-start | bytes 30728 | tf_op jit(solution)/shard_map/ppermute | solution.py:117
  94.1 7.0 %collective-permute-start.3 = (bf16[10,512]{1,0:T(8,128)(2,1)S(1)}, bf16[10,512]{1,0:T(8,128)(2,1)S(1)}, u32[]{:S(2)}, u32[]{:S(2)}) collective-permute-start(bf16[10,512]{1,0:T(8,128)(2,1)S(1)} %get-tuple-element.11), channel_id=1, source_target_pairs={{1,0},{2,1},{3,2},{4,3},{5,4},{6,5},{7,6},{8,7},{9,8},{10,9},{11,1... | collective-permute-start | bytes 30728 | tf_op jit(solution)/shard_map/ppermute | solution.py:118

commit v9 on v8

--- a/solution.py
+++ b/solution.py
@@ -4,7 +4,6 @@
 from jax import lax
 from jax.sharding import PartitionSpec as P
 
-NB = 5
 REACH = 10
 CAP = 2
 PATCH = 512
@@ -36,7 +35,7 @@
     return jnp.sum(coeffs.astype(jnp.float32) * horiz, axis=1).astype(jnp.bfloat16)
 
 
-def coadd_patch(matched, slot_weight, offsets, patch):
+def coadd_parts(matched, slot_weight, offsets, patch):
     slot_count = matched.shape[0]
     size = matched.shape[1]
     local = jnp.arange(size, dtype=jnp.int32)
@@ -49,34 +48,25 @@
     ).astype(jnp.bfloat16)
     zero_weight = jnp.zeros((), jnp.bfloat16)
     row_place = jnp.where(row_hit, slot_weight[None, :, None], zero_weight)
-    numer = jnp.dot(
-        row_place.reshape(patch, slot_count * size),
-        shifted.reshape(slot_count * size, patch),
-        preferred_element_type=jnp.float32,
-    )
     row_gap = pixel[:, None] - offsets[0][None, :]
     col_gap = pixel[None, :] - offsets[1][:, None]
     row_in = (row_gap >= 0) & (row_gap < size)
     col_in = (col_gap >= 0) & (col_gap < size)
     row_cover = jnp.where(row_in, slot_weight[None, :], zero_weight)
     col_cover = col_in.astype(jnp.bfloat16)
-    cover = jnp.dot(row_cover, col_cover, preferred_element_type=jnp.float32)
-    return numer / (1.0 + cover)
+    return (
+        row_place.reshape(patch, slot_count * size),
+        shifted.reshape(slot_count * size, patch),
+        row_cover,
+        col_cover,
+    )
 
 
-def split(x):
-    hi = lax.reduce_precision(x, exponent_bits=8, mantissa_bits=7)
-    return hi.astype(jnp.bfloat16), (x - hi).astype(jnp.bfloat16)
-
-
-def mm3(a, b, dims=(((1,), (0,)), ((), ()))):
-    ah, al = a
-    bh, bl = b
-
-    def one(x, y):
-        return lax.dot_general(x, y, dims, preferred_element_type=jnp.float32)
-
-    return one(ah, bh) + (one(al, bh) + one(ah, bl))
+def coadd_rows(parts, rows):
+    row_place, shifted, row_cover, col_cover = parts
+    numer = jnp.dot(row_place[rows], shifted, preferred_element_type=jnp.float32)
+    cover = jnp.dot(row_cover[rows], col_cover, preferred_element_type=jnp.float32)
+    return numer / (1.0 + cover)
 
 
 def detect_filters(patch):
@@ -97,19 +87,21 @@
     return jnp.asarray(mid), jnp.asarray(edge)
 
 
-def detect(coadd, mid, edge):
+def detect(parts, mid, edge, patch):
     ny = lax.axis_size("skyy")
     nx = lax.axis_size("skyx")
     r = REACH
-    patch = coadd.shape[0]
     down = [(i, i + 1) for i in range(ny - 1)]
     up = [(i + 1, i) for i in range(ny - 1)]
     right = [(j, j + 1) for j in range(nx - 1)]
     left = [(j + 1, j) for j in range(nx - 1)]
     f32 = jnp.float32
+    last = coadd_rows(parts, slice(patch - r, patch)).astype(jnp.bfloat16)
+    first = coadd_rows(parts, slice(0, r)).astype(jnp.bfloat16)
+    top = lax.ppermute(last, "skyy", down)
+    bottom = lax.ppermute(first, "skyy", up)
+    coadd = coadd_rows(parts, slice(0, patch))
     own = coadd.astype(jnp.bfloat16)
-    top = lax.ppermute(own[-r:, :], "skyy", down)
-    bottom = lax.ppermute(own[:r, :], "skyy", up)
     vert = jnp.dot(mid, jnp.concatenate([own, own], axis=0), preferred_element_type=f32)
     rim = jnp.concatenate([top, bottom, top, bottom], axis=0)
     vert = vert + jnp.dot(edge, rim, preferred_element_type=f32)
@@ -122,10 +114,10 @@
         jnp.concatenate([vown, vown], axis=1), mid, on_cols, preferred_element_type=f32
     )
     side = jnp.concatenate([west, east, west, east], axis=0)
-    return result + lax.dot_general(side, edge, by_rows, preferred_element_type=f32)
+    return coadd, result + lax.dot_general(side, edge, by_rows, preferred_element_type=f32)
 
 
-def body(tiles, coeffs, weights, tile_slot, slot_offset):
+def body_inner(tiles, coeffs, weights, tile_slot, slot_offset):
     count = tiles.shape[1]
     size = tiles.shape[2]
     columns = lax.axis_size("skyx")
@@ -156,8 +148,8 @@
     recv = recv.reshape(slots, size + extra, size)
     matched = recv[:, :size, :]
     recv_weight = recv[:, size, 0]
-    coadd = coadd_patch(matched, recv_weight, offsets, patch)
-    detection = detect(coadd, *filters)
+    parts = coadd_parts(matched, recv_weight, offsets, patch)
+    coadd, detection = detect(parts, *filters, patch)
     return (coadd, detection)
 
 
@@ -170,4 +162,4 @@
         P(None, "skyy", "skyx"),
     )
     out_specs = (P("skyy", "skyx"), P("skyy", "skyx"))
-    return jax.shard_map(body, mesh=mesh, in_specs=in_specs, out_specs=out_specs, check_vma=False)
+    return jax.shard_map(body_inner, mesh=mesh, in_specs=in_specs, out_specs=out_specs, check_vma=False)

time: 103 us -> 110 us (1.068)
  the two profiles are of different devices: /device:TPU:29 before, /device:TPU:36 now
where the time goes in v9:
time: 110 us; the launch traced here: 109 us
  blocking collectives  59.9 us (54%)
  matrix products  21.7 us (20%)
  starting transfers between devices  10.4 us (9%)
  waiting for transfers between devices  6.91 us (6%)
  other arithmetic  6.22 us (6%)
  local copies, waits for them, and re-layouts  3.31 us (3%)
    all_to_all x1, blocking collectives, body_inner(): recv = lax.all_to_all(send, 'skyx', split_axis=0, concat_axis=0, tiled=True)  59.9 us
    dot_general x3, matrix products, coadd_rows(): jnp.dot(row_place[rows], shifted, preferred_element_type=jnp.float32)  6.89 us
    dot_general x1, matrix products, match_all(): jnp.einsum('mbik,bjk->mbij', vert, basis, preferred_element_type=jnp.floa...  5.49 us
    ppermute x1, waiting for transfers between devices, detect(): west = lax.ppermute(vown[:, -r:].T, 'skyx', right)  5.05 us
    dot_general x1, matrix products, coadd_parts(): jnp.einsum('sij,sjq->siq', matched, col_place, preferred_element_type=jnp...  4.42 us
    ppermute x1, starting transfers between devices, detect(): east = lax.ppermute(vown[:, :r].T, 'skyx', left)  4.14 us
    select_n x1, other arithmetic, coadd_parts(): row_place = jnp.where(row_hit, slot_weight[None, :, None], zero_weight)  3.68 us
    gather x1, local copies, waits for them, and re-layouts, body_inner(): send = carry[which].reshape(columns, CAP, size + extra, size)  2.88 us
  transfers between devices with their start and end apart: 4, of which 2 were waited for; matrix products, arithmetic and copies ran while one was open for 2% of the time, Pallas kernels for 0%

profile of v9, /device:TPU:36, one launch (start us, length us, event | category | flops | bytes accessed | tf_op | source)
XLA Modules:
  0.0 109.3 jit_solution(3360837302871222440)
XLA Ops:
  0.6 0.0 copy-start
  0.7 0.8 fusion.62
  1.5 0.7 select_reduce_fusion
  2.2 0.7 broadcast_select_fusion
  3.0 0.0 copy-done
  3.0 5.5 %fusion.2 = bf16[8,256,256]{2,1,0:T(8,128)(2,1)S(1)} fusion(bf16[1,8,5,256,256]{4,3,2,1,0:T(8,128)(2,1)} %param.9, bf16[5,256,256,1]{2,1,3,0:T(8,128)(2,1)} %constant.39, bf16[1,8,256,256]{3,2,1,0:T(8,128)(2,1)S(1)} %copy-done), kind=kOutput, calls=%fused_computation.6 | convolution fusion | flops 2694316032 | bytes 7995392 | tf_op jit(solution)/shard_map/mbik,bjk->mbij/dot_general | solution.py:34
  8.5 0.1 mul.9
  8.6 0.1 fusion.17
  8.6 2.9 %gather_fusion = bf16[32,272,256]{2,1,0:T(8,128)(2,1)} fusion(bf16[9,272,256]{2,1,0:T(8,128)(2,1)S(1)} %fusion.17, s32[1024]{0:T(1024)S(1)} %pad_clamp_fusion), kind=kCustom, calls=%fused_computation | custom fusion | bytes 8913024 | tf_op jit(solution)/shard_map/gather | solution.py:144
  11.5 0.0 copy-start.2
  11.5 59.9 %all_to_all.5 = bf16[16,2,272,256]{3,2,1,0:T(8,128)(2,1)S(1)} all-to-all(bf16[16,2,272,256]{3,2,1,0:T(8,128)(2,1)} %bitcast.50), channel_id=1, replica_groups=mesh['skyy'=8,'skyx'=16] {'skyx'}, dimensions={0} | all-to-all | bytes 8912896 | tf_op jit(solution)/shard_map/all_to_all | solution.py:146
  71.5 0.0 copy-done.2
  71.5 0.3 slice_reduce_fusion
  71.8 0.1 iota_add_fusion
  71.9 4.4 %fusion.4 = bf16[32,256,512]{2,1,0:T(8,128)(2,1)S(1)} fusion(s32[32,256]{1,0:T(8,128)S(1)} %get-tuple-element.16, bf16[32,272,256]{2,1,0:T(8,128)(2,1)S(1)} %bitcast.52), kind=kOutput, calls=%fused_computation.8 | convolution fusion | flops 2155872256 | bytes 12615680 | tf_op jit(solution)/shard_map/sij,sjq->siq/dot_general | solution.py:46
  76.3 0.1 fusion.38
  76.4 3.7 %fusion = bf16[512,32,256]{2,0,1:T(8,128)(2,1)S(1)} fusion(s32[32,256]{1,0:T(8,128)S(1)} %get-tuple-element.17, bf16[32]{0:T(256)(128)(2,1)S(1)} %slice_reduce_fusion), kind=kLoop, calls=%fused_computation.3 | loop fusion | flops 8388608 | bytes 8421440 | tf_op jit(solution)/shard_map/jit(_where)/select_n | solution.py:50
  80.1 4.5 %convolution_bitcast_fusion = f32[512,512]{1,0:T(8,128)S(1)} fusion(bf16[32,256,512]{2,1,0:T(8,128)(2,1)S(1)} %fusion.4, s32[32,256]{1,0:T(8,128)S(1)} %get-tuple-element.17, bf16[32]{0:T(256)(128)(2,1)S(1)} %slice_reduce_fusion), kind=kOutput, calls=%fused_computation.21 | convolution fusion | flops 4303355904 | bytes 9470016 | tf_op jit(solution)/shard_map/dot_general | solution.py:67
  84.6 1.2 %convolution_bitcast_fusion.1 = f32[10,512]{1,0:T(8,128)S(1)} fusion(bf16[32,256,512]{2,1,0:T(8,128)(2,1)S(1)} %fusion.4, bf16[512,32,256]{2,0,1:T(8,128)(2,1)S(1)} %fusion), kind=kOutput, calls=%fused_computation.26 | convolution fusion | flops 83886080 | bytes 8671232 | tf_op jit(solution)/shard_map/dot_general | solution.py:67
  85.8 0.0 copy-start.3
  85.8 1.2 %convolution_bitcast_fusion.2 = f32[10,512]{1,0:T(8,128)S(1)} fusion(bf16[32,256,512]{2,1,0:T(8,128)(2,1)S(1)} %fusion.4, bf16[512,32,256]{2,0,1:T(8,128)(2,1)S(1)} %fusion), kind=kOutput, calls=%fused_computation.29 | convolution fusion | flops 83886080 | bytes 8671232 | tf_op jit(solution)/shard_map/dot_general | solution.py:67
  87.0 0.0 copy-start.1
  87.0 1.3 %fusion.76 = (bf16[512,512]{1,0:T(8,128)(2,1)S(1)}, f32[512,512]{1,0:T(8,128)}) fusion(f32[512,512]{1,0:T(8,128)S(1)} %convolution_bitcast_fusion, s32[32]{0:T(128)S(1)} %get-tuple-element.13, s32[32]{0:T(128)S(1)} %get-tuple-element.12, bf16[32]{0:T(256)(128)(2,1)S(1)} %slice_reduce_fusion), kind=kOutput, calls=%fused_computation.95 | convolution fusion | flops 17711104 | bytes 2621760 | tf_op jit(solution)/shard_map/dot_general | solution.py:68
  88.3 0.2 fusion.22
  88.5 1.9 %collective-permute-start.1 = (bf16[10,512]{1,0:T(8,128)(2,1)S(1)}, bf16[10,512]{1,0:T(8,128)(2,1)S(1)}, u32[]{:S(2)}, u32[]{:S(2)}) collective-permute-start(bf16[10,512]{1,0:T(8,128)(2,1)S(1)} %fusion.22), channel_id=1, source_target_pairs={{16,0},{32,16},{48,32},{64,48},{80,64},{96,80},{112,96},{17,1},{33... | collective-permute-start | bytes 30728 | tf_op jit(solution)/shard_map/ppermute | solution.py:102
  90.4 0.2 fusion.21
  90.7 2.4 %collective-permute-start = (bf16[10,512]{1,0:T(8,128)(2,1)S(1)}, bf16[10,512]{1,0:T(8,128)(2,1)S(1)}, u32[]{:S(2)}, u32[]{:S(2)}) collective-permute-start(bf16[10,512]{1,0:T(8,128)(2,1)S(1)} %fusion.21), channel_id=1, source_target_pairs={{0,16},{16,32},{32,48},{48,64},{64,80},{80,96},{96,112},{1,17},{17... | collective-permute-start | bytes 30728 | tf_op jit(solution)/shard_map/ppermute | solution.py:101
  93.1 0.0 copy-done.3
  93.1 0.8 fusion.23
  93.8 0.0 collective-permute-done.1
  93.9 1.9 %collective-permute-done = bf16[10,512]{1,0:T(8,128)(2,1)S(1)} collective-permute-done((bf16[10,512]{1,0:T(8,128)(2,1)S(1)}, bf16[10,512]{1,0:T(8,128)(2,1)S(1)}, u32[]{:S(2)}, u32[]{:S(2)}) %collective-permute-start) | collective-permute-done | bytes 10272 | tf_op jit(solution)/shard_map/ppermute | solution.py:101
  95.7 0.0 copy-done.1
  95.7 0.3 fusion.16
  96.1 4.1 %collective-permute-start.3 = (bf16[10,512]{1,0:T(8,128)(2,1)S(1)}, bf16[10,512]{1,0:T(8,128)(2,1)S(1)}, u32[]{:S(2)}, u32[]{:S(2)}) collective-permute-start(bf16[10,512]{1,0:T(8,128)(2,1)S(1)} %get-tuple-element.11), channel_id=1, source_target_pairs={{1,0},{2,1},{3,2},{4,3},{5,4},{6,5},{7,6},{8,7},{9,8},{10,9},{11,1... | collective-permute-start | bytes 30728 | tf_op jit(solution)/shard_map/ppermute | solution.py:110
  100.2 1.9 %collective-permute-start.2 = (bf16[10,512]{1,0:T(8,128)(2,1)S(1)}, bf16[10,512]{1,0:T(8,128)(2,1)S(1)}, u32[]{:S(2)}, u32[]{:S(2)}) collective-permute-start(bf16[10,512]{1,0:T(8,128)(2,1)S(1)} %get-tuple-element.10), channel_id=1, source_target_pairs={{0,1},{1,2},{2,3},{3,4},{4,5},{5,6},{6,7},{7,8},{8,9},{9,10},{10,1... | collective-permute-start | bytes 30728 | tf_op jit(solution)/shard_map/ppermute | solution.py:109
  102.2 0.8 fusion.27
  102.9 0.0 collective-permute-done.3
  102.9 5.0 %collective-permute-done.2 = bf16[10,512]{1,0:T(8,128)(2,1)S(1)} collective-permute-done((bf16[10,512]{1,0:T(8,128)(2,1)S(1)}, bf16[10,512]{1,0:T(8,128)(2,1)S(1)}, u32[]{:S(2)}, u32[]{:S(2)}) %collective-permute-start.2) | collective-permute-done | bytes 10272 | tf_op jit(solution)/shard_map/ppermute | solution.py:109
  108.0 1.3 %convolution_add_fusion = f32[512,512]{1,0:T(8,128)} fusion(f32[512,512]{1,0:T(8,128)S(1)} %fusion.27, bf16[512,40]{1,0:T(8,128)(2,1)S(1)} %copy-done.1, bf16[10,512]{1,0:T(8,128)(2,1)S(1)} %collective-permute-done.3, bf16[10,512]{1,0:T(8,128)(2,1)S(1)} %collective-permute-done.2), kind=kOutput, calls=%fused_computation.17 | convolution fusion | flops 21397504 | bytes 2158592 | tf_op jit(solution)/shard_map/dot_general | solution.py:117
  (5 shorter events, 0.0 us)
Async XLA Ops:
  0.6 2.3 %copy-start = (bf16[1,8,256,256]{3,2,1,0:T(8,128)(2,1)S(1)}, bf16[1,8,256,256]{3,2,1,0:T(8,128)(2,1)}, u32[]{:S(2)}) copy-start(bf16[1,8,256,256]{3,2,1,0:T(8,128)(2,1)} %param.8) | copy-start | bytes 3145732
  11.5 59.9 %copy-start.2 = (s32[2,1,32]{2,1,0:T(1,128)S(1)}, s32[2,1,32]{2,1,0:T(1,128)}, u32[]{:S(2)}) copy-start(s32[2,1,32]{2,1,0:T(1,128)} %param.12) | copy-start | bytes 772
  85.8 7.3 %copy-start.3 = (bf16[512,1024]{1,0:T(8,128)(2,1)S(1)}, bf16[512,1024]{1,0:T(8,128)(2,1)}, u32[]{:S(2)}) copy-start(bf16[512,1024]{1,0:T(8,128)(2,1)} %constant.5.clone) | copy-start | bytes 3145732
  87.0 8.8 %copy-start.1 = (bf16[512,40]{1,0:T(8,128)(2,1)S(1)}, bf16[512,40]{1,0:T(8,128)(2,1)}, u32[]{:S(2)}) copy-start(bf16[512,40]{1,0:T(8,128)(2,1)} %constant.6.clone) | copy-start | bytes 122884
  88.5 5.3 %collective-permute-start.1 = (bf16[10,512]{1,0:T(8,128)(2,1)S(1)}, bf16[10,512]{1,0:T(8,128)(2,1)S(1)}, u32[]{:S(2)}, u32[]{:S(2)}) collective-permute-start(bf16[10,512]{1,0:T(8,128)(2,1)S(1)} %fusion.22), channel_id=1, source_target_pairs={{16,0},{32,16},{48,32},{64,48},{80,64},{96,80},{112,96},{17,1},{33... | collective-permute-start | bytes 30728 | tf_op jit(solution)/shard_map/ppermute | solution.py:102
  90.7 5.1 %collective-permute-start = (bf16[10,512]{1,0:T(8,128)(2,1)S(1)}, bf16[10,512]{1,0:T(8,128)(2,1)S(1)}, u32[]{:S(2)}, u32[]{:S(2)}) collective-permute-start(bf16[10,512]{1,0:T(8,128)(2,1)S(1)} %fusion.21), channel_id=1, source_target_pairs={{0,16},{16,32},{32,48},{48,64},{64,80},{80,96},{96,112},{1,17},{17... | collective-permute-start | bytes 30728 | tf_op jit(solution)/shard_map/ppermute | solution.py:101
  96.1 6.8 %collective-permute-start.3 = (bf16[10,512]{1,0:T(8,128)(2,1)S(1)}, bf16[10,512]{1,0:T(8,128)(2,1)S(1)}, u32[]{:S(2)}, u32[]{:S(2)}) collective-permute-start(bf16[10,512]{1,0:T(8,128)(2,1)S(1)} %get-tuple-element.11), channel_id=1, source_target_pairs={{1,0},{2,1},{3,2},{4,3},{5,4},{6,5},{7,6},{8,7},{9,8},{10,9},{11,1... | collective-permute-start | bytes 30728 | tf_op jit(solution)/shard_map/ppermute | solution.py:110
  100.2 7.7 %collective-permute-start.2 = (bf16[10,512]{1,0:T(8,128)(2,1)S(1)}, bf16[10,512]{1,0:T(8,128)(2,1)S(1)}, u32[]{:S(2)}, u32[]{:S(2)}) collective-permute-start(bf16[10,512]{1,0:T(8,128)(2,1)S(1)} %get-tuple-element.10), channel_id=1, source_target_pairs={{0,1},{1,2},{2,3},{3,4},{4,5},{5,6},{6,7},{7,8},{8,9},{9,10},{10,1... | collective-permute-start | bytes 30728 | tf_op jit(solution)/shard_map/ppermute | solution.py:109

commit v10 on v8

--- a/solution.py
+++ b/solution.py
@@ -4,7 +4,6 @@
 from jax import lax
 from jax.sharding import PartitionSpec as P
 
-NB = 5
 REACH = 10
 CAP = 2
 PATCH = 512
@@ -64,21 +63,6 @@
     return numer / (1.0 + cover)
 
 
-def split(x):
-    hi = lax.reduce_precision(x, exponent_bits=8, mantissa_bits=7)
-    return hi.astype(jnp.bfloat16), (x - hi).astype(jnp.bfloat16)
-
-
-def mm3(a, b, dims=(((1,), (0,)), ((), ()))):
-    ah, al = a
-    bh, bl = b
-
-    def one(x, y):
-        return lax.dot_general(x, y, dims, preferred_element_type=jnp.float32)
-
-    return one(ah, bh) + (one(al, bh) + one(ah, bl))
-
-
 def detect_filters(patch):
     r = REACH
     taps = np.arange(-r, r + 1).astype(np.float32)
@@ -101,7 +85,6 @@
     ny = lax.axis_size("skyy")
     nx = lax.axis_size("skyx")
     r = REACH
-    patch = coadd.shape[0]
     down = [(i, i + 1) for i in range(ny - 1)]
     up = [(i + 1, i) for i in range(ny - 1)]
     right = [(j, j + 1) for j in range(nx - 1)]
@@ -110,9 +93,10 @@
     own = coadd.astype(jnp.bfloat16)
     top = lax.ppermute(own[-r:, :], "skyy", down)
     bottom = lax.ppermute(own[:r, :], "skyy", up)
-    vert = jnp.dot(mid, jnp.concatenate([own, own], axis=0), preferred_element_type=f32)
+    inner = jnp.dot(mid, jnp.concatenate([own, own], axis=0), preferred_element_type=f32)
+    inner = lax.optimization_barrier(inner)
     rim = jnp.concatenate([top, bottom, top, bottom], axis=0)
-    vert = vert + jnp.dot(edge, rim, preferred_element_type=f32)
+    vert = inner + jnp.dot(edge, rim, preferred_element_type=f32)
     vown = vert.astype(jnp.bfloat16)
     west = lax.ppermute(vown[:, -r:].T, "skyx", right)
     east = lax.ppermute(vown[:, :r].T, "skyx", left)
@@ -121,11 +105,12 @@
     result = lax.dot_general(
         jnp.concatenate([vown, vown], axis=1), mid, on_cols, preferred_element_type=f32
     )
+    result = lax.optimization_barrier(result)
     side = jnp.concatenate([west, east, west, east], axis=0)
     return result + lax.dot_general(side, edge, by_rows, preferred_element_type=f32)
 
 
-def body(tiles, coeffs, weights, tile_slot, slot_offset):
+def body_inner(tiles, coeffs, weights, tile_slot, slot_offset):
     count = tiles.shape[1]
     size = tiles.shape[2]
     columns = lax.axis_size("skyx")
@@ -170,4 +155,4 @@
         P(None, "skyy", "skyx"),
     )
     out_specs = (P("skyy", "skyx"), P("skyy", "skyx"))
-    return jax.shard_map(body, mesh=mesh, in_specs=in_specs, out_specs=out_specs, check_vma=False)
+    return jax.shard_map(body_inner, mesh=mesh, in_specs=in_specs, out_specs=out_specs, check_vma=False)

time: 103 us -> 105 us (1.019)
  waiting for transfers between devices: 6.61 us -> 9.05 us
    ppermute x1, waiting for transfers between devices: 4.26 us -> 6.06 us  [detect(): east = lax.ppermute(vown[:, :r].T, 'skyx', left)]
  transfers between devices with their start and end apart: 4 -> 4, of which waited for: 2 -> 3; matrix products, arithmetic and copies ran while one was open for 1% -> 1% of each run, Pallas kernels for 0% -> 0%
where the time goes in v10:
time: 105 us
  blocking collectives  58.5 us (56%)
  matrix products  18.7 us (18%)
  starting transfers between devices  11.9 us (11%)
  waiting for transfers between devices  9.05 us (9%)
  local copies, waits for them, and re-layouts  3.63 us (3%)
  other arithmetic  2.47 us (2%)
    all_to_all x1, blocking collectives, body_inner(): recv = lax.all_to_all(send, 'skyx', split_axis=0, concat_axis=0, tiled=True)  58.5 us
    ppermute x1, waiting for transfers between devices, detect(): east = lax.ppermute(vown[:, :r].T, 'skyx', left)  6.06 us
    dot_general x1, matrix products, match_all(): jnp.einsum('mbik,bjk->mbij', vert, basis, preferred_element_type=jnp.floa...  5.39 us
    dot_general x1, matrix products, coadd_patch(): jnp.dot(row_place.reshape(patch, slot_count * size), shifted.reshape(slot...  4.51 us
    ppermute x1, starting transfers between devices, detect(): top = lax.ppermute(own[-r:, :], 'skyy', down)  4.48 us
    dot_general x1, matrix products, coadd_patch(): jnp.einsum('sij,sjq->siq', matched, col_place, preferred_element_type=jnp...  4.39 us
    ppermute x1, starting transfers between devices, detect(): west = lax.ppermute(vown[:, -r:].T, 'skyx', right)  3.55 us
    gather x1, local copies, waits for them, and re-layouts, body_inner(): send = carry[which].reshape(columns, CAP, size + extra, size)  2.87 us
  transfers between devices with their start and end apart: 4, of which 3 were waited for; matrix products, arithmetic and copies ran while one was open for 1% of the time, Pallas kernels for 0%

profile of v10, /device:TPU:29, one launch (start us, length us, event | category | flops | bytes accessed | tf_op | source)
XLA Modules:
  0.0 104.9 jit_solution(11317821497046720582)
XLA Ops:
  0.6 0.0 copy-start
  0.6 0.8 fusion.73
  1.5 0.7 select_reduce_fusion
  2.2 0.7 broadcast_select_fusion
  3.0 0.0 copy-done
  3.0 5.4 %fusion.2 = bf16[8,256,256]{2,1,0:T(8,128)(2,1)S(1)} fusion(bf16[1,8,5,256,256]{4,3,2,1,0:T(8,128)(2,1)} %param.9, bf16[5,256,256,1]{2,1,3,0:T(8,128)(2,1)} %constant.38, bf16[1,8,256,256]{3,2,1,0:T(8,128)(2,1)S(1)} %copy-done), kind=kOutput, calls=%fused_computation.6 | convolution fusion | flops 2694316032 | bytes 7995392 | tf_op jit(solution)/shard_map/mbik,bjk->mbij/dot_general | solution.py:34
  8.4 0.1 mul.9
  8.5 0.1 fusion.30
  8.6 2.9 %gather_fusion = bf16[32,272,256]{2,1,0:T(8,128)(2,1)} fusion(bf16[9,272,256]{2,1,0:T(8,128)(2,1)S(1)} %fusion.30, s32[1024]{0:T(1024)S(1)} %pad_clamp_fusion), kind=kCustom, calls=%fused_computation | custom fusion | bytes 8913024 | tf_op jit(solution)/shard_map/gather | solution.py:137
  11.4 0.0 copy-start.2
  11.4 58.5 %all_to_all.5 = bf16[16,2,272,256]{3,2,1,0:T(8,128)(2,1)S(1)} all-to-all(bf16[16,2,272,256]{3,2,1,0:T(8,128)(2,1)} %bitcast.46), channel_id=1, replica_groups=mesh['skyy'=8,'skyx'=16] {'skyx'}, dimensions={0} | all-to-all | bytes 8912896 | tf_op jit(solution)/shard_map/all_to_all | solution.py:139
  69.9 0.0 copy-done.2
  69.9 0.3 slice_reduce_fusion
  70.2 0.1 iota_add_fusion
  70.3 4.4 %fusion.101 = bf16[32,256,512]{2,1,0:T(8,128)(2,1)S(1)} fusion(s32[32,256]{1,0:T(8,128)S(1)} %get-tuple-element.18, bf16[32,272,256]{2,1,0:T(8,128)(2,1)S(1)} %bitcast.48), kind=kOutput, calls=%fused_computation.8.clone.clone.clone.2 | convolution fusion | flops 2155872256 | bytes 12615680 | tf_op jit(solution)/shard_map/sij,sjq->siq/dot_general | solution.py:46
  74.7 0.0 copy-start.3
  74.7 4.5 %fusion.22 = f32[512,512]{1,0:T(8,128)S(1)} fusion(s32[32,256]{1,0:T(8,128)S(1)} %get-tuple-element.19, bf16[32]{0:T(256)(128)(2,1)S(1)} %slice_reduce_fusion, bf16[32,256,512]{2,1,0:T(8,128)(2,1)S(1)} %fusion.101), kind=kOutput, calls=%fused_computation.25 | convolution fusion | flops 4303355904 | bytes 9470016 | tf_op jit(solution)/shard_map/dot_general | solution.py:51
  79.2 0.0 copy-start.1
  79.2 1.3 %fusion.84 = (bf16[512,512]{1,0:T(8,128)(2,1)S(1)}, f32[512,512]{1,0:T(8,128)}) fusion(f32[512,512]{1,0:T(8,128)S(1)} %fusion.22, s32[32]{0:T(128)S(1)} %get-tuple-element.15, s32[32]{0:T(128)S(1)} %get-tuple-element.14, bf16[32]{0:T(256)(128)(2,1)S(1)} %slice_reduce_fusion), kind=kOutput, calls=%fused_computation.92 | convolution fusion | flops 17711104 | bytes 2621760 | tf_op jit(solution)/shard_map/dot_general | solution.py:62
  80.6 4.5 %collective-permute-start = (bf16[10,512]{1,0:T(8,128)(2,1)S(1)}, bf16[10,512]{1,0:T(8,128)(2,1)S(1)}, u32[]{:S(2)}, u32[]{:S(2)}) collective-permute-start(bf16[10,512]{1,0:T(8,128)(2,1)S(1)} %get-tuple-element.12), channel_id=1, source_target_pairs={{0,16},{16,32},{32,48},{48,64},{64,80},{80,96},{96,112},{1,17},{17... | collective-permute-start | bytes 30728 | tf_op jit(solution)/shard_map/ppermute | solution.py:94
  85.1 1.9 %collective-permute-start.1 = (bf16[10,512]{1,0:T(8,128)(2,1)S(1)}, bf16[10,512]{1,0:T(8,128)(2,1)S(1)}, u32[]{:S(2)}, u32[]{:S(2)}) collective-permute-start(bf16[10,512]{1,0:T(8,128)(2,1)S(1)} %get-tuple-element.13), channel_id=1, source_target_pairs={{16,0},{32,16},{48,32},{64,48},{80,64},{96,80},{112,96},{17,1},{33... | collective-permute-start | bytes 30728 | tf_op jit(solution)/shard_map/ppermute | solution.py:95
  87.0 0.0 copy-done.3
  87.0 0.7 fusion.31
  87.7 0.0 collective-permute-done
  87.7 2.4 %collective-permute-done.1 = bf16[10,512]{1,0:T(8,128)(2,1)S(1)} collective-permute-done((bf16[10,512]{1,0:T(8,128)(2,1)S(1)}, bf16[10,512]{1,0:T(8,128)(2,1)S(1)}, u32[]{:S(2)}, u32[]{:S(2)}) %collective-permute-start.1) | collective-permute-done | bytes 10272 | tf_op jit(solution)/shard_map/ppermute | solution.py:95
  90.1 0.0 copy-done.1
  90.1 0.3 fusion.29
  90.4 0.1 slice_bitcast_fusion.1
  90.5 3.5 %collective-permute-start.2 = (bf16[10,512]{0,1:T(8,128)(2,1)S(1)}, bf16[10,512]{0,1:T(8,128)(2,1)S(1)}, u32[]{:S(2)}, u32[]{:S(2)}) collective-permute-start(bf16[10,512]{0,1:T(8,128)(2,1)S(1)} %get-tuple-element.10), channel_id=1, source_target_pairs={{0,1},{1,2},{2,3},{3,4},{4,5},{5,6},{6,7},{7,8},{8,9},{9,10},{10,1... | collective-permute-start | bytes 30728 | tf_op jit(solution)/shard_map/ppermute | solution.py:101
  94.1 1.9 %collective-permute-start.3 = (bf16[10,512]{0,1:T(8,128)(2,1)S(1)}, bf16[10,512]{0,1:T(8,128)(2,1)S(1)}, u32[]{:S(2)}, u32[]{:S(2)}) collective-permute-start(bf16[10,512]{0,1:T(8,128)(2,1)S(1)} %get-tuple-element.11), channel_id=1, source_target_pairs={{1,0},{2,1},{3,2},{4,3},{5,4},{6,5},{7,6},{8,7},{9,8},{10,9},{11,1... | collective-permute-start | bytes 30728 | tf_op jit(solution)/shard_map/ppermute | solution.py:102
  96.0 0.7 fusion.35
  96.8 0.6 collective-permute-done.2
  97.3 0.1 copy.24
  97.5 6.1 %collective-permute-done.3 = bf16[10,512]{0,1:T(8,128)(2,1)S(1)} collective-permute-done((bf16[10,512]{0,1:T(8,128)(2,1)S(1)}, bf16[10,512]{0,1:T(8,128)(2,1)S(1)}, u32[]{:S(2)}, u32[]{:S(2)}) %collective-permute-start.3) | collective-permute-done | bytes 10272 | tf_op jit(solution)/shard_map/ppermute | solution.py:102
  103.5 0.1 copy.25
  103.6 1.3 %convolution_add_fusion = f32[512,512]{1,0:T(8,128)} fusion(f32[512,512]{1,0:T(8,128)S(1)} %fusion.35, bf16[512,40]{1,0:T(8,128)(2,1)S(1)} %copy-done.1, bf16[10,512]{1,0:T(8,128)(2,1)S(1)} %copy.25, bf16[10,512]{1,0:T(8,128)(2,1)S(1)} %copy.24), kind=kOutput, calls=%fused_computation.21 | convolution fusion | flops 21397504 | bytes 2158592 | tf_op jit(solution)/shard_map/dot_general | solution.py:110
  (5 shorter events, 0.0 us)
Async XLA Ops:
  0.6 2.3 %copy-start = (bf16[1,8,256,256]{3,2,1,0:T(8,128)(2,1)S(1)}, bf16[1,8,256,256]{3,2,1,0:T(8,128)(2,1)}, u32[]{:S(2)}) copy-start(bf16[1,8,256,256]{3,2,1,0:T(8,128)(2,1)} %param.8) | copy-start | bytes 3145732
  11.4 58.5 %copy-start.2 = (s32[2,1,32]{2,1,0:T(1,128)S(1)}, s32[2,1,32]{2,1,0:T(1,128)}, u32[]{:S(2)}) copy-start(s32[2,1,32]{2,1,0:T(1,128)} %param.12) | copy-start | bytes 772
  74.7 12.3 %copy-start.3 = (bf16[512,1024]{1,0:T(8,128)(2,1)S(1)}, bf16[512,1024]{1,0:T(8,128)(2,1)}, u32[]{:S(2)}) copy-start(bf16[512,1024]{1,0:T(8,128)(2,1)} %constant.6.clone) | copy-start | bytes 3145732
  79.2 10.9 %copy-start.1 = (bf16[512,40]{1,0:T(8,128)(2,1)S(1)}, bf16[512,40]{1,0:T(8,128)(2,1)}, u32[]{:S(2)}) copy-start(bf16[512,40]{1,0:T(8,128)(2,1)} %constant.7.clone) | copy-start | bytes 122884
  80.6 7.1 %collective-permute-start = (bf16[10,512]{1,0:T(8,128)(2,1)S(1)}, bf16[10,512]{1,0:T(8,128)(2,1)S(1)}, u32[]{:S(2)}, u32[]{:S(2)}) collective-permute-start(bf16[10,512]{1,0:T(8,128)(2,1)S(1)} %get-tuple-element.12), channel_id=1, source_target_pairs={{0,16},{16,32},{32,48},{48,64},{64,80},{80,96},{96,112},{1,17},{17... | collective-permute-start | bytes 30728 | tf_op jit(solution)/shard_map/ppermute | solution.py:94
  85.1 5.1 %collective-permute-start.1 = (bf16[10,512]{1,0:T(8,128)(2,1)S(1)}, bf16[10,512]{1,0:T(8,128)(2,1)S(1)}, u32[]{:S(2)}, u32[]{:S(2)}) collective-permute-start(bf16[10,512]{1,0:T(8,128)(2,1)S(1)} %get-tuple-element.13), channel_id=1, source_target_pairs={{16,0},{32,16},{48,32},{64,48},{80,64},{96,80},{112,96},{17,1},{33... | collective-permute-start | bytes 30728 | tf_op jit(solution)/shard_map/ppermute | solution.py:95
  90.5 6.8 %collective-permute-start.2 = (bf16[10,512]{0,1:T(8,128)(2,1)S(1)}, bf16[10,512]{0,1:T(8,128)(2,1)S(1)}, u32[]{:S(2)}, u32[]{:S(2)}) collective-permute-start(bf16[10,512]{0,1:T(8,128)(2,1)S(1)} %get-tuple-element.10), channel_id=1, source_target_pairs={{0,1},{1,2},{2,3},{3,4},{4,5},{5,6},{6,7},{7,8},{8,9},{9,10},{10,1... | collective-permute-start | bytes 30728 | tf_op jit(solution)/shard_map/ppermute | solution.py:101
  94.1 9.4 %collective-permute-start.3 = (bf16[10,512]{0,1:T(8,128)(2,1)S(1)}, bf16[10,512]{0,1:T(8,128)(2,1)S(1)}, u32[]{:S(2)}, u32[]{:S(2)}) collective-permute-start(bf16[10,512]{0,1:T(8,128)(2,1)S(1)} %get-tuple-element.11), channel_id=1, source_target_pairs={{1,0},{2,1},{3,2},{4,3},{5,4},{6,5},{7,6},{8,7},{9,8},{10,9},{11,1... | collective-permute-start | bytes 30728 | tf_op jit(solution)/shard_map/ppermute | solution.py:102

commit v11 on v8

--- a/solution.py
+++ b/solution.py
@@ -108,21 +108,21 @@
     left = [(j + 1, j) for j in range(nx - 1)]
     f32 = jnp.float32
     own = coadd.astype(jnp.bfloat16)
-    top = lax.ppermute(own[-r:, :], "skyy", down)
-    bottom = lax.ppermute(own[:r, :], "skyy", up)
-    vert = jnp.dot(mid, jnp.concatenate([own, own], axis=0), preferred_element_type=f32)
-    rim = jnp.concatenate([top, bottom, top, bottom], axis=0)
-    vert = vert + jnp.dot(edge, rim, preferred_element_type=f32)
-    vown = vert.astype(jnp.bfloat16)
-    west = lax.ppermute(vown[:, -r:].T, "skyx", right)
-    east = lax.ppermute(vown[:, :r].T, "skyx", left)
+    west = lax.ppermute(own[:, -r:].T, "skyx", right)
+    east = lax.ppermute(own[:, :r].T, "skyx", left)
     on_cols = (((1,), (1,)), ((), ()))
     by_rows = (((0,), (1,)), ((), ()))
-    result = lax.dot_general(
-        jnp.concatenate([vown, vown], axis=1), mid, on_cols, preferred_element_type=f32
+    horiz = lax.dot_general(
+        jnp.concatenate([own, own], axis=1), mid, on_cols, preferred_element_type=f32
     )
     side = jnp.concatenate([west, east, west, east], axis=0)
-    return result + lax.dot_general(side, edge, by_rows, preferred_element_type=f32)
+    horiz = horiz + lax.dot_general(side, edge, by_rows, preferred_element_type=f32)
+    hown = horiz.astype(jnp.bfloat16)
+    top = lax.ppermute(hown[-r:, :], "skyy", down)
+    bottom = lax.ppermute(hown[:r, :], "skyy", up)
+    result = jnp.dot(mid, jnp.concatenate([hown, hown], axis=0), preferred_element_type=f32)
+    rim = jnp.concatenate([top, bottom, top, bottom], axis=0)
+    return result + jnp.dot(edge, rim, preferred_element_type=f32)
 
 
 def body(tiles, coeffs, weights, tile_slot, slot_offset):

time: 103 us -> 105 us (1.019)
  waiting for transfers between devices: 6.61 us -> 3.25 us
  matrix products: 18.8 us -> 21.3 us
  starting transfers between devices: 11.9 us -> 13.8 us
  local copies, waits for them, and re-layouts: 3.32 us -> 4.63 us
    ppermute x4, waiting for transfers between devices: 6.61 us -> 3.25 us  [the longest x1 2.06 us: detect(): east = lax.ppermute(own[:, :r].T, 'skyx', left)]
    dot_general x1, matrix products: 4.51 us -> 6.85 us  [coadd_patch(): jnp.dot(row_place.reshape(patch, slot_count * size), shifted.reshape(slot...]
    dot_general x3, matrix products: 1.85 us -> 3.95 us  [the longest x1 1.93 us: detect(): jnp.dot(mid, jnp.concatenate([hown, hown], axis=0), preferred_element_typ...]
    ppermute x4, starting transfers between devices: 11.9 us -> 13.8 us  [the longest x1 6.63 us: detect(): top = lax.ppermute(hown[-r:, :], 'skyy', down)]
    unnamed x8 -> x9, local copies, waits for them, and re-layouts: 0.03 us -> 1.33 us
  transfers between devices with their start and end apart: 4 -> 4, of which waited for: 2 -> 2; matrix products, arithmetic and copies ran while one was open for 1% -> 4% of each run, Pallas kernels for 0% -> 0%
where the time goes in v11:
time: 105 us
  blocking collectives  58.5 us (56%)
  matrix products  21.3 us (20%)
  starting transfers between devices  13.8 us (13%)
  local copies, waits for them, and re-layouts  4.63 us (4%)
  waiting for transfers between devices  3.25 us (3%)
  other arithmetic  2.47 us (2%)
    all_to_all x1, blocking collectives, body(): recv = lax.all_to_all(send, 'skyx', split_axis=0, concat_axis=0, tiled=True)  58.5 us
    dot_general x1, matrix products, coadd_patch(): jnp.dot(row_place.reshape(patch, slot_count * size), shifted.reshape(slot...  6.85 us
    ppermute x1, starting transfers between devices, detect(): top = lax.ppermute(hown[-r:, :], 'skyy', down)  6.63 us
    dot_general x1, matrix products, match_all(): jnp.einsum('mbik,bjk->mbij', vert, basis, preferred_element_type=jnp.floa...  5.39 us
    dot_general x1, matrix products, coadd_patch(): jnp.einsum('sij,sjq->siq', matched, col_place, preferred_element_type=jnp...  4.39 us
    gather x1, local copies, waits for them, and re-layouts, body(): send = carry[which].reshape(columns, CAP, size + extra, size)  2.87 us
    ppermute x1, starting transfers between devices, detect(): west = lax.ppermute(own[:, -r:].T, 'skyx', right)  2.84 us
    ppermute x1, starting transfers between devices, detect(): east = lax.ppermute(own[:, :r].T, 'skyx', left)  2.45 us
  transfers between devices with their start and end apart: 4, of which 2 were waited for; matrix products, arithmetic and copies ran while one was open for 4% of the time, Pallas kernels for 0%

profile of v11, /device:TPU:29, one launch (start us, length us, event | category | flops | bytes accessed | tf_op | source)
XLA Modules:
  0.0 104.8 jit_solution(13462213434644920323)
XLA Ops:
  0.6 0.0 copy-start
  0.6 0.8 fusion.73
  1.5 0.7 select_reduce_fusion
  2.2 0.7 broadcast_select_fusion
  3.0 0.0 copy-done
  3.0 5.4 %fusion.2 = bf16[8,256,256]{2,1,0:T(8,128)(2,1)S(1)} fusion(bf16[1,8,5,256,256]{4,3,2,1,0:T(8,128)(2,1)} %param.9, bf16[5,256,256,1]{2,1,3,0:T(8,128)(2,1)} %constant.38, bf16[1,8,256,256]{3,2,1,0:T(8,128)(2,1)S(1)} %copy-done), kind=kOutput, calls=%fused_computation.6 | convolution fusion | flops 2694316032 | bytes 7995392 | tf_op jit(solution)/shard_map/mbik,bjk->mbij/dot_general | solution.py:35
  8.4 0.1 mul.9
  8.5 0.1 fusion.30
  8.6 2.9 %gather_fusion = bf16[32,272,256]{2,1,0:T(8,128)(2,1)} fusion(bf16[9,272,256]{2,1,0:T(8,128)(2,1)S(1)} %fusion.30, s32[1024]{0:T(1024)S(1)} %pad_clamp_fusion), kind=kCustom, calls=%fused_computation | custom fusion | bytes 8913024 | tf_op jit(solution)/shard_map/gather | solution.py:152
  11.4 0.0 copy-start.2
  11.4 58.5 %all_to_all.5 = bf16[16,2,272,256]{3,2,1,0:T(8,128)(2,1)S(1)} all-to-all(bf16[16,2,272,256]{3,2,1,0:T(8,128)(2,1)} %bitcast.46), channel_id=1, replica_groups=mesh['skyy'=8,'skyx'=16] {'skyx'}, dimensions={0} | all-to-all | bytes 8912896 | tf_op jit(solution)/shard_map/all_to_all | solution.py:154
  69.9 0.0 copy-done.2
  69.9 0.3 slice_reduce_fusion
  70.2 0.1 iota_add_fusion
  70.3 4.4 %fusion.101 = bf16[32,256,512]{2,1,0:T(8,128)(2,1)S(1)} fusion(s32[32,256]{1,0:T(8,128)S(1)} %get-tuple-element.26, bf16[32,272,256]{2,1,0:T(8,128)(2,1)S(1)} %bitcast.48), kind=kOutput, calls=%fused_computation.8.clone.clone.clone.2 | convolution fusion | flops 2155872256 | bytes 12615680 | tf_op jit(solution)/shard_map/sij,sjq->siq/dot_general | solution.py:47
  74.7 0.0 copy-start.3
  74.7 6.8 %fusion.21 = f32[512,512]{0,1:T(8,128)S(1)} fusion(s32[32,256]{1,0:T(8,128)S(1)} %get-tuple-element.27, bf16[32]{0:T(256)(128)(2,1)S(1)} %slice_reduce_fusion, bf16[32,256,512]{2,1,0:T(8,128)(2,1)S(1)} %fusion.101), kind=kOutput, calls=%fused_computation.21 | convolution fusion | flops 4303355904 | bytes 9470016 | tf_op jit(solution)/shard_map/dot_general | solution.py:52
  81.6 0.0 copy-start.1
  81.6 0.4 fusion.84
  82.0 2.8 %collective-permute-start = (bf16[10,512]{1,0:T(8,128)(2,1)S(1)}, bf16[10,512]{1,0:T(8,128)(2,1)S(1)}, u32[]{:S(2)}, u32[]{:S(2)}) collective-permute-start(bf16[10,512]{1,0:T(8,128)(2,1)S(1)} %get-tuple-element.20), channel_id=1, source_target_pairs={{0,1},{1,2},{2,3},{3,4},{4,5},{5,6},{6,7},{7,8},{8,9},{9,10},{10,1... | collective-permute-start | bytes 30728 | tf_op jit(solution)/shard_map/ppermute | solution.py:111
  84.9 2.4 %collective-permute-start.1 = (bf16[10,512]{1,0:T(8,128)(2,1)S(1)}, bf16[10,512]{1,0:T(8,128)(2,1)S(1)}, u32[]{:S(2)}, u32[]{:S(2)}) collective-permute-start(bf16[10,512]{1,0:T(8,128)(2,1)S(1)} %get-tuple-element.21), channel_id=1, source_target_pairs={{1,0},{2,1},{3,2},{4,3},{5,4},{6,5},{7,6},{8,7},{9,8},{10,9},{11,1... | collective-permute-start | bytes 30728 | tf_op jit(solution)/shard_map/ppermute | solution.py:112
  87.3 0.0 copy-done.3
  87.3 0.8 fusion.31
  88.1 1.3 %copy.19 = f32[512,512]{1,0:T(8,128)} copy(f32[512,512]{0,1:T(8,128)S(1)} %get-tuple-element.25) | data formatting | bytes 2097152
  89.4 0.0 collective-permute-done
  89.4 2.1 %collective-permute-done.1 = bf16[10,512]{1,0:T(8,128)(2,1)S(1)} collective-permute-done((bf16[10,512]{1,0:T(8,128)(2,1)S(1)}, bf16[10,512]{1,0:T(8,128)(2,1)S(1)}, u32[]{:S(2)}, u32[]{:S(2)}) %collective-permute-start.1) | collective-permute-done | bytes 10272 | tf_op jit(solution)/shard_map/ppermute | solution.py:112
  91.5 0.0 copy-done.1
  91.5 0.3 fusion.29
  91.8 6.6 %collective-permute-start.2 = (bf16[10,512]{1,0:T(8,128)(2,1)S(1)}, bf16[10,512]{1,0:T(8,128)(2,1)S(1)}, u32[]{:S(2)}, u32[]{:S(2)}) collective-permute-start(bf16[10,512]{1,0:T(8,128)(2,1)S(1)} %get-tuple-element.18), channel_id=1, source_target_pairs={{0,16},{16,32},{32,48},{48,64},{64,80},{80,96},{96,112},{1,17},{17... | collective-permute-start | bytes 30728 | tf_op jit(solution)/shard_map/ppermute | solution.py:121
  98.5 1.9 %collective-permute-start.3 = (bf16[10,512]{1,0:T(8,128)(2,1)S(1)}, bf16[10,512]{1,0:T(8,128)(2,1)S(1)}, u32[]{:S(2)}, u32[]{:S(2)}) collective-permute-start(bf16[10,512]{1,0:T(8,128)(2,1)S(1)} %get-tuple-element.19), channel_id=1, source_target_pairs={{16,0},{32,16},{48,32},{64,48},{80,64},{96,80},{112,96},{17,1},{33... | collective-permute-start | bytes 30728 | tf_op jit(solution)/shard_map/ppermute | solution.py:122
  100.4 1.9 %fusion.35 = f32[512,512]{1,0:T(8,128)S(1)} fusion(bf16[512,1024]{1,0:T(8,128)(2,1)} %constant.6.clone, bf16[512,512]{1,0:T(8,128)(2,1)S(1)} %fusion.29), kind=kOutput, calls=%fused_computation.32 | convolution fusion | flops 538968064 | bytes 2621440 | tf_op jit(solution)/shard_map/dot_general | solution.py:123
  102.3 0.0 collective-permute-done.2
  102.3 1.2 %collective-permute-done.3 = bf16[10,512]{1,0:T(8,128)(2,1)S(1)} collective-permute-done((bf16[10,512]{1,0:T(8,128)(2,1)S(1)}, bf16[10,512]{1,0:T(8,128)(2,1)S(1)}, u32[]{:S(2)}, u32[]{:S(2)}) %collective-permute-start.3) | collective-permute-done | bytes 10272 | tf_op jit(solution)/shard_map/ppermute | solution.py:122
  103.5 1.3 %convolution_add_fusion = f32[512,512]{1,0:T(8,128)} fusion(f32[512,512]{1,0:T(8,128)S(1)} %fusion.35, bf16[512,40]{1,0:T(8,128)(2,1)S(1)} %copy-done.1, bf16[10,512]{1,0:T(8,128)(2,1)S(1)} %collective-permute-done.3, bf16[10,512]{1,0:T(8,128)(2,1)S(1)} %collective-permute-done.2), kind=kOutput, calls=%fused_computation.22 | convolution fusion | flops 21397504 | bytes 2158592 | tf_op jit(solution)/shard_map/dot_general | solution.py:125
  (6 shorter events, 0.0 us)
Async XLA Ops:
  0.6 2.3 %copy-start = (bf16[1,8,256,256]{3,2,1,0:T(8,128)(2,1)S(1)}, bf16[1,8,256,256]{3,2,1,0:T(8,128)(2,1)}, u32[]{:S(2)}) copy-start(bf16[1,8,256,256]{3,2,1,0:T(8,128)(2,1)} %param.8) | copy-start | bytes 3145732
  11.4 58.5 %copy-start.2 = (s32[2,1,32]{2,1,0:T(1,128)S(1)}, s32[2,1,32]{2,1,0:T(1,128)}, u32[]{:S(2)}) copy-start(s32[2,1,32]{2,1,0:T(1,128)} %param.12) | copy-start | bytes 772
  74.7 12.6 %copy-start.3 = (bf16[512,1024]{1,0:T(8,128)(2,1)S(1)}, bf16[512,1024]{1,0:T(8,128)(2,1)}, u32[]{:S(2)}) copy-start(bf16[512,1024]{1,0:T(8,128)(2,1)} %constant.6.clone) | copy-start | bytes 3145732
  81.6 9.9 %copy-start.1 = (bf16[512,40]{1,0:T(8,128)(2,1)S(1)}, bf16[512,40]{1,0:T(8,128)(2,1)}, u32[]{:S(2)}) copy-start(bf16[512,40]{1,0:T(8,128)(2,1)} %constant.7.clone) | copy-start | bytes 122884
  82.0 7.4 %collective-permute-start = (bf16[10,512]{1,0:T(8,128)(2,1)S(1)}, bf16[10,512]{1,0:T(8,128)(2,1)S(1)}, u32[]{:S(2)}, u32[]{:S(2)}) collective-permute-start(bf16[10,512]{1,0:T(8,128)(2,1)S(1)} %get-tuple-element.20), channel_id=1, source_target_pairs={{0,1},{1,2},{2,3},{3,4},{4,5},{5,6},{6,7},{7,8},{8,9},{9,10},{10,1... | collective-permute-start | bytes 30728 | tf_op jit(solution)/shard_map/ppermute | solution.py:111
  84.9 6.6 %collective-permute-start.1 = (bf16[10,512]{1,0:T(8,128)(2,1)S(1)}, bf16[10,512]{1,0:T(8,128)(2,1)S(1)}, u32[]{:S(2)}, u32[]{:S(2)}) collective-permute-start(bf16[10,512]{1,0:T(8,128)(2,1)S(1)} %get-tuple-element.21), channel_id=1, source_target_pairs={{1,0},{2,1},{3,2},{4,3},{5,4},{6,5},{7,6},{8,7},{9,8},{10,9},{11,1... | collective-permute-start | bytes 30728 | tf_op jit(solution)/shard_map/ppermute | solution.py:112
  91.8 10.5 %collective-permute-start.2 = (bf16[10,512]{1,0:T(8,128)(2,1)S(1)}, bf16[10,512]{1,0:T(8,128)(2,1)S(1)}, u32[]{:S(2)}, u32[]{:S(2)}) collective-permute-start(bf16[10,512]{1,0:T(8,128)(2,1)S(1)} %get-tuple-element.18), channel_id=1, source_target_pairs={{0,16},{16,32},{32,48},{48,64},{64,80},{80,96},{96,112},{1,17},{17... | collective-permute-start | bytes 30728 | tf_op jit(solution)/shard_map/ppermute | solution.py:121
  98.5 5.1 %collective-permute-start.3 = (bf16[10,512]{1,0:T(8,128)(2,1)S(1)}, bf16[10,512]{1,0:T(8,128)(2,1)S(1)}, u32[]{:S(2)}, u32[]{:S(2)}) collective-permute-start(bf16[10,512]{1,0:T(8,128)(2,1)S(1)} %get-tuple-element.19), channel_id=1, source_target_pairs={{16,0},{32,16},{48,32},{64,48},{80,64},{96,80},{112,96},{17,1},{33... | collective-permute-start | bytes 30728 | tf_op jit(solution)/shard_map/ppermute | solution.py:122

commit v12 on v8

--- a/solution.py
+++ b/solution.py
@@ -137,10 +137,9 @@
     own_weight = weights[0]
     own_slot = tile_slot[0]
     offsets = slot_offset[:, 0, :]
-    hits = own_slot[None, :] == jnp.arange(slots, dtype=jnp.int32)[:, None]
-    present = jnp.any(hits, axis=1)
-    which = jnp.sum(jnp.where(hits, jnp.arange(count, dtype=jnp.int32)[None, :], 0), axis=1)
-    which = jnp.where(present, which, count)
+    which = jnp.full((slots,), count, jnp.int32).at[own_slot].set(
+        jnp.arange(count, dtype=jnp.int32), unique_indices=True, mode="promise_in_bounds"
+    )
     own_matched = match_all(own_tiles, own_coeffs, basis)
     extra = 16
     line = jnp.arange(extra, dtype=jnp.int32)[None, :, None] == 0

time: 103 us -> 102 us (level)
  no operation moved by 1% of the time
where the time goes in v12:
time: 102 us
  blocking collectives  58.5 us (57%)
  matrix products  18.8 us (18%)
  starting transfers between devices  11.9 us (12%)
  waiting for transfers between devices  6.66 us (7%)
  local copies, waits for them, and re-layouts  3.9 us (4%)
  other arithmetic  1.65 us (2%)
    all_to_all x1, blocking collectives, body(): recv = lax.all_to_all(send, 'skyx', split_axis=0, concat_axis=0, tiled=True)  58.5 us
    dot_general x1, matrix products, match_all(): jnp.einsum('mbik,bjk->mbij', vert, basis, preferred_element_type=jnp.floa...  5.39 us
    dot_general x1, matrix products, coadd_patch(): jnp.dot(row_place.reshape(patch, slot_count * size), shifted.reshape(slot...  4.51 us
    ppermute x1, starting transfers between devices, detect(): top = lax.ppermute(own[-r:, :], 'skyy', down)  4.51 us
    dot_general x1, matrix products, coadd_patch(): jnp.einsum('sij,sjq->siq', matched, col_place, preferred_element_type=jnp...  4.37 us
    ppermute x1, waiting for transfers between devices, detect(): east = lax.ppermute(vown[:, :r].T, 'skyx', left)  4.31 us
    ppermute x1, starting transfers between devices, detect(): west = lax.ppermute(vown[:, -r:].T, 'skyx', right)  3.53 us
    gather x1, local copies, waits for them, and re-layouts, body(): send = carry[which].reshape(columns, CAP, size + extra, size)  2.85 us
  transfers between devices with their start and end apart: 4, of which 2 were waited for; matrix products, arithmetic and copies ran while one was open for 1% of the time, Pallas kernels for 0%

profile of v12, /device:TPU:29, one launch (start us, length us, event | category | flops | bytes accessed | tf_op | source)
XLA Modules:
  0.0 102.1 jit_solution(5257696870374081099)
XLA Ops:
  0.6 0.0 copy-start
  0.7 0.7 fusion.73
  1.4 0.6 scatter_custom_fusion
  2.0 0.7 broadcast_select_fusion
  2.8 0.0 copy-done
  2.8 5.4 %fusion.2 = bf16[8,256,256]{2,1,0:T(8,128)(2,1)S(1)} fusion(bf16[1,8,5,256,256]{4,3,2,1,0:T(8,128)(2,1)} %param.9, bf16[5,256,256,1]{2,1,3,0:T(8,128)(2,1)} %constant.38, bf16[1,8,256,256]{3,2,1,0:T(8,128)(2,1)S(1)} %copy-done), kind=kOutput, calls=%fused_computation.7 | convolution fusion | flops 2694316032 | bytes 7995392 | tf_op jit(solution)/shard_map/mbik,bjk->mbij/dot_general | solution.py:35
  8.2 0.1 mul.9
  8.3 0.1 fusion.30
  8.3 2.9 %gather_fusion = bf16[32,272,256]{2,1,0:T(8,128)(2,1)} fusion(bf16[9,272,256]{2,1,0:T(8,128)(2,1)S(1)} %fusion.30, s32[1024]{0:T(1024)S(1)} %pad_clamp_fusion), kind=kCustom, calls=%fused_computation | custom fusion | bytes 8913024 | tf_op jit(solution)/shard_map/gather | solution.py:151
  11.2 0.0 copy-start.2
  11.2 58.5 %all_to_all.5 = bf16[16,2,272,256]{3,2,1,0:T(8,128)(2,1)S(1)} all-to-all(bf16[16,2,272,256]{3,2,1,0:T(8,128)(2,1)} %bitcast.45), channel_id=1, replica_groups=mesh['skyy'=8,'skyx'=16] {'skyx'}, dimensions={0} | all-to-all | bytes 8912896 | tf_op jit(solution)/shard_map/all_to_all | solution.py:153
  69.7 0.0 copy-done.2
  69.7 0.3 slice_reduce_fusion
  70.0 0.1 iota_add_fusion
  70.1 4.4 %fusion.102 = bf16[32,256,512]{2,1,0:T(8,128)(2,1)S(1)} fusion(s32[32,256]{1,0:T(8,128)S(1)} %get-tuple-element.18, bf16[32,272,256]{2,1,0:T(8,128)(2,1)S(1)} %bitcast.47), kind=kOutput, calls=%fused_computation.9.clone.clone.clone.2 | convolution fusion | flops 2155872256 | bytes 12615680 | tf_op jit(solution)/shard_map/sij,sjq->siq/dot_general | solution.py:47
  74.5 0.0 copy-start.3
  74.5 4.5 %fusion.22 = f32[512,512]{1,0:T(8,128)S(1)} fusion(s32[32,256]{1,0:T(8,128)S(1)} %get-tuple-element.19, bf16[32]{0:T(256)(128)(2,1)S(1)} %slice_reduce_fusion, bf16[32,256,512]{2,1,0:T(8,128)(2,1)S(1)} %fusion.102), kind=kOutput, calls=%fused_computation.26 | convolution fusion | flops 4303355904 | bytes 9470016 | tf_op jit(solution)/shard_map/dot_general | solution.py:52
  79.0 0.0 copy-start.1
  79.0 1.3 %fusion.85 = (bf16[512,512]{1,0:T(8,128)(2,1)S(1)}, f32[512,512]{1,0:T(8,128)}) fusion(f32[512,512]{1,0:T(8,128)S(1)} %fusion.22, s32[32]{0:T(128)S(1)} %get-tuple-element.15, s32[32]{0:T(128)S(1)} %get-tuple-element.14, bf16[32]{0:T(256)(128)(2,1)S(1)} %slice_reduce_fusion), kind=kOutput, calls=%fused_computation.93 | convolution fusion | flops 17711104 | bytes 2621760 | tf_op jit(solution)/shard_map/dot_general | solution.py:63
  80.3 4.5 %collective-permute-start = (bf16[10,512]{1,0:T(8,128)(2,1)S(1)}, bf16[10,512]{1,0:T(8,128)(2,1)S(1)}, u32[]{:S(2)}, u32[]{:S(2)}) collective-permute-start(bf16[10,512]{1,0:T(8,128)(2,1)S(1)} %get-tuple-element.12), channel_id=1, source_target_pairs={{0,16},{16,32},{32,48},{48,64},{64,80},{80,96},{96,112},{1,17},{17... | collective-permute-start | bytes 30728 | tf_op jit(solution)/shard_map/ppermute | solution.py:111
  84.9 1.9 %collective-permute-start.1 = (bf16[10,512]{1,0:T(8,128)(2,1)S(1)}, bf16[10,512]{1,0:T(8,128)(2,1)S(1)}, u32[]{:S(2)}, u32[]{:S(2)}) collective-permute-start(bf16[10,512]{1,0:T(8,128)(2,1)S(1)} %get-tuple-element.13), channel_id=1, source_target_pairs={{16,0},{32,16},{48,32},{64,48},{80,64},{96,80},{112,96},{17,1},{33... | collective-permute-start | bytes 30728 | tf_op jit(solution)/shard_map/ppermute | solution.py:112
  86.8 0.0 copy-done.3
  86.8 0.8 fusion.31
  87.6 0.0 collective-permute-done
  87.6 2.3 %collective-permute-done.1 = bf16[10,512]{1,0:T(8,128)(2,1)S(1)} collective-permute-done((bf16[10,512]{1,0:T(8,128)(2,1)S(1)}, bf16[10,512]{1,0:T(8,128)(2,1)S(1)}, u32[]{:S(2)}, u32[]{:S(2)}) %collective-permute-start.1) | collective-permute-done | bytes 10272 | tf_op jit(solution)/shard_map/ppermute | solution.py:112
  89.9 0.0 copy-done.1
  89.9 0.3 fusion.29
  90.3 3.5 %collective-permute-start.2 = (bf16[10,512]{1,0:T(8,128)(2,1)S(1)}, bf16[10,512]{1,0:T(8,128)(2,1)S(1)}, u32[]{:S(2)}, u32[]{:S(2)}) collective-permute-start(bf16[10,512]{1,0:T(8,128)(2,1)S(1)} %get-tuple-element.10), channel_id=1, source_target_pairs={{0,1},{1,2},{2,3},{3,4},{4,5},{5,6},{6,7},{7,8},{8,9},{9,10},{10,1... | collective-permute-start | bytes 30728 | tf_op jit(solution)/shard_map/ppermute | solution.py:117
  93.8 1.9 %collective-permute-start.3 = (bf16[10,512]{1,0:T(8,128)(2,1)S(1)}, bf16[10,512]{1,0:T(8,128)(2,1)S(1)}, u32[]{:S(2)}, u32[]{:S(2)}) collective-permute-start(bf16[10,512]{1,0:T(8,128)(2,1)S(1)} %get-tuple-element.11), channel_id=1, source_target_pairs={{1,0},{2,1},{3,2},{4,3},{5,4},{6,5},{7,6},{8,7},{9,8},{10,9},{11,1... | collective-permute-start | bytes 30728 | tf_op jit(solution)/shard_map/ppermute | solution.py:118
  95.7 0.8 fusion.35
  96.5 0.0 collective-permute-done.2
  96.5 4.3 %collective-permute-done.3 = bf16[10,512]{1,0:T(8,128)(2,1)S(1)} collective-permute-done((bf16[10,512]{1,0:T(8,128)(2,1)S(1)}, bf16[10,512]{1,0:T(8,128)(2,1)S(1)}, u32[]{:S(2)}, u32[]{:S(2)}) %collective-permute-start.3) | collective-permute-done | bytes 10272 | tf_op jit(solution)/shard_map/ppermute | solution.py:118
  100.8 1.3 %convolution_add_fusion = f32[512,512]{1,0:T(8,128)} fusion(f32[512,512]{1,0:T(8,128)S(1)} %fusion.35, bf16[512,40]{1,0:T(8,128)(2,1)S(1)} %copy-done.1, bf16[10,512]{1,0:T(8,128)(2,1)S(1)} %collective-permute-done.3, bf16[10,512]{1,0:T(8,128)(2,1)S(1)} %collective-permute-done.2), kind=kOutput, calls=%fused_computation.22 | convolution fusion | flops 21397504 | bytes 2158592 | tf_op jit(solution)/shard_map/dot_general | solution.py:125
  (7 shorter events, 0.0 us)
Async XLA Ops:
  0.6 2.1 %copy-start = (bf16[1,8,256,256]{3,2,1,0:T(8,128)(2,1)S(1)}, bf16[1,8,256,256]{3,2,1,0:T(8,128)(2,1)}, u32[]{:S(2)}) copy-start(bf16[1,8,256,256]{3,2,1,0:T(8,128)(2,1)} %param.8) | copy-start | bytes 3145732
  11.2 58.5 %copy-start.2 = (s32[2,1,32]{2,1,0:T(1,128)S(1)}, s32[2,1,32]{2,1,0:T(1,128)}, u32[]{:S(2)}) copy-start(s32[2,1,32]{2,1,0:T(1,128)} %param.12) | copy-start | bytes 772
  74.5 12.3 %copy-start.3 = (bf16[512,1024]{1,0:T(8,128)(2,1)S(1)}, bf16[512,1024]{1,0:T(8,128)(2,1)}, u32[]{:S(2)}) copy-start(bf16[512,1024]{1,0:T(8,128)(2,1)} %constant.6.clone) | copy-start | bytes 3145732
  79.0 10.9 %copy-start.1 = (bf16[512,40]{1,0:T(8,128)(2,1)S(1)}, bf16[512,40]{1,0:T(8,128)(2,1)}, u32[]{:S(2)}) copy-start(bf16[512,40]{1,0:T(8,128)(2,1)} %constant.7.clone) | copy-start | bytes 122884
  80.3 7.2 %collective-permute-start = (bf16[10,512]{1,0:T(8,128)(2,1)S(1)}, bf16[10,512]{1,0:T(8,128)(2,1)S(1)}, u32[]{:S(2)}, u32[]{:S(2)}) collective-permute-start(bf16[10,512]{1,0:T(8,128)(2,1)S(1)} %get-tuple-element.12), channel_id=1, source_target_pairs={{0,16},{16,32},{32,48},{48,64},{64,80},{80,96},{96,112},{1,17},{17... | collective-permute-start | bytes 30728 | tf_op jit(solution)/shard_map/ppermute | solution.py:111
  84.9 5.1 %collective-permute-start.1 = (bf16[10,512]{1,0:T(8,128)(2,1)S(1)}, bf16[10,512]{1,0:T(8,128)(2,1)S(1)}, u32[]{:S(2)}, u32[]{:S(2)}) collective-permute-start(bf16[10,512]{1,0:T(8,128)(2,1)S(1)} %get-tuple-element.13), channel_id=1, source_target_pairs={{16,0},{32,16},{48,32},{64,48},{80,64},{96,80},{112,96},{17,1},{33... | collective-permute-start | bytes 30728 | tf_op jit(solution)/shard_map/ppermute | solution.py:112
  90.3 6.2 %collective-permute-start.2 = (bf16[10,512]{1,0:T(8,128)(2,1)S(1)}, bf16[10,512]{1,0:T(8,128)(2,1)S(1)}, u32[]{:S(2)}, u32[]{:S(2)}) collective-permute-start(bf16[10,512]{1,0:T(8,128)(2,1)S(1)} %get-tuple-element.10), channel_id=1, source_target_pairs={{0,1},{1,2},{2,3},{3,4},{4,5},{5,6},{6,7},{7,8},{8,9},{9,10},{10,1... | collective-permute-start | bytes 30728 | tf_op jit(solution)/shard_map/ppermute | solution.py:117
  93.8 7.0 %collective-permute-start.3 = (bf16[10,512]{1,0:T(8,128)(2,1)S(1)}, bf16[10,512]{1,0:T(8,128)(2,1)S(1)}, u32[]{:S(2)}, u32[]{:S(2)}) collective-permute-start(bf16[10,512]{1,0:T(8,128)(2,1)S(1)} %get-tuple-element.11), channel_id=1, source_target_pairs={{1,0},{2,1},{3,2},{4,3},{5,4},{6,5},{7,6},{8,7},{9,8},{10,9},{11,1... | collective-permute-start | bytes 30728 | tf_op jit(solution)/shard_map/ppermute | solution.py:118

commit v13 on v8

--- a/solution.py
+++ b/solution.py
@@ -143,10 +143,7 @@
     which = jnp.where(present, which, count)
     own_matched = match_all(own_tiles, own_coeffs, basis)
     extra = 16
-    line = jnp.arange(extra, dtype=jnp.int32)[None, :, None] == 0
-    weight_rows = jnp.where(
-        line, own_weight[:, None, None], jnp.zeros((), jnp.bfloat16)
-    ) * jnp.ones((1, 1, size), jnp.bfloat16)
+    weight_rows = jnp.broadcast_to(own_weight[:, None, None], (count, extra, size))
     carry = jnp.concatenate([own_matched, weight_rows], axis=1)
     carry = jnp.concatenate([carry, jnp.zeros((1, size + extra, size), jnp.bfloat16)], axis=0)
     send = carry[which].reshape(columns, CAP, size + extra, size)

time: 103 us -> 102 us (level)
  no operation moved by 1% of the time
where the time goes in v13:
time: 102 us
  blocking collectives  58.5 us (57%)
  matrix products  18.8 us (18%)
  starting transfers between devices  11.9 us (12%)
  waiting for transfers between devices  6.61 us (6%)
  local copies, waits for them, and re-layouts  3.32 us (3%)
  other arithmetic  1.74 us (2%)
    all_to_all x1, blocking collectives, body(): recv = lax.all_to_all(send, 'skyx', split_axis=0, concat_axis=0, tiled=True)  58.5 us
    dot_general x1, matrix products, match_all(): jnp.einsum('mbik,bjk->mbij', vert, basis, preferred_element_type=jnp.floa...  5.4 us
    dot_general x1, matrix products, coadd_patch(): jnp.dot(row_place.reshape(patch, slot_count * size), shifted.reshape(slot...  4.51 us
    ppermute x1, starting transfers between devices, detect(): top = lax.ppermute(own[-r:, :], 'skyy', down)  4.5 us
    dot_general x1, matrix products, coadd_patch(): jnp.einsum('sij,sjq->siq', matched, col_place, preferred_element_type=jnp...  4.39 us
    ppermute x1, waiting for transfers between devices, detect(): east = lax.ppermute(vown[:, :r].T, 'skyx', left)  4.26 us
    ppermute x1, starting transfers between devices, detect(): west = lax.ppermute(vown[:, -r:].T, 'skyx', right)  3.54 us
    gather x1, local copies, waits for them, and re-layouts, body(): send = carry[which].reshape(columns, CAP, size + extra, size)  2.87 us
  transfers between devices with their start and end apart: 4, of which 2 were waited for; matrix products, arithmetic and copies ran while one was open for 1% of the time, Pallas kernels for 0%

profile of v13, /device:TPU:29, one launch (start us, length us, event | category | flops | bytes accessed | tf_op | source)
XLA Modules:
  0.0 101.6 jit_solution(17935711017490872731)
XLA Ops:
  0.6 0.0 copy-start
  0.6 0.8 fusion.73
  1.5 0.7 select_reduce_fusion
  2.2 0.0 copy-done
  2.2 0.0 copy-start.3
  2.2 5.4 %fusion.2 = bf16[8,256,256]{2,1,0:T(8,128)(2,1)S(1)} fusion(bf16[1,8,5,256,256]{4,3,2,1,0:T(8,128)(2,1)} %param.9, bf16[5,256,256,1]{2,1,3,0:T(8,128)(2,1)} %constant.37, bf16[1,8,256,256]{3,2,1,0:T(8,128)(2,1)S(1)} %copy-done), kind=kOutput, calls=%fused_computation.6 | convolution fusion | flops 2694316032 | bytes 7995392 | tf_op jit(solution)/shard_map/mbik,bjk->mbij/dot_general | solution.py:35
  7.7 0.0 copy-done.3
  7.7 0.1 broadcast_in_dim.60
  7.7 0.1 fusion.30
  7.8 2.9 %gather_fusion = bf16[32,272,256]{2,1,0:T(8,128)(2,1)} fusion(bf16[9,272,256]{2,1,0:T(8,128)(2,1)S(1)} %fusion.30, s32[1024]{0:T(1024)S(1)} %pad_clamp_fusion), kind=kCustom, calls=%fused_computation | custom fusion | bytes 8913024 | tf_op jit(solution)/shard_map/gather | solution.py:149
  10.7 0.0 copy-start.2
  10.7 58.5 %all_to_all.5 = bf16[16,2,272,256]{3,2,1,0:T(8,128)(2,1)S(1)} all-to-all(bf16[16,2,272,256]{3,2,1,0:T(8,128)(2,1)} %bitcast.46), channel_id=1, replica_groups=mesh['skyy'=8,'skyx'=16] {'skyx'}, dimensions={0} | all-to-all | bytes 8912896 | tf_op jit(solution)/shard_map/all_to_all | solution.py:151
  69.2 0.0 copy-done.2
  69.2 0.3 slice_reduce_fusion
  69.5 0.1 iota_add_fusion
  69.6 4.4 %fusion.101 = bf16[32,256,512]{2,1,0:T(8,128)(2,1)S(1)} fusion(s32[32,256]{1,0:T(8,128)S(1)} %get-tuple-element.18, bf16[32,272,256]{2,1,0:T(8,128)(2,1)S(1)} %bitcast.48), kind=kOutput, calls=%fused_computation.8.clone.clone.clone.2 | convolution fusion | flops 2155872256 | bytes 12615680 | tf_op jit(solution)/shard_map/sij,sjq->siq/dot_general | solution.py:47
  74.0 0.0 copy-start.4
  74.0 4.5 %fusion.22 = f32[512,512]{1,0:T(8,128)S(1)} fusion(s32[32,256]{1,0:T(8,128)S(1)} %get-tuple-element.19, bf16[32]{0:T(256)(128)(2,1)S(1)} %slice_reduce_fusion, bf16[32,256,512]{2,1,0:T(8,128)(2,1)S(1)} %fusion.101), kind=kOutput, calls=%fused_computation.25 | convolution fusion | flops 4303355904 | bytes 9470016 | tf_op jit(solution)/shard_map/dot_general | solution.py:52
  78.5 0.0 copy-start.1
  78.5 1.3 %fusion.84 = (bf16[512,512]{1,0:T(8,128)(2,1)S(1)}, f32[512,512]{1,0:T(8,128)}) fusion(f32[512,512]{1,0:T(8,128)S(1)} %fusion.22, s32[32]{0:T(128)S(1)} %get-tuple-element.15, s32[32]{0:T(128)S(1)} %get-tuple-element.14, bf16[32]{0:T(256)(128)(2,1)S(1)} %slice_reduce_fusion), kind=kOutput, calls=%fused_computation.90 | convolution fusion | flops 17711104 | bytes 2621760 | tf_op jit(solution)/shard_map/dot_general | solution.py:63
  79.9 4.5 %collective-permute-start = (bf16[10,512]{1,0:T(8,128)(2,1)S(1)}, bf16[10,512]{1,0:T(8,128)(2,1)S(1)}, u32[]{:S(2)}, u32[]{:S(2)}) collective-permute-start(bf16[10,512]{1,0:T(8,128)(2,1)S(1)} %get-tuple-element.12), channel_id=1, source_target_pairs={{0,16},{16,32},{32,48},{48,64},{64,80},{80,96},{96,112},{1,17},{17... | collective-permute-start | bytes 30728 | tf_op jit(solution)/shard_map/ppermute | solution.py:111
  84.4 1.9 %collective-permute-start.1 = (bf16[10,512]{1,0:T(8,128)(2,1)S(1)}, bf16[10,512]{1,0:T(8,128)(2,1)S(1)}, u32[]{:S(2)}, u32[]{:S(2)}) collective-permute-start(bf16[10,512]{1,0:T(8,128)(2,1)S(1)} %get-tuple-element.13), channel_id=1, source_target_pairs={{16,0},{32,16},{48,32},{64,48},{80,64},{96,80},{112,96},{17,1},{33... | collective-permute-start | bytes 30728 | tf_op jit(solution)/shard_map/ppermute | solution.py:112
  86.3 0.0 copy-done.4
  86.3 0.8 fusion.31
  87.1 0.0 collective-permute-done
  87.1 2.3 %collective-permute-done.1 = bf16[10,512]{1,0:T(8,128)(2,1)S(1)} collective-permute-done((bf16[10,512]{1,0:T(8,128)(2,1)S(1)}, bf16[10,512]{1,0:T(8,128)(2,1)S(1)}, u32[]{:S(2)}, u32[]{:S(2)}) %collective-permute-start.1) | collective-permute-done | bytes 10272 | tf_op jit(solution)/shard_map/ppermute | solution.py:112
  89.4 0.0 copy-done.1
  89.4 0.3 fusion.29
  89.8 3.5 %collective-permute-start.2 = (bf16[10,512]{1,0:T(8,128)(2,1)S(1)}, bf16[10,512]{1,0:T(8,128)(2,1)S(1)}, u32[]{:S(2)}, u32[]{:S(2)}) collective-permute-start(bf16[10,512]{1,0:T(8,128)(2,1)S(1)} %get-tuple-element.10), channel_id=1, source_target_pairs={{0,1},{1,2},{2,3},{3,4},{4,5},{5,6},{6,7},{7,8},{8,9},{9,10},{10,1... | collective-permute-start | bytes 30728 | tf_op jit(solution)/shard_map/ppermute | solution.py:117
  93.3 1.9 %collective-permute-start.3 = (bf16[10,512]{1,0:T(8,128)(2,1)S(1)}, bf16[10,512]{1,0:T(8,128)(2,1)S(1)}, u32[]{:S(2)}, u32[]{:S(2)}) collective-permute-start(bf16[10,512]{1,0:T(8,128)(2,1)S(1)} %get-tuple-element.11), channel_id=1, source_target_pairs={{1,0},{2,1},{3,2},{4,3},{5,4},{6,5},{7,6},{8,7},{9,8},{10,9},{11,1... | collective-permute-start | bytes 30728 | tf_op jit(solution)/shard_map/ppermute | solution.py:118
  95.3 0.8 fusion.35
  96.0 0.0 collective-permute-done.2
  96.0 4.3 %collective-permute-done.3 = bf16[10,512]{1,0:T(8,128)(2,1)S(1)} collective-permute-done((bf16[10,512]{1,0:T(8,128)(2,1)S(1)}, bf16[10,512]{1,0:T(8,128)(2,1)S(1)}, u32[]{:S(2)}, u32[]{:S(2)}) %collective-permute-start.3) | collective-permute-done | bytes 10272 | tf_op jit(solution)/shard_map/ppermute | solution.py:118
  100.3 1.3 %convolution_add_fusion = f32[512,512]{1,0:T(8,128)} fusion(f32[512,512]{1,0:T(8,128)S(1)} %fusion.35, bf16[512,40]{1,0:T(8,128)(2,1)S(1)} %copy-done.1, bf16[10,512]{1,0:T(8,128)(2,1)S(1)} %collective-permute-done.3, bf16[10,512]{1,0:T(8,128)(2,1)S(1)} %collective-permute-done.2), kind=kOutput, calls=%fused_computation.21 | convolution fusion | flops 21397504 | bytes 2158592 | tf_op jit(solution)/shard_map/dot_general | solution.py:125
  (5 shorter events, 0.0 us)
Async XLA Ops:
  0.6 1.6 %copy-start = (bf16[1,8,256,256]{3,2,1,0:T(8,128)(2,1)S(1)}, bf16[1,8,256,256]{3,2,1,0:T(8,128)(2,1)}, u32[]{:S(2)}) copy-start(bf16[1,8,256,256]{3,2,1,0:T(8,128)(2,1)} %param.8) | copy-start | bytes 3145732
  2.2 5.4 %copy-start.3 = (bf16[1,8]{1,0:T(2,128)(2,1)S(1)}, bf16[1,8]{1,0:T(2,128)(2,1)}, u32[]{:S(2)}) copy-start(bf16[1,8]{1,0:T(2,128)(2,1)} %param.10) | copy-start | bytes 52
  10.7 58.5 %copy-start.2 = (s32[2,1,32]{2,1,0:T(1,128)S(1)}, s32[2,1,32]{2,1,0:T(1,128)}, u32[]{:S(2)}) copy-start(s32[2,1,32]{2,1,0:T(1,128)} %param.12) | copy-start | bytes 772
  74.0 12.3 %copy-start.4 = (bf16[512,1024]{1,0:T(8,128)(2,1)S(1)}, bf16[512,1024]{1,0:T(8,128)(2,1)}, u32[]{:S(2)}) copy-start(bf16[512,1024]{1,0:T(8,128)(2,1)} %constant.7.clone) | copy-start | bytes 3145732
  78.5 10.9 %copy-start.1 = (bf16[512,40]{1,0:T(8,128)(2,1)S(1)}, bf16[512,40]{1,0:T(8,128)(2,1)}, u32[]{:S(2)}) copy-start(bf16[512,40]{1,0:T(8,128)(2,1)} %constant.8.clone) | copy-start | bytes 122884
  79.9 7.2 %collective-permute-start = (bf16[10,512]{1,0:T(8,128)(2,1)S(1)}, bf16[10,512]{1,0:T(8,128)(2,1)S(1)}, u32[]{:S(2)}, u32[]{:S(2)}) collective-permute-start(bf16[10,512]{1,0:T(8,128)(2,1)S(1)} %get-tuple-element.12), channel_id=1, source_target_pairs={{0,16},{16,32},{32,48},{48,64},{64,80},{80,96},{96,112},{1,17},{17... | collective-permute-start | bytes 30728 | tf_op jit(solution)/shard_map/ppermute | solution.py:111
  84.4 5.1 %collective-permute-start.1 = (bf16[10,512]{1,0:T(8,128)(2,1)S(1)}, bf16[10,512]{1,0:T(8,128)(2,1)S(1)}, u32[]{:S(2)}, u32[]{:S(2)}) collective-permute-start(bf16[10,512]{1,0:T(8,128)(2,1)S(1)} %get-tuple-element.13), channel_id=1, source_target_pairs={{16,0},{32,16},{48,32},{64,48},{80,64},{96,80},{112,96},{17,1},{33... | collective-permute-start | bytes 30728 | tf_op jit(solution)/shard_map/ppermute | solution.py:112
  89.8 6.2 %collective-permute-start.2 = (bf16[10,512]{1,0:T(8,128)(2,1)S(1)}, bf16[10,512]{1,0:T(8,128)(2,1)S(1)}, u32[]{:S(2)}, u32[]{:S(2)}) collective-permute-start(bf16[10,512]{1,0:T(8,128)(2,1)S(1)} %get-tuple-element.10), channel_id=1, source_target_pairs={{0,1},{1,2},{2,3},{3,4},{4,5},{5,6},{6,7},{7,8},{8,9},{9,10},{10,1... | collective-permute-start | bytes 30728 | tf_op jit(solution)/shard_map/ppermute | solution.py:117
  93.3 7.0 %collective-permute-start.3 = (bf16[10,512]{1,0:T(8,128)(2,1)S(1)}, bf16[10,512]{1,0:T(8,128)(2,1)S(1)}, u32[]{:S(2)}, u32[]{:S(2)}) collective-permute-start(bf16[10,512]{1,0:T(8,128)(2,1)S(1)} %get-tuple-element.11), channel_id=1, source_target_pairs={{1,0},{2,1},{3,2},{4,3},{5,4},{6,5},{7,6},{8,7},{9,8},{10,9},{11,1... | collective-permute-start | bytes 30728 | tf_op jit(solution)/shard_map/ppermute | solution.py:118

commit v14 on v12

--- a/solution.py
+++ b/solution.py
@@ -142,10 +142,7 @@
     )
     own_matched = match_all(own_tiles, own_coeffs, basis)
     extra = 16
-    line = jnp.arange(extra, dtype=jnp.int32)[None, :, None] == 0
-    weight_rows = jnp.where(
-        line, own_weight[:, None, None], jnp.zeros((), jnp.bfloat16)
-    ) * jnp.ones((1, 1, size), jnp.bfloat16)
+    weight_rows = jnp.broadcast_to(own_weight[:, None, None], (count, extra, size))
     carry = jnp.concatenate([own_matched, weight_rows], axis=1)
     carry = jnp.concatenate([carry, jnp.zeros((1, size + extra, size), jnp.bfloat16)], axis=0)
     send = carry[which].reshape(columns, CAP, size + extra, size)

time: 102 us -> 102 us (level)
  no operation moved by 1% of the time
where the time goes in v14:
time: 102 us; the launch traced here: 101 us
  blocking collectives  58.5 us (57%)
  matrix products  18.8 us (18%)
  starting transfers between devices  11.9 us (12%)
  waiting for transfers between devices  6.67 us (7%)
  local copies, waits for them, and re-layouts  3.9 us (4%)
    all_to_all x1, blocking collectives, body(): recv = lax.all_to_all(send, 'skyx', split_axis=0, concat_axis=0, tiled=True)  58.5 us
    dot_general x1, matrix products, match_all(): jnp.einsum('mbik,bjk->mbij', vert, basis, preferred_element_type=jnp.floa...  5.4 us
    dot_general x1, matrix products, coadd_patch(): jnp.dot(row_place.reshape(patch, slot_count * size), shifted.reshape(slot...  4.51 us
    ppermute x1, starting transfers between devices, detect(): top = lax.ppermute(own[-r:, :], 'skyy', down)  4.48 us
    dot_general x1, matrix products, coadd_patch(): jnp.einsum('sij,sjq->siq', matched, col_place, preferred_element_type=jnp...  4.39 us
    ppermute x1, waiting for transfers between devices, detect(): east = lax.ppermute(vown[:, :r].T, 'skyx', left)  4.31 us
    ppermute x1, starting transfers between devices, detect(): west = lax.ppermute(vown[:, -r:].T, 'skyx', right)  3.54 us
    gather x1, local copies, waits for them, and re-layouts, body(): send = carry[which].reshape(columns, CAP, size + extra, size)  2.85 us
  transfers between devices with their start and end apart: 4, of which 2 were waited for; matrix products, arithmetic and copies ran while one was open for 1% of the time, Pallas kernels for 0%

profile of v14, /device:TPU:29, one launch (start us, length us, event | category | flops | bytes accessed | tf_op | source)
XLA Modules:
  0.0 101.4 jit_solution(10550655270598582098)
XLA Ops:
  0.6 0.0 copy-start
  0.6 0.7 fusion.73
  1.4 0.6 scatter_custom_fusion
  2.0 0.0 copy-done
  2.0 0.0 copy-start.3
  2.0 5.4 %fusion.2 = bf16[8,256,256]{2,1,0:T(8,128)(2,1)S(1)} fusion(bf16[1,8,5,256,256]{4,3,2,1,0:T(8,128)(2,1)} %param.9, bf16[5,256,256,1]{2,1,3,0:T(8,128)(2,1)} %constant.37, bf16[1,8,256,256]{3,2,1,0:T(8,128)(2,1)S(1)} %copy-done), kind=kOutput, calls=%fused_computation.7 | convolution fusion | flops 2694316032 | bytes 7995392 | tf_op jit(solution)/shard_map/mbik,bjk->mbij/dot_general | solution.py:35
  7.5 0.0 copy-done.3
  7.5 0.1 broadcast_in_dim.48
  7.5 0.1 fusion.30
  7.6 2.8 %gather_fusion = bf16[32,272,256]{2,1,0:T(8,128)(2,1)} fusion(bf16[9,272,256]{2,1,0:T(8,128)(2,1)S(1)} %fusion.30, s32[1024]{0:T(1024)S(1)} %pad_clamp_fusion), kind=kCustom, calls=%fused_computation | custom fusion | bytes 8913024 | tf_op jit(solution)/shard_map/gather | solution.py:148
  10.5 0.0 copy-start.2
  10.5 58.5 %all_to_all.5 = bf16[16,2,272,256]{3,2,1,0:T(8,128)(2,1)S(1)} all-to-all(bf16[16,2,272,256]{3,2,1,0:T(8,128)(2,1)} %bitcast.45), channel_id=1, replica_groups=mesh['skyy'=8,'skyx'=16] {'skyx'}, dimensions={0} | all-to-all | bytes 8912896 | tf_op jit(solution)/shard_map/all_to_all | solution.py:150
  69.0 0.0 copy-done.2
  69.0 0.3 slice_reduce_fusion
  69.3 0.1 iota_add_fusion
  69.4 4.4 %fusion.102 = bf16[32,256,512]{2,1,0:T(8,128)(2,1)S(1)} fusion(s32[32,256]{1,0:T(8,128)S(1)} %get-tuple-element.18, bf16[32,272,256]{2,1,0:T(8,128)(2,1)S(1)} %bitcast.47), kind=kOutput, calls=%fused_computation.9.clone.clone.clone.2 | convolution fusion | flops 2155872256 | bytes 12615680 | tf_op jit(solution)/shard_map/sij,sjq->siq/dot_general | solution.py:47
  73.8 0.0 copy-start.4
  73.8 4.5 %fusion.22 = f32[512,512]{1,0:T(8,128)S(1)} fusion(s32[32,256]{1,0:T(8,128)S(1)} %get-tuple-element.19, bf16[32]{0:T(256)(128)(2,1)S(1)} %slice_reduce_fusion, bf16[32,256,512]{2,1,0:T(8,128)(2,1)S(1)} %fusion.102), kind=kOutput, calls=%fused_computation.26 | convolution fusion | flops 4303355904 | bytes 9470016 | tf_op jit(solution)/shard_map/dot_general | solution.py:52
  78.3 0.0 copy-start.1
  78.3 1.3 %fusion.85 = (bf16[512,512]{1,0:T(8,128)(2,1)S(1)}, f32[512,512]{1,0:T(8,128)}) fusion(f32[512,512]{1,0:T(8,128)S(1)} %fusion.22, s32[32]{0:T(128)S(1)} %get-tuple-element.15, s32[32]{0:T(128)S(1)} %get-tuple-element.14, bf16[32]{0:T(256)(128)(2,1)S(1)} %slice_reduce_fusion), kind=kOutput, calls=%fused_computation.91 | convolution fusion | flops 17711104 | bytes 2621760 | tf_op jit(solution)/shard_map/dot_general | solution.py:63
  79.6 4.5 %collective-permute-start = (bf16[10,512]{1,0:T(8,128)(2,1)S(1)}, bf16[10,512]{1,0:T(8,128)(2,1)S(1)}, u32[]{:S(2)}, u32[]{:S(2)}) collective-permute-start(bf16[10,512]{1,0:T(8,128)(2,1)S(1)} %get-tuple-element.12), channel_id=1, source_target_pairs={{0,16},{16,32},{32,48},{48,64},{64,80},{80,96},{96,112},{1,17},{17... | collective-permute-start | bytes 30728 | tf_op jit(solution)/shard_map/ppermute | solution.py:111
  84.1 1.9 %collective-permute-start.1 = (bf16[10,512]{1,0:T(8,128)(2,1)S(1)}, bf16[10,512]{1,0:T(8,128)(2,1)S(1)}, u32[]{:S(2)}, u32[]{:S(2)}) collective-permute-start(bf16[10,512]{1,0:T(8,128)(2,1)S(1)} %get-tuple-element.13), channel_id=1, source_target_pairs={{16,0},{32,16},{48,32},{64,48},{80,64},{96,80},{112,96},{17,1},{33... | collective-permute-start | bytes 30728 | tf_op jit(solution)/shard_map/ppermute | solution.py:112
  86.1 0.0 copy-done.4
  86.1 0.8 fusion.31
  86.8 0.0 collective-permute-done
  86.8 2.3 %collective-permute-done.1 = bf16[10,512]{1,0:T(8,128)(2,1)S(1)} collective-permute-done((bf16[10,512]{1,0:T(8,128)(2,1)S(1)}, bf16[10,512]{1,0:T(8,128)(2,1)S(1)}, u32[]{:S(2)}, u32[]{:S(2)}) %collective-permute-start.1) | collective-permute-done | bytes 10272 | tf_op jit(solution)/shard_map/ppermute | solution.py:112
  89.2 0.0 copy-done.1
  89.2 0.3 fusion.29
  89.6 3.5 %collective-permute-start.2 = (bf16[10,512]{1,0:T(8,128)(2,1)S(1)}, bf16[10,512]{1,0:T(8,128)(2,1)S(1)}, u32[]{:S(2)}, u32[]{:S(2)}) collective-permute-start(bf16[10,512]{1,0:T(8,128)(2,1)S(1)} %get-tuple-element.10), channel_id=1, source_target_pairs={{0,1},{1,2},{2,3},{3,4},{4,5},{5,6},{6,7},{7,8},{8,9},{9,10},{10,1... | collective-permute-start | bytes 30728 | tf_op jit(solution)/shard_map/ppermute | solution.py:117
  93.1 1.9 %collective-permute-start.3 = (bf16[10,512]{1,0:T(8,128)(2,1)S(1)}, bf16[10,512]{1,0:T(8,128)(2,1)S(1)}, u32[]{:S(2)}, u32[]{:S(2)}) collective-permute-start(bf16[10,512]{1,0:T(8,128)(2,1)S(1)} %get-tuple-element.11), channel_id=1, source_target_pairs={{1,0},{2,1},{3,2},{4,3},{5,4},{6,5},{7,6},{8,7},{9,8},{10,9},{11,1... | collective-permute-start | bytes 30728 | tf_op jit(solution)/shard_map/ppermute | solution.py:118
  95.0 0.8 fusion.35
  95.8 0.0 collective-permute-done.2
  95.8 4.3 %collective-permute-done.3 = bf16[10,512]{1,0:T(8,128)(2,1)S(1)} collective-permute-done((bf16[10,512]{1,0:T(8,128)(2,1)S(1)}, bf16[10,512]{1,0:T(8,128)(2,1)S(1)}, u32[]{:S(2)}, u32[]{:S(2)}) %collective-permute-start.3) | collective-permute-done | bytes 10272 | tf_op jit(solution)/shard_map/ppermute | solution.py:118
  100.1 1.3 %convolution_add_fusion = f32[512,512]{1,0:T(8,128)} fusion(f32[512,512]{1,0:T(8,128)S(1)} %fusion.35, bf16[512,40]{1,0:T(8,128)(2,1)S(1)} %copy-done.1, bf16[10,512]{1,0:T(8,128)(2,1)S(1)} %collective-permute-done.3, bf16[10,512]{1,0:T(8,128)(2,1)S(1)} %collective-permute-done.2), kind=kOutput, calls=%fused_computation.22 | convolution fusion | flops 21397504 | bytes 2158592 | tf_op jit(solution)/shard_map/dot_general | solution.py:125
  (6 shorter events, 0.0 us)
Async XLA Ops:
  0.6 1.4 %copy-start = (bf16[1,8,256,256]{3,2,1,0:T(8,128)(2,1)S(1)}, bf16[1,8,256,256]{3,2,1,0:T(8,128)(2,1)}, u32[]{:S(2)}) copy-start(bf16[1,8,256,256]{3,2,1,0:T(8,128)(2,1)} %param.8) | copy-start | bytes 3145732
  2.0 5.4 %copy-start.3 = (bf16[1,8]{1,0:T(2,128)(2,1)S(1)}, bf16[1,8]{1,0:T(2,128)(2,1)}, u32[]{:S(2)}) copy-start(bf16[1,8]{1,0:T(2,128)(2,1)} %param.10) | copy-start | bytes 52
  10.5 58.5 %copy-start.2 = (s32[2,1,32]{2,1,0:T(1,128)S(1)}, s32[2,1,32]{2,1,0:T(1,128)}, u32[]{:S(2)}) copy-start(s32[2,1,32]{2,1,0:T(1,128)} %param.12) | copy-start | bytes 772
  73.8 12.3 %copy-start.4 = (bf16[512,1024]{1,0:T(8,128)(2,1)S(1)}, bf16[512,1024]{1,0:T(8,128)(2,1)}, u32[]{:S(2)}) copy-start(bf16[512,1024]{1,0:T(8,128)(2,1)} %constant.7.clone) | copy-start | bytes 3145732
  78.3 10.9 %copy-start.1 = (bf16[512,40]{1,0:T(8,128)(2,1)S(1)}, bf16[512,40]{1,0:T(8,128)(2,1)}, u32[]{:S(2)}) copy-start(bf16[512,40]{1,0:T(8,128)(2,1)} %constant.8.clone) | copy-start | bytes 122884
  79.6 7.2 %collective-permute-start = (bf16[10,512]{1,0:T(8,128)(2,1)S(1)}, bf16[10,512]{1,0:T(8,128)(2,1)S(1)}, u32[]{:S(2)}, u32[]{:S(2)}) collective-permute-start(bf16[10,512]{1,0:T(8,128)(2,1)S(1)} %get-tuple-element.12), channel_id=1, source_target_pairs={{0,16},{16,32},{32,48},{48,64},{64,80},{80,96},{96,112},{1,17},{17... | collective-permute-start | bytes 30728 | tf_op jit(solution)/shard_map/ppermute | solution.py:111
  84.1 5.1 %collective-permute-start.1 = (bf16[10,512]{1,0:T(8,128)(2,1)S(1)}, bf16[10,512]{1,0:T(8,128)(2,1)S(1)}, u32[]{:S(2)}, u32[]{:S(2)}) collective-permute-start(bf16[10,512]{1,0:T(8,128)(2,1)S(1)} %get-tuple-element.13), channel_id=1, source_target_pairs={{16,0},{32,16},{48,32},{64,48},{80,64},{96,80},{112,96},{17,1},{33... | collective-permute-start | bytes 30728 | tf_op jit(solution)/shard_map/ppermute | solution.py:112
  89.6 6.2 %collective-permute-start.2 = (bf16[10,512]{1,0:T(8,128)(2,1)S(1)}, bf16[10,512]{1,0:T(8,128)(2,1)S(1)}, u32[]{:S(2)}, u32[]{:S(2)}) collective-permute-start(bf16[10,512]{1,0:T(8,128)(2,1)S(1)} %get-tuple-element.10), channel_id=1, source_target_pairs={{0,1},{1,2},{2,3},{3,4},{4,5},{5,6},{6,7},{7,8},{8,9},{9,10},{10,1... | collective-permute-start | bytes 30728 | tf_op jit(solution)/shard_map/ppermute | solution.py:117
  93.1 7.0 %collective-permute-start.3 = (bf16[10,512]{1,0:T(8,128)(2,1)S(1)}, bf16[10,512]{1,0:T(8,128)(2,1)S(1)}, u32[]{:S(2)}, u32[]{:S(2)}) collective-permute-start(bf16[10,512]{1,0:T(8,128)(2,1)S(1)} %get-tuple-element.11), channel_id=1, source_target_pairs={{1,0},{2,1},{3,2},{4,3},{5,4},{6,5},{7,6},{8,7},{9,8},{10,9},{11,1... | collective-permute-start | bytes 30728 | tf_op jit(solution)/shard_map/ppermute | solution.py:118

commit v15 on v13

--- a/solution.py
+++ b/solution.py
@@ -138,9 +138,7 @@
     own_slot = tile_slot[0]
     offsets = slot_offset[:, 0, :]
     hits = own_slot[None, :] == jnp.arange(slots, dtype=jnp.int32)[:, None]
-    present = jnp.any(hits, axis=1)
-    which = jnp.sum(jnp.where(hits, jnp.arange(count, dtype=jnp.int32)[None, :], 0), axis=1)
-    which = jnp.where(present, which, count)
+    which = jnp.min(jnp.where(hits, jnp.arange(count, dtype=jnp.int32)[None, :], count), axis=1)
     own_matched = match_all(own_tiles, own_coeffs, basis)
     extra = 16
     weight_rows = jnp.broadcast_to(own_weight[:, None, None], (count, extra, size))

time: 102 us -> 102 us (level)
  no operation moved by 1% of the time
where the time goes in v15:
time: 102 us; the launch traced here: 101 us
  blocking collectives  58.5 us (57%)
  matrix products  18.8 us (18%)
  starting transfers between devices  11.9 us (12%)
  waiting for transfers between devices  6.65 us (7%)
  local copies, waits for them, and re-layouts  3.68 us (4%)
    all_to_all x1, blocking collectives, body(): recv = lax.all_to_all(send, 'skyx', split_axis=0, concat_axis=0, tiled=True)  58.5 us
    dot_general x1, matrix products, match_all(): jnp.einsum('mbik,bjk->mbij', vert, basis, preferred_element_type=jnp.floa...  5.39 us
    dot_general x1, matrix products, coadd_patch(): jnp.dot(row_place.reshape(patch, slot_count * size), shifted.reshape(slot...  4.51 us
    ppermute x1, starting transfers between devices, detect(): top = lax.ppermute(own[-r:, :], 'skyy', down)  4.49 us
    dot_general x1, matrix products, coadd_patch(): jnp.einsum('sij,sjq->siq', matched, col_place, preferred_element_type=jnp...  4.38 us
    ppermute x1, waiting for transfers between devices, detect(): east = lax.ppermute(vown[:, :r].T, 'skyx', left)  4.29 us
    ppermute x1, starting transfers between devices, detect(): west = lax.ppermute(vown[:, -r:].T, 'skyx', right)  3.55 us
    gather x1, local copies, waits for them, and re-layouts, body(): send = carry[which].reshape(columns, CAP, size + extra, size)  2.85 us
  transfers between devices with their start and end apart: 4, of which 2 were waited for; matrix products, arithmetic and copies ran while one was open for 1% of the time, Pallas kernels for 0%

profile of v15, /device:TPU:29, one launch (start us, length us, event | category | flops | bytes accessed | tf_op | source)
XLA Modules:
  0.0 101.2 jit_solution(3351290550150693474)
XLA Ops:
  0.6 0.0 copy-start
  0.6 0.8 select_reduce_fusion
  1.5 0.4 copy-done
  1.9 0.0 copy-start.3
  1.9 5.4 %fusion.2 = bf16[8,256,256]{2,1,0:T(8,128)(2,1)S(1)} fusion(bf16[1,8,5,256,256]{4,3,2,1,0:T(8,128)(2,1)} %param.9, bf16[5,256,256,1]{2,1,3,0:T(8,128)(2,1)} %constant.36, bf16[1,8,256,256]{3,2,1,0:T(8,128)(2,1)S(1)} %copy-done), kind=kOutput, calls=%fused_computation.6 | convolution fusion | flops 2694316032 | bytes 7995392 | tf_op jit(solution)/shard_map/mbik,bjk->mbij/dot_general | solution.py:35
  7.3 0.0 copy-done.3
  7.3 0.1 broadcast_in_dim.56
  7.4 0.1 fusion.30
  7.5 2.9 %gather_fusion = bf16[32,272,256]{2,1,0:T(8,128)(2,1)} fusion(bf16[9,272,256]{2,1,0:T(8,128)(2,1)S(1)} %fusion.30, s32[1024]{0:T(1024)S(1)} %pad_clamp_fusion), kind=kCustom, calls=%fused_computation | custom fusion | bytes 8913024 | tf_op jit(solution)/shard_map/gather | solution.py:147
  10.3 0.0 copy-start.2
  10.3 58.5 %all_to_all.5 = bf16[16,2,272,256]{3,2,1,0:T(8,128)(2,1)S(1)} all-to-all(bf16[16,2,272,256]{3,2,1,0:T(8,128)(2,1)} %bitcast.46), channel_id=1, replica_groups=mesh['skyy'=8,'skyx'=16] {'skyx'}, dimensions={0} | all-to-all | bytes 8912896 | tf_op jit(solution)/shard_map/all_to_all | solution.py:149
  68.8 0.0 copy-done.2
  68.8 0.3 slice_reduce_fusion
  69.1 0.1 iota_add_fusion
  69.2 4.4 %fusion.100 = bf16[32,256,512]{2,1,0:T(8,128)(2,1)S(1)} fusion(s32[32,256]{1,0:T(8,128)S(1)} %get-tuple-element.18, bf16[32,272,256]{2,1,0:T(8,128)(2,1)S(1)} %bitcast.48), kind=kOutput, calls=%fused_computation.8.clone.clone.clone.2 | convolution fusion | flops 2155872256 | bytes 12615680 | tf_op jit(solution)/shard_map/sij,sjq->siq/dot_general | solution.py:47
  73.6 0.0 copy-start.4
  73.6 4.5 %fusion.22 = f32[512,512]{1,0:T(8,128)S(1)} fusion(s32[32,256]{1,0:T(8,128)S(1)} %get-tuple-element.19, bf16[32]{0:T(256)(128)(2,1)S(1)} %slice_reduce_fusion, bf16[32,256,512]{2,1,0:T(8,128)(2,1)S(1)} %fusion.100), kind=kOutput, calls=%fused_computation.25 | convolution fusion | flops 4303355904 | bytes 9470016 | tf_op jit(solution)/shard_map/dot_general | solution.py:52
  78.1 0.0 copy-start.1
  78.1 1.3 %fusion.83 = (bf16[512,512]{1,0:T(8,128)(2,1)S(1)}, f32[512,512]{1,0:T(8,128)}) fusion(f32[512,512]{1,0:T(8,128)S(1)} %fusion.22, s32[32]{0:T(128)S(1)} %get-tuple-element.15, s32[32]{0:T(128)S(1)} %get-tuple-element.14, bf16[32]{0:T(256)(128)(2,1)S(1)} %slice_reduce_fusion), kind=kOutput, calls=%fused_computation.89 | convolution fusion | flops 17711104 | bytes 2621760 | tf_op jit(solution)/shard_map/dot_general | solution.py:63
  79.5 4.5 %collective-permute-start = (bf16[10,512]{1,0:T(8,128)(2,1)S(1)}, bf16[10,512]{1,0:T(8,128)(2,1)S(1)}, u32[]{:S(2)}, u32[]{:S(2)}) collective-permute-start(bf16[10,512]{1,0:T(8,128)(2,1)S(1)} %get-tuple-element.12), channel_id=1, source_target_pairs={{0,16},{16,32},{32,48},{48,64},{64,80},{80,96},{96,112},{1,17},{17... | collective-permute-start | bytes 30728 | tf_op jit(solution)/shard_map/ppermute | solution.py:111
  84.0 1.9 %collective-permute-start.1 = (bf16[10,512]{1,0:T(8,128)(2,1)S(1)}, bf16[10,512]{1,0:T(8,128)(2,1)S(1)}, u32[]{:S(2)}, u32[]{:S(2)}) collective-permute-start(bf16[10,512]{1,0:T(8,128)(2,1)S(1)} %get-tuple-element.13), channel_id=1, source_target_pairs={{16,0},{32,16},{48,32},{64,48},{80,64},{96,80},{112,96},{17,1},{33... | collective-permute-start | bytes 30728 | tf_op jit(solution)/shard_map/ppermute | solution.py:112
  85.9 0.0 copy-done.4
  85.9 0.8 fusion.31
  86.7 0.0 collective-permute-done
  86.7 2.3 %collective-permute-done.1 = bf16[10,512]{1,0:T(8,128)(2,1)S(1)} collective-permute-done((bf16[10,512]{1,0:T(8,128)(2,1)S(1)}, bf16[10,512]{1,0:T(8,128)(2,1)S(1)}, u32[]{:S(2)}, u32[]{:S(2)}) %collective-permute-start.1) | collective-permute-done | bytes 10272 | tf_op jit(solution)/shard_map/ppermute | solution.py:112
  89.0 0.0 copy-done.1
  89.0 0.3 fusion.29
  89.4 3.5 %collective-permute-start.2 = (bf16[10,512]{1,0:T(8,128)(2,1)S(1)}, bf16[10,512]{1,0:T(8,128)(2,1)S(1)}, u32[]{:S(2)}, u32[]{:S(2)}) collective-permute-start(bf16[10,512]{1,0:T(8,128)(2,1)S(1)} %get-tuple-element.10), channel_id=1, source_target_pairs={{0,1},{1,2},{2,3},{3,4},{4,5},{5,6},{6,7},{7,8},{8,9},{9,10},{10,1... | collective-permute-start | bytes 30728 | tf_op jit(solution)/shard_map/ppermute | solution.py:117
  92.9 1.9 %collective-permute-start.3 = (bf16[10,512]{1,0:T(8,128)(2,1)S(1)}, bf16[10,512]{1,0:T(8,128)(2,1)S(1)}, u32[]{:S(2)}, u32[]{:S(2)}) collective-permute-start(bf16[10,512]{1,0:T(8,128)(2,1)S(1)} %get-tuple-element.11), channel_id=1, source_target_pairs={{1,0},{2,1},{3,2},{4,3},{5,4},{6,5},{7,6},{8,7},{9,8},{10,9},{11,1... | collective-permute-start | bytes 30728 | tf_op jit(solution)/shard_map/ppermute | solution.py:118
  94.9 0.8 fusion.35
  95.6 0.0 collective-permute-done.2
  95.6 4.3 %collective-permute-done.3 = bf16[10,512]{1,0:T(8,128)(2,1)S(1)} collective-permute-done((bf16[10,512]{1,0:T(8,128)(2,1)S(1)}, bf16[10,512]{1,0:T(8,128)(2,1)S(1)}, u32[]{:S(2)}, u32[]{:S(2)}) %collective-permute-start.3) | collective-permute-done | bytes 10272 | tf_op jit(solution)/shard_map/ppermute | solution.py:118
  99.9 1.3 %convolution_add_fusion = f32[512,512]{1,0:T(8,128)} fusion(f32[512,512]{1,0:T(8,128)S(1)} %fusion.35, bf16[512,40]{1,0:T(8,128)(2,1)S(1)} %copy-done.1, bf16[10,512]{1,0:T(8,128)(2,1)S(1)} %collective-permute-done.3, bf16[10,512]{1,0:T(8,128)(2,1)S(1)} %collective-permute-done.2), kind=kOutput, calls=%fused_computation.21 | convolution fusion | flops 21397504 | bytes 2158592 | tf_op jit(solution)/shard_map/dot_general | solution.py:125
  (5 shorter events, 0.0 us)
Async XLA Ops:
  0.6 1.2 %copy-start = (bf16[1,8,256,256]{3,2,1,0:T(8,128)(2,1)S(1)}, bf16[1,8,256,256]{3,2,1,0:T(8,128)(2,1)}, u32[]{:S(2)}) copy-start(bf16[1,8,256,256]{3,2,1,0:T(8,128)(2,1)} %param.8) | copy-start | bytes 3145732
  1.9 5.4 %copy-start.3 = (bf16[1,8]{1,0:T(2,128)(2,1)S(1)}, bf16[1,8]{1,0:T(2,128)(2,1)}, u32[]{:S(2)}) copy-start(bf16[1,8]{1,0:T(2,128)(2,1)} %param.10) | copy-start | bytes 52
  10.3 58.5 %copy-start.2 = (s32[2,1,32]{2,1,0:T(1,128)S(1)}, s32[2,1,32]{2,1,0:T(1,128)}, u32[]{:S(2)}) copy-start(s32[2,1,32]{2,1,0:T(1,128)} %param.12) | copy-start | bytes 772
  73.6 12.3 %copy-start.4 = (bf16[512,1024]{1,0:T(8,128)(2,1)S(1)}, bf16[512,1024]{1,0:T(8,128)(2,1)}, u32[]{:S(2)}) copy-start(bf16[512,1024]{1,0:T(8,128)(2,1)} %constant.8.clone) | copy-start | bytes 3145732
  78.1 10.9 %copy-start.1 = (bf16[512,40]{1,0:T(8,128)(2,1)S(1)}, bf16[512,40]{1,0:T(8,128)(2,1)}, u32[]{:S(2)}) copy-start(bf16[512,40]{1,0:T(8,128)(2,1)} %constant.9.clone) | copy-start | bytes 122884
  79.5 7.2 %collective-permute-start = (bf16[10,512]{1,0:T(8,128)(2,1)S(1)}, bf16[10,512]{1,0:T(8,128)(2,1)S(1)}, u32[]{:S(2)}, u32[]{:S(2)}) collective-permute-start(bf16[10,512]{1,0:T(8,128)(2,1)S(1)} %get-tuple-element.12), channel_id=1, source_target_pairs={{0,16},{16,32},{32,48},{48,64},{64,80},{80,96},{96,112},{1,17},{17... | collective-permute-start | bytes 30728 | tf_op jit(solution)/shard_map/ppermute | solution.py:111
  84.0 5.1 %collective-permute-start.1 = (bf16[10,512]{1,0:T(8,128)(2,1)S(1)}, bf16[10,512]{1,0:T(8,128)(2,1)S(1)}, u32[]{:S(2)}, u32[]{:S(2)}) collective-permute-start(bf16[10,512]{1,0:T(8,128)(2,1)S(1)} %get-tuple-element.13), channel_id=1, source_target_pairs={{16,0},{32,16},{48,32},{64,48},{80,64},{96,80},{112,96},{17,1},{33... | collective-permute-start | bytes 30728 | tf_op jit(solution)/shard_map/ppermute | solution.py:112
  89.4 6.2 %collective-permute-start.2 = (bf16[10,512]{1,0:T(8,128)(2,1)S(1)}, bf16[10,512]{1,0:T(8,128)(2,1)S(1)}, u32[]{:S(2)}, u32[]{:S(2)}) collective-permute-start(bf16[10,512]{1,0:T(8,128)(2,1)S(1)} %get-tuple-element.10), channel_id=1, source_target_pairs={{0,1},{1,2},{2,3},{3,4},{4,5},{5,6},{6,7},{7,8},{8,9},{9,10},{10,1... | collective-permute-start | bytes 30728 | tf_op jit(solution)/shard_map/ppermute | solution.py:117
  92.9 7.0 %collective-permute-start.3 = (bf16[10,512]{1,0:T(8,128)(2,1)S(1)}, bf16[10,512]{1,0:T(8,128)(2,1)S(1)}, u32[]{:S(2)}, u32[]{:S(2)}) collective-permute-start(bf16[10,512]{1,0:T(8,128)(2,1)S(1)} %get-tuple-element.11), channel_id=1, source_target_pairs={{1,0},{2,1},{3,2},{4,3},{5,4},{6,5},{7,6},{8,7},{9,8},{10,9},{11,1... | collective-permute-start | bytes 30728 | tf_op jit(solution)/shard_map/ppermute | solution.py:118
